TPU v7x, 512 devices: a whole 4x8x8 slice. The times are simulated.
512 devices in a mesh: req: 64 (over z, x, core), tp: 8 (over y).
Axes of the slice: x: 4, y: 8, z: 8, core: 2. Of those that a mesh axis runs over, the one named last changes fastest.
Arguments:
- q_new: bfloat16 [4096, 5120], P('req', 'tp'), may hold values from -6 to 6
- k_new: bfloat16 [4096, 1024], P('req', 'tp'), may hold values from -15 to 15
- v_new: bfloat16 [4096, 1024], P('req', 'tp'), may hold values from -6 to 6
- k_cache: bfloat16 [1024, 128, 1024], P('req', None, 'tp'), may hold values from -16 to 16
- v_cache: bfloat16 [1024, 128, 1024], P('req', None, 'tp'), may hold values from -6 to 6
- lengths: int32 [32], replicated, may hold values from 1 to 4096, as said below
- page_table: int32 [32, 32], replicated, may hold values from -1 to 1023, as said below
- w_out: bfloat16 [5120, 5120], P('req', 'tp'), may hold values from -0.078125 to 0.078125
Outputs:
- attn_out: bfloat16 [4096, 5120], P('req')
Inputs may be any that keep to these rules, and one draw needn't show every extreme that they name: `lengths`: the last request, 31, has exactly 4096 cached tokens; every request has at least one. `page_table`: request r uses ceil(lengths[r] / 128) logical pages. Its first ceil(ceil(lengths[r] / 128) / 2) logical pages lie among global pages 2r * 16 to (2r + 1) * 16 - 1, the rest among (2r + 1) * 16 to (2r + 2) * 16 - 1; distinct logical pages use distinct global pages; entries past a request's last page are -1.
All inputs are finite; a program needn't handle non-finite values.
Results may differ from a plain program's by a relative error of at most 0.024.
Values may be sent and summed in bfloat16 or wider, within the bound.
No kernel may reach another device: no remote copies, remote signals or barrier semaphores. Data moves between devices by JAX's collectives and lax.ppermute only.
A program may use at most 64 MiB of HBM per device.

v0:
```python
import math

import jax
import jax.numpy as jnp
from jax import lax
from jax.sharding import PartitionSpec as P

HD = 128
GROUP = 5
BLOCK_PAGES = 4


ROPE_BASE = 1000000.0
FLOOR_SCORE = -1e30


def from_partner(value, axis, distance):
    return lax.ppermute(value, axis, [(i, i ^ 1 << distance) for i in range(lax.axis_size(axis))])


def rotate(values, places):
    inverse = 1.0 / ROPE_BASE ** (jnp.arange(0, HD, 2).astype(jnp.float32) / HD)
    angles = places.astype(jnp.float32)[:, None] * inverse[None, :]
    cosine = jnp.concatenate([jnp.cos(angles), jnp.cos(angles)], axis=-1)[:, None, :]
    sine = jnp.concatenate([jnp.sin(angles), jnp.sin(angles)], axis=-1)[:, None, :]
    first_half = values[..., : HD // 2]
    second_half = values[..., HD // 2 :]
    turned = jnp.concatenate([-second_half, first_half], axis=-1)
    return values * cosine + turned * sine


def absorb(state, queries, block_keys, block_values, allowed, scale):
    running_max, running_sum, output = state
    scores = (
        jnp.einsum("qcgd,kcd->cgqk", queries, block_keys, preferred_element_type=jnp.float32)
        * scale
    )
    scores = jnp.where(allowed[None, None], scores, FLOOR_SCORE)
    new_max = jnp.maximum(running_max, jnp.max(scores, axis=-1))
    factor = jnp.exp(running_max - new_max)
    weights = jnp.where(allowed[None, None], jnp.exp(scores - new_max[..., None]), 0.0)
    running_sum = running_sum * factor + jnp.sum(weights, axis=-1)
    mixed = jnp.einsum(
        "cgqk,kcd->qcgd",
        weights.astype(jnp.bfloat16),
        block_values,
        preferred_element_type=jnp.float32,
    )
    output = output * jnp.transpose(factor, (2, 0, 1))[..., None] + mixed
    return (new_max, running_sum, output)


def tensor_total(partial_value):
    return lax.psum(partial_value.astype(jnp.bfloat16), "tp")


def shards(q_new, k_new, v_new, k_cache, v_cache, lengths, page_table, w_out):
    own_rows = q_new.shape[0]
    all_rows = 2 * own_rows
    local_heads = k_new.shape[1] // HD
    pages_local = k_cache.shape[0]
    page_rows = k_cache.shape[1]
    block_rows = BLOCK_PAGES * page_rows
    scale = 1.0 / math.sqrt(HD)
    device_row = lax.axis_index("req")
    parity = device_row % 2
    request = device_row // 2
    length = lengths[request]
    own_places = length + parity * own_rows + jnp.arange(own_rows)
    own_queries = rotate(
        q_new.reshape(own_rows, local_heads * GROUP, HD).astype(jnp.float32), own_places
    ).astype(jnp.bfloat16)
    own_keys = rotate(
        k_new.reshape(own_rows, local_heads, HD).astype(jnp.float32), own_places
    ).astype(jnp.bfloat16)
    own_values = v_new.reshape(own_rows, local_heads, HD)
    peer_queries, peer_keys, peer_values = from_partner(
        (own_queries, own_keys, own_values), "req", 0
    )

    def ordered(mine, theirs):
        return jnp.where(
            parity == 0,
            jnp.concatenate([mine, theirs], axis=0),
            jnp.concatenate([theirs, mine], axis=0),
        )

    queries = ordered(own_queries, peer_queries).reshape(all_rows, local_heads, GROUP, HD)
    fresh_keys = ordered(own_keys, peer_keys)
    fresh_values = ordered(own_values, peer_values)
    state = (
        jnp.full((local_heads, GROUP, all_rows), FLOOR_SCORE, jnp.float32),
        jnp.zeros((local_heads, GROUP, all_rows), jnp.float32),
        jnp.zeros((all_rows, local_heads, GROUP, HD), jnp.float32),
    )
    token_index = jnp.arange(all_rows)
    causal = (token_index[None, :] <= token_index[:, None]) & (parity == 1)
    state = absorb(state, queries, fresh_keys, fresh_values, causal, scale)
    page_count = (length + page_rows - 1) // page_rows
    even_pages = (page_count + 1) // 2
    first_page = jnp.where(parity == 0, 0, even_pages)
    last_page = jnp.where(parity == 0, even_pages, page_count)
    table_row = jnp.concatenate([page_table[request], jnp.full((BLOCK_PAGES,), -1, jnp.int32)])
    offset = device_row * pages_local
    block_count = (last_page - first_page + BLOCK_PAGES - 1) // BLOCK_PAGES

    def visit(block, carry):
        block_first = first_page + block * BLOCK_PAGES
        logical = block_first + jnp.arange(BLOCK_PAGES)
        physical = lax.dynamic_slice(table_row, (block_first,), (BLOCK_PAGES,))
        slots = jnp.clip(physical - offset, 0, pages_local - 1)
        block_keys = k_cache[slots].reshape(block_rows, local_heads, HD)
        block_values = v_cache[slots].reshape(block_rows, local_heads, HD)
        key_places = (logical[:, None] * page_rows + jnp.arange(page_rows)[None, :]).reshape(
            block_rows
        )
        usable = jnp.repeat(logical < last_page, page_rows) & (key_places < length)
        allowed = jnp.broadcast_to(usable[None, :], (all_rows, block_rows))
        return absorb(carry, queries, block_keys, block_values, allowed, scale)

    running_max, running_sum, output = lax.fori_loop(0, block_count, visit, state)
    peer_start = (1 - parity) * own_rows
    own_start = parity * own_rows
    outgoing = (
        lax.dynamic_slice_in_dim(output, peer_start, own_rows, 0),
        lax.dynamic_slice_in_dim(running_max, peer_start, own_rows, 2),
        lax.dynamic_slice_in_dim(running_sum, peer_start, own_rows, 2),
    )
    other_output, other_max, other_sum = (
        from_partner(outgoing[0].astype(jnp.bfloat16), "req", 0).astype(jnp.float32),
        from_partner(outgoing[1].astype(jnp.bfloat16), "req", 0).astype(jnp.float32),
        from_partner(outgoing[2].astype(jnp.bfloat16), "req", 0).astype(jnp.float32),
    )
    mine_output = lax.dynamic_slice_in_dim(output, own_start, own_rows, 0)
    mine_max = lax.dynamic_slice_in_dim(running_max, own_start, own_rows, 2)
    mine_sum = lax.dynamic_slice_in_dim(running_sum, own_start, own_rows, 2)
    joint_max = jnp.maximum(mine_max, other_max)
    mine_factor = jnp.exp(mine_max - joint_max)
    other_factor = jnp.exp(other_max - joint_max)
    joint_sum = mine_sum * mine_factor + other_sum * other_factor
    joint_output = (
        mine_output * jnp.transpose(mine_factor, (2, 0, 1))[..., None]
        + other_output * jnp.transpose(other_factor, (2, 0, 1))[..., None]
    )
    attention = (
        (joint_output / jnp.transpose(joint_sum, (2, 0, 1))[..., None])
        .reshape(own_rows, local_heads * GROUP * HD)
        .astype(jnp.bfloat16)
    )
    partial_value = lax.dot_general(
        lax.all_gather(attention, "req", axis=0, tiled=True),
        w_out,
        (((1,), (1,)), ((), ())),
        preferred_element_type=jnp.float32,
    )
    return lax.all_to_all(
        tensor_total(partial_value), "req", split_axis=0, concat_axis=1, tiled=True
    )


def solution(mesh):
    in_specs = (
        P("req", "tp"),
        P("req", "tp"),
        P("req", "tp"),
        P("req", None, "tp"),
        P("req", None, "tp"),
        P(),
        P(),
        P("req", "tp"),
    )
    out_specs = P("req", None)
    return jax.shard_map(shards, mesh=mesh, in_specs=in_specs, out_specs=out_specs, check_vma=False)
```

profile of v0, /device:TPU:6, one launch (start us, length us, event | category | flops | bytes accessed | tf_op | source)
XLA Modules:
  0.0 279.8 jit_solution(12929491694747640108)
XLA Ops:
  6.5 2.0 collective-permute-start.2
  8.6 1.3 dynamic_slice.27
  10.6 0.7 convert_bitcast_fusion
  11.6 0.8 fusion.34
  12.4 2.4 collective-permute-start
  14.8 1.0 reshape.300
  16.1 1.9 collective-permute-start.1
  20.4 10.5 %while.14 = (s32[]{:T(128)}, f32[1,5,128]{2,1,0:T(8,128)S(1)}, f32[1,5,128]{2,1,0:T(8,128)S(1)}, f32[128,1,5,128]{0,3,2,1:T(8,128)S(1)}, s32[]{:T(128)}, /*index...) while((s32[]{:T(128)}, f32[1,5,128]{2,1,0:T(8,128)S(1)}, ...), condition=%wide.region_5.6_spmd, body=%wide.region_2.5_spmd.sunk | while | flops 170889632 | bytes 5585255 | solution.py:121
  21.2 1.6 gather_fusion.1
  22.8 1.6 gather_fusion
  26.5 1.6 gather_fusion.1
  28.1 1.6 gather_fusion
  31.1 2.4 collective-permute-start.5
  33.4 1.9 collective-permute-start.3
  35.5 2.4 collective-permute-start.4
  38.0 0.9 collective-permute-done.4
  39.1 0.8 copy.51
  39.9 99.8 %all-gather.2.cloned.1.call-done = bf16[4096,640]{1,0:T(8,128)(2,1)} async-done(((bf16[64,640]{1,0:T(8,128)(2,1)}), bf16[4096,640]{1,0:T(8,128)(2,1)}) %all-gather.2.cloned.1.call-update) | async-done | bytes 5242896 | tf_op jit(solution)/shard_map/all_gather | solution.py:151
  139.7 4.2 %convolution_convert_fusion = bf16[4096,80]{0,1:T(8,128)(2,1)S(1)} fusion(bf16[4096,640]{1,0:T(8,128)(2,1)} %all-gather.2.cloned.1.call-done, bf16[80,640]{1,0:T(8,128)(2,1)S(1)} %copy-done), kind=kOutput, calls=%fused_computation.31 | convolution fusion | flops 419758080 | bytes 6000640 | tf_op jit(solution)/shard_map/dot_general | solution.py:150
  143.9 2.5 all_to_all.14
  146.4 81.0 %all-reduce.3.cloned.1.call-done = bf16[64,64,80]{1,0,2:T(8,128)(2,1)} async-done(((bf16[64,64,80]{1,0,2:T(8,128)(2,1)}), bf16[64,64,80]{1,0,2:T(8,128)(2,1)}) %all-reduce.3.cloned.1.call-update) | async-done | bytes 655376 | tf_op jit(solution)/shard_map/psum | solution.py:54
  227.3 2.5 copy.43
  229.8 39.5 %all_to_all.19 = bf16[64,64,80]{2,1,0:T(8,128)(2,1)S(1)} all-to-all(bf16[64,64,80]{2,1,0:T(8,128)(2,1)S(1)} %copy.43), channel_id=1, replica_groups=mesh['req'=64,'tp'=8] {'req'}, dimensions={0} | all-to-all | bytes 1310720 | tf_op jit(solution)/shard_map/all_to_all | solution.py:156
  270.0 3.0 %all_to_all.17 = bf16[64,5120]{1,0:T(8,128)(2,1)} reshape(bf16[64,64,80]{2,1,0:T(8,128)(2,1)S(1)} %copy.44) | data formatting | bytes 1310720 | tf_op jit(solution)/shard_map/all_to_all | solution.py:156
  (58 shorter events, 7.3 us)
Async XLA Ops:
  6.5 133.2 %copy-start = (bf16[80,640]{1,0:T(8,128)(2,1)S(1)}, bf16[80,640]{1,0:T(8,128)(2,1)}, u32[]{:S(2)}) copy-start(bf16[80,640]{1,0:T(8,128)(2,1)} %param.17) | copy-start | bytes 307204
  6.5 133.1 %all-gather.2.cloned.1.call-start = ((), (), s32[]{:S(2)}) async-start(), calls=%async_computation.1 | async-start | bytes 5324800 | tf_op jit(solution)/shard_map/all_gather | solution.py:151
  6.5 13.6 %collective-permute-start.2 = (bf16[64,1,128]{2,0,1:T(8,128)(2,1)}, bf16[64,1,128]{2,0,1:T(8,128)(2,1)S(1)}, u32[]{:S(2)}, u32[]{:S(2)}) collective-permute-start(bf16[64,1,128]{2,0,1:T(8,128)(2,1)} %bitcast.155), channel_id=1, source_target_pairs={{0,8},{8,0},{16,24},{24,16},{32,40},{40,32},{48,56},{56,48},{64,72... | collective-permute-start | bytes 49160 | tf_op jit(solution)/shard_map/ppermute | solution.py:18
  12.4 7.2 %collective-permute-start = (bf16[64,1,128]{2,0,1:T(8,128)(2,1)S(1)}, bf16[64,1,128]{2,0,1:T(8,128)(2,1)S(1)}, u32[]{:S(2)}, u32[]{:S(2)}) collective-permute-start(bf16[64,1,128]{2,0,1:T(8,128)(2,1)S(1)} %bitcast.154), channel_id=1, source_target_pairs={{0,8},{8,0},{16,24},{24,16},{32,40},{40,32},{48,56},{56,48},{64,72... | collective-permute-start | bytes 49160 | tf_op jit(solution)/shard_map/ppermute | solution.py:18
  16.1 3.4 %collective-permute-start.1 = (bf16[64,5,128]{2,1,0:T(8,128)(2,1)S(1)}, bf16[64,5,128]{2,1,0:T(8,128)(2,1)S(1)}, u32[]{:S(2)}, u32[]{:S(2)}) collective-permute-start(bf16[64,5,128]{2,1,0:T(8,128)(2,1)S(1)} %fusion.25), channel_id=1, source_target_pairs={{0,8},{8,0},{16,24},{24,16},{32,40},{40,32},{48,56},{56,48},{64,72... | collective-permute-start | bytes 245768 | tf_op jit(solution)/shard_map/ppermute | solution.py:18
  18.7 1.5 copy-start.1
  31.1 6.9 %collective-permute-start.5 = (bf16[1,5,64]{2,1,0:T(8,128)(2,1)S(1)}, bf16[1,5,64]{2,1,0:T(8,128)(2,1)S(1)}, u32[]{:S(2)}, u32[]{:S(2)}) collective-permute-start(bf16[1,5,64]{2,1,0:T(8,128)(2,1)S(1)} %dynamic-slice_convert_fusion.1), channel_id=1, source_target_pairs={{0,8},{8,0},{16,24},{24,16},{32,40},{40,32},{48,56},{56,48},{64,72... | collective-permute-start | bytes 1928 | tf_op jit(solution)/shard_map/ppermute | solution.py:18
  33.4 4.5 %collective-permute-start.3 = (bf16[1,5,64]{2,1,0:T(8,128)(2,1)S(1)}, bf16[1,5,64]{2,1,0:T(8,128)(2,1)S(1)}, u32[]{:S(2)}, u32[]{:S(2)}) collective-permute-start(bf16[1,5,64]{2,1,0:T(8,128)(2,1)S(1)} %dynamic-slice_convert_fusion.2), channel_id=1, source_target_pairs={{0,8},{8,0},{16,24},{24,16},{32,40},{40,32},{48,56},{56,48},{64,72... | collective-permute-start | bytes 1928 | tf_op jit(solution)/shard_map/ppermute | solution.py:18
  35.5 3.4 %collective-permute-start.4 = (bf16[64,1,5,128]{0,3,2,1:T(8,128)(2,1)S(1)}, bf16[64,1,5,128]{0,3,2,1:T(8,128)(2,1)S(1)}, u32[]{:S(2)}, u32[]{:S(2)}) collective-permute-start(bf16[64,1,5,128]{0,3,2,1:T(8,128)(2,1)S(1)} %dynamic-slice_convert_fusion), channel_id=1, source_target_pairs={{0,8},{8,0},{16,24},{24,16},{32,40},{40,32},{48,56},{56,48},{64,72... | collective-permute-start | bytes 245768 | tf_op jit(solution)/shard_map/ppermute | solution.py:18
  39.9 187.5 %all-reduce.3.cloned.1.call-start = ((), (), s32[]{:S(2)}) async-start(), calls=%async_computation.2 | async-start | bytes 2621440 | tf_op jit(solution)/shard_map/psum | solution.py:54
Sparse Core Ops, SparseCore 0:
  40.0 99.6 all-gather.1
  146.5 80.8 all-reduce.2
where the time goes:
time: 281 us; the launch traced here: 280 us
  waiting for transfers between devices  182 us (65%)
  blocking collectives  39.5 us (14%)
  local copies, waits for them, and re-layouts  19.1 us (7%)
  between operations  15 us (5%)
  starting transfers between devices  13.1 us (5%)
  matrix products  6.36 us (2%)
  other arithmetic  4.86 us (2%)
    all_gather x1, waiting for transfers between devices, shards(): lax.all_gather(attention, 'req', axis=0, tiled=True)  99.8 us
    psum x1, waiting for transfers between devices, tensor_total(): return lax.psum(partial_value.astype(jnp.bfloat16), 'tp')  81 us
    all_to_all x1, blocking collectives, shards(): lax.all_to_all(tensor_total(partial_value), 'req', split_axis=0, concat_a...  39.5 us
    ppermute x6, starting transfers between devices, from_partner(): lax.ppermute(value, axis, [(i, i ^ 1 << distance) for i in range(lax.axis...  13.1 us
    all_to_all x3, local copies, waits for them, and re-layouts, shards(): lax.all_to_all(tensor_total(partial_value), 'req', split_axis=0, concat_a...  6.1 us
  transfers between devices with their start and end apart: 8, of which 3 were waited for; matrix products, arithmetic and copies ran while one was open for 2% of the time, Pallas kernels for 0%

commit v1 on v0

--- a/solution.py
+++ b/solution.py
@@ -62,6 +62,7 @@
     page_rows = k_cache.shape[1]
     block_rows = BLOCK_PAGES * page_rows
     scale = 1.0 / math.sqrt(HD)
+    weights_all = lax.all_gather(w_out, "req", axis=0, tiled=True)
     device_row = lax.axis_index("req")
     parity = device_row % 2
     request = device_row // 2
@@ -148,14 +149,12 @@
         .astype(jnp.bfloat16)
     )
     partial_value = lax.dot_general(
-        lax.all_gather(attention, "req", axis=0, tiled=True),
-        w_out,
+        attention,
+        weights_all,
         (((1,), (1,)), ((), ())),
         preferred_element_type=jnp.float32,
     )
-    return lax.all_to_all(
-        tensor_total(partial_value), "req", split_axis=0, concat_axis=1, tiled=True
-    )
+    return tensor_total(partial_value)
 
 
 def solution(mesh):

time: 281 us -> 194 us (0.69)
  blocking collectives: 39.5 us -> 0 us
  waiting for transfers between devices: 182 us -> 146 us
  local copies, waits for them, and re-layouts: 19.1 us -> 7.82 us
    all_to_all x1 -> x0, blocking collectives: 39.5 us -> none  [shards(): lax.all_to_all(tensor_total(partial_value), 'req', split_axis=0, concat_a...]
    all_gather x1, waiting for transfers between devices: 99.8 us -> 67.6 us  [shards(): weights_all = lax.all_gather(w_out, 'req', axis=0, tiled=True)]
    all_to_all x3 -> x0, local copies, waits for them, and re-layouts: 6.1 us -> none  [shards(): lax.all_to_all(tensor_total(partial_value), 'req', split_axis=0, concat_a...]
    psum x1, waiting for transfers between devices: 81 us -> 76.8 us  [tensor_total(): return lax.psum(partial_value.astype(jnp.bfloat16), 'tp')]
  transfers between devices with their start and end apart: 8 -> 8, of which waited for: 3 -> 3; matrix products, arithmetic and copies ran while one was open for 2% -> 6% of each run, Pallas kernels for 0% -> 0%
where the time goes in v1:
time: 194 us; the launch traced here: 193 us
  waiting for transfers between devices  146 us (75%)
  between operations  15.2 us (8%)
  starting transfers between devices  12.5 us (6%)
  local copies, waits for them, and re-layouts  7.82 us (4%)
  matrix products  7.14 us (4%)
  other arithmetic  3.82 us (2%)
    psum x1, waiting for transfers between devices, tensor_total(): return lax.psum(partial_value.astype(jnp.bfloat16), 'tp')  76.8 us
    all_gather x1, waiting for transfers between devices, shards(): weights_all = lax.all_gather(w_out, 'req', axis=0, tiled=True)  67.6 us
    ppermute x6, starting transfers between devices, from_partner(): lax.ppermute(value, axis, [(i, i ^ 1 << distance) for i in range(lax.axis...  12.5 us
    dot_general x1, matrix products, shards(): lax.dot_general(attention, weights_all, (((1,), (1,)), ((), ())), preferr...  5.84 us
  transfers between devices with their start and end apart: 8, of which 3 were waited for; matrix products, arithmetic and copies ran while one was open for 6% of the time, Pallas kernels for 0%

profile of v1, /device:TPU:6, one launch (start us, length us, event | category | flops | bytes accessed | tf_op | source)
XLA Modules:
  0.0 192.9 jit_solution(12969337353587671796)
XLA Ops:
  6.5 0.7 all-gather.2.cloned.1.call-update
  7.3 1.0 reshape.297
  8.3 1.3 dynamic_slice.27
  10.4 0.7 convert_bitcast_fusion
  11.4 0.8 fusion.34
  12.5 1.9 collective-permute-start.1
  14.4 2.4 %collective-permute-start = (bf16[64,1,128]{2,0,1:T(8,128)(2,1)S(1)}, bf16[64,1,128]{2,0,1:T(8,128)(2,1)S(1)}, u32[]{:S(2)}, u32[]{:S(2)}) collective-permute-start(bf16[64,1,128]{2,0,1:T(8,128)(2,1)S(1)} %bitcast.150), channel_id=1, source_target_pairs={{0,8},{8,0},{16,24},{24,16},{32,40},{40,32},{48,56},{56,48},{64,72... | collective-permute-start | bytes 49160 | tf_op jit(solution)/shard_map/ppermute | solution.py:18
  16.8 1.9 collective-permute-start.2
  20.3 0.2 fusion.20
  20.5 5.3 %while.14 = (s32[]{:T(128)}, f32[1,5,128]{2,1,0:T(8,128)S(1)}, f32[1,5,128]{2,1,0:T(8,128)S(1)}, f32[128,1,5,128]{0,3,2,1:T(8,128)S(1)}, s32[]{:T(128)}, /*index...) while((s32[]{:T(128)}, f32[1,5,128]{2,1,0:T(8,128)S(1)}, ...), condition=%wide.region_5.6_spmd, body=%wide.region_2.5_spmd.sunk | while | flops 170889632 | bytes 5585255 | solution.py:122
  20.6 1.6 gather_fusion
  22.3 0.8 fusion.81
  23.0 0.4 bitcast_reduce_fusion.2
  23.4 1.6 gather_fusion.1
  25.1 0.5 fusion.84
  25.5 0.3 fusion.83
  25.9 1.9 collective-permute-start.3
  27.9 2.4 %collective-permute-start.5 = (bf16[1,5,64]{2,1,0:T(8,128)(2,1)S(1)}, bf16[1,5,64]{2,1,0:T(8,128)(2,1)S(1)}, u32[]{:S(2)}, u32[]{:S(2)}) collective-permute-start(bf16[1,5,64]{2,1,0:T(8,128)(2,1)S(1)} %dynamic-slice_convert_fusion.1), channel_id=1, source_target_pairs={{0,8},{8,0},{16,24},{24,16},{32,40},{40,32},{48,56},{56,48},{64,72... | collective-permute-start | bytes 1928 | tf_op jit(solution)/shard_map/ppermute | solution.py:18
  30.4 1.9 collective-permute-start.4
  32.5 1.3 collective-permute-done.4
  33.9 67.6 %all-gather.2.cloned.1.call-done = bf16[5120,640]{1,0:T(8,128)(2,1)} async-done(((bf16[80,640]{1,0:T(8,128)(2,1)}), bf16[5120,640]{1,0:T(8,128)(2,1)}) %all-gather.2.cloned.1.call-update) | async-done | bytes 6553616 | tf_op jit(solution)/shard_map/all_gather | solution.py:65
  101.5 5.8 %convolution_convert_fusion = bf16[64,5120]{1,0:T(8,128)(2,1)} fusion(bf16[64,640]{0,1:T(8,128)(2,1)S(1)} %bitcast.148, bf16[5120,640]{1,0:T(8,128)(2,1)} %all-gather.2.cloned.1.call-done), kind=kOutput, calls=%fused_computation.31 | convolution fusion | flops 419758080 | bytes 7290880 | tf_op jit(solution)/shard_map/dot_general | solution.py:151
  107.3 76.8 %all-reduce.3.cloned.1.call-done = bf16[64,5120]{1,0:T(8,128)(2,1)} async-done(((bf16[64,5120]{1,0:T(8,128)(2,1)}), bf16[64,5120]{1,0:T(8,128)(2,1)}) %all-reduce.3.cloned.1.call-update) | async-done | bytes 655376 | tf_op jit(solution)/shard_map/psum | solution.py:54
  184.1 2.0 %copy.42 = bf16[64,5120]{1,0:T(8,128)(2,1)} copy(bf16[64,5120]{1,0:T(8,128)(2,1)} %all-reduce.3.cloned.1.call-done) | data formatting | bytes 1310720
  (40 shorter events, 1.9 us)
Async XLA Ops:
  6.5 13.0 %copy-start = (s32[32,32]{1,0:T(8,128)S(1)}, s32[32,32]{1,0:T(8,128)}, u32[]{:S(2)}) copy-start(s32[32,32]{1,0:T(8,128)} %param.16) | copy-start | bytes 12292
  6.5 94.9 %all-gather.2.cloned.1.call-start = ((), (), s32[]{:S(2)}) async-start(), calls=%async_computation | async-start | bytes 6656000 | tf_op jit(solution)/shard_map/all_gather | solution.py:65
  7.3 176.8 %all-reduce.3.cloned.1.call-start = ((), (), s32[]{:S(2)}) async-start(), calls=%async_computation.1 | async-start | bytes 1310720 | tf_op jit(solution)/shard_map/psum | solution.py:54
  8.3 8.5 %copy-start.1 = (bf16[64,128]{1,0:T(8,128)(2,1)S(1)}, bf16[64,128]{1,0:T(8,128)(2,1)}, u32[]{:S(2)}) copy-start(bf16[64,128]{1,0:T(8,128)(2,1)} %param.12) | copy-start | bytes 49156
  12.5 7.1 %collective-permute-start.1 = (bf16[64,5,128]{2,1,0:T(8,128)(2,1)S(1)}, bf16[64,5,128]{2,1,0:T(8,128)(2,1)S(1)}, u32[]{:S(2)}, u32[]{:S(2)}) collective-permute-start(bf16[64,5,128]{2,1,0:T(8,128)(2,1)S(1)} %fusion.25), channel_id=1, source_target_pairs={{0,8},{8,0},{16,24},{24,16},{32,40},{40,32},{48,56},{56,48},{64,72... | collective-permute-start | bytes 245768 | tf_op jit(solution)/shard_map/ppermute | solution.py:18
  14.4 5.4 %collective-permute-start = (bf16[64,1,128]{2,0,1:T(8,128)(2,1)S(1)}, bf16[64,1,128]{2,0,1:T(8,128)(2,1)S(1)}, u32[]{:S(2)}, u32[]{:S(2)}) collective-permute-start(bf16[64,1,128]{2,0,1:T(8,128)(2,1)S(1)} %bitcast.150), channel_id=1, source_target_pairs={{0,8},{8,0},{16,24},{24,16},{32,40},{40,32},{48,56},{56,48},{64,72... | collective-permute-start | bytes 49160 | tf_op jit(solution)/shard_map/ppermute | solution.py:18
  16.8 3.4 %collective-permute-start.2 = (bf16[64,1,128]{2,0,1:T(8,128)(2,1)S(1)}, bf16[64,1,128]{2,0,1:T(8,128)(2,1)S(1)}, u32[]{:S(2)}, u32[]{:S(2)}) collective-permute-start(bf16[64,1,128]{2,0,1:T(8,128)(2,1)S(1)} %bitcast.151), channel_id=1, source_target_pairs={{0,8},{8,0},{16,24},{24,16},{32,40},{40,32},{48,56},{56,48},{64,72... | collective-permute-start | bytes 49160 | tf_op jit(solution)/shard_map/ppermute | solution.py:18
  25.9 6.4 %collective-permute-start.3 = (bf16[1,5,64]{2,1,0:T(8,128)(2,1)S(1)}, bf16[1,5,64]{2,1,0:T(8,128)(2,1)S(1)}, u32[]{:S(2)}, u32[]{:S(2)}) collective-permute-start(bf16[1,5,64]{2,1,0:T(8,128)(2,1)S(1)} %dynamic-slice_convert_fusion.2), channel_id=1, source_target_pairs={{0,8},{8,0},{16,24},{24,16},{32,40},{40,32},{48,56},{56,48},{64,72... | collective-permute-start | bytes 1928 | tf_op jit(solution)/shard_map/ppermute | solution.py:18
  27.9 4.5 %collective-permute-start.5 = (bf16[1,5,64]{2,1,0:T(8,128)(2,1)S(1)}, bf16[1,5,64]{2,1,0:T(8,128)(2,1)S(1)}, u32[]{:S(2)}, u32[]{:S(2)}) collective-permute-start(bf16[1,5,64]{2,1,0:T(8,128)(2,1)S(1)} %dynamic-slice_convert_fusion.1), channel_id=1, source_target_pairs={{0,8},{8,0},{16,24},{24,16},{32,40},{40,32},{48,56},{56,48},{64,72... | collective-permute-start | bytes 1928 | tf_op jit(solution)/shard_map/ppermute | solution.py:18
  30.4 3.3 %collective-permute-start.4 = (bf16[64,1,5,128]{0,3,2,1:T(8,128)(2,1)S(1)}, bf16[64,1,5,128]{0,3,2,1:T(8,128)(2,1)S(1)}, u32[]{:S(2)}, u32[]{:S(2)}) collective-permute-start(bf16[64,1,5,128]{0,3,2,1:T(8,128)(2,1)S(1)} %dynamic-slice_convert_fusion), channel_id=1, source_target_pairs={{0,8},{8,0},{16,24},{24,16},{32,40},{40,32},{48,56},{56,48},{64,72... | collective-permute-start | bytes 245768 | tf_op jit(solution)/shard_map/ppermute | solution.py:18
Sparse Core Ops, SparseCore 0:
  10.6 90.7 all-gather.1
  107.5 76.6 all-reduce.2

commit v2 on v1

--- a/solution.py
+++ b/solution.py
@@ -51,7 +51,12 @@
 
 
 def tensor_total(partial_value):
-    return lax.psum(partial_value.astype(jnp.bfloat16), "tp")
+    rows, features = partial_value.shape
+    parts = lax.axis_size("tp")
+    pieces = partial_value.astype(jnp.bfloat16).reshape(rows, parts, features // parts)
+    pieces = lax.all_to_all(pieces, "tp", 1, 1, tiled=True)
+    summed = jnp.sum(pieces.astype(jnp.float32), axis=1).astype(jnp.bfloat16)
+    return lax.all_gather(summed, "tp", axis=1, tiled=True)
 
 
 def shards(q_new, k_new, v_new, k_cache, v_cache, lengths, page_table, w_out):

time: 194 us -> 169 us (0.87)
  waiting for transfers between devices: 146 us -> 63.8 us
  blocking collectives: 0 us -> 53.1 us
  local copies, waits for them, and re-layouts: 7.82 us -> 9.99 us
    psum x1 -> x0, waiting for transfers between devices: 76.8 us -> none  [tensor_total(): return lax.psum(partial_value.astype(jnp.bfloat16), 'tp')]
    all_to_all x0 -> x1, blocking collectives: none -> 27.3 us  [tensor_total(): pieces = lax.all_to_all(pieces, 'tp', 1, 1, tiled=True)]
    all_gather x0 -> x1, blocking collectives: none -> 25.9 us  [tensor_total(): return lax.all_gather(summed, 'tp', axis=1, tiled=True)]
    all_gather x1, waiting for transfers between devices: 67.6 us -> 62.2 us  [shards(): weights_all = lax.all_gather(w_out, 'req', axis=0, tiled=True)]
  transfers between devices with their start and end apart: 8 -> 7, of which waited for: 3 -> 2; matrix products, arithmetic and copies ran while one was open for 6% -> 10% of each run, Pallas kernels for 0% -> 0%
where the time goes in v2:
time: 169 us; the launch traced here: 167 us
  waiting for transfers between devices  63.8 us (38%)
  blocking collectives  53.1 us (31%)
  between operations  15.2 us (9%)
  starting transfers between devices  13 us (8%)
  local copies, waits for them, and re-layouts  9.99 us (6%)
  matrix products  7.14 us (4%)
  other arithmetic  5.05 us (3%)
    all_gather x1, waiting for transfers between devices, shards(): weights_all = lax.all_gather(w_out, 'req', axis=0, tiled=True)  62.2 us
    all_to_all x1, blocking collectives, tensor_total(): pieces = lax.all_to_all(pieces, 'tp', 1, 1, tiled=True)  27.3 us
    all_gather x1, blocking collectives, tensor_total(): return lax.all_gather(summed, 'tp', axis=1, tiled=True)  25.9 us
    ppermute x6, starting transfers between devices, from_partner(): lax.ppermute(value, axis, [(i, i ^ 1 << distance) for i in range(lax.axis...  13 us
    dot_general x1, matrix products, shards(): lax.dot_general(attention, weights_all, (((1,), (1,)), ((), ())), preferr...  5 us
  transfers between devices with their start and end apart: 7, of which 2 were waited for; matrix products, arithmetic and copies ran while one was open for 10% of the time, Pallas kernels for 0%

profile of v2, /device:TPU:6, one launch (start us, length us, event | category | flops | bytes accessed | tf_op | source)
XLA Modules:
  0.0 167.4 jit_solution(10939948370457504164)
XLA Ops:
  6.5 0.7 all-gather.2.cloned.1.call-update
  7.3 1.0 reshape.301
  8.3 1.3 dynamic_slice.27
  10.3 0.7 convert_bitcast_fusion
  11.3 0.8 fusion.34
  12.4 1.9 %collective-permute-start.1 = (bf16[64,5,128]{2,1,0:T(8,128)(2,1)S(1)}, bf16[64,5,128]{2,1,0:T(8,128)(2,1)S(1)}, u32[]{:S(2)}, u32[]{:S(2)}) collective-permute-start(bf16[64,5,128]{2,1,0:T(8,128)(2,1)S(1)} %fusion.25), channel_id=1, source_target_pairs={{0,8},{8,0},{16,24},{24,16},{32,40},{40,32},{48,56},{56,48},{64,72... | collective-permute-start | bytes 245768 | tf_op jit(solution)/shard_map/ppermute | solution.py:18
  14.4 2.4 %collective-permute-start = (bf16[64,1,128]{2,0,1:T(8,128)(2,1)S(1)}, bf16[64,1,128]{2,0,1:T(8,128)(2,1)S(1)}, u32[]{:S(2)}, u32[]{:S(2)}) collective-permute-start(bf16[64,1,128]{2,0,1:T(8,128)(2,1)S(1)} %bitcast.156), channel_id=1, source_target_pairs={{0,8},{8,0},{16,24},{24,16},{32,40},{40,32},{48,56},{56,48},{64,72... | collective-permute-start | bytes 49160 | tf_op jit(solution)/shard_map/ppermute | solution.py:18
  16.8 1.9 %collective-permute-start.2 = (bf16[64,1,128]{2,0,1:T(8,128)(2,1)S(1)}, bf16[64,1,128]{2,0,1:T(8,128)(2,1)S(1)}, u32[]{:S(2)}, u32[]{:S(2)}) collective-permute-start(bf16[64,1,128]{2,0,1:T(8,128)(2,1)S(1)} %bitcast.157), channel_id=1, source_target_pairs={{0,8},{8,0},{16,24},{24,16},{32,40},{40,32},{48,56},{56,48},{64,72... | collective-permute-start | bytes 49160 | tf_op jit(solution)/shard_map/ppermute | solution.py:18
  20.5 10.6 %while.14 = (s32[]{:T(128)}, f32[1,5,128]{2,1,0:T(8,128)S(1)}, f32[1,5,128]{2,1,0:T(8,128)S(1)}, f32[128,1,5,128]{0,3,2,1:T(8,128)S(1)}, s32[]{:T(128)}, /*index...) while((s32[]{:T(128)}, f32[1,5,128]{2,1,0:T(8,128)S(1)}, ...), condition=%wide.region_5.6_spmd, body=%wide.region_2.5_spmd.sunk | while | flops 170889632 | bytes 5585255 | solution.py:127
  20.6 1.6 gather_fusion
  22.2 0.8 fusion.81
  23.4 1.6 gather_fusion.1
  25.9 1.6 gather_fusion
  27.5 0.8 fusion.81
  28.7 1.6 gather_fusion.1
  31.2 2.4 %collective-permute-start.3 = (bf16[1,5,64]{2,1,0:T(8,128)(2,1)S(1)}, bf16[1,5,64]{2,1,0:T(8,128)(2,1)S(1)}, u32[]{:S(2)}, u32[]{:S(2)}) collective-permute-start(bf16[1,5,64]{2,1,0:T(8,128)(2,1)S(1)} %dynamic-slice_convert_fusion.2), channel_id=1, source_target_pairs={{0,8},{8,0},{16,24},{24,16},{32,40},{40,32},{48,56},{56,48},{64,72... | collective-permute-start | bytes 1928 | tf_op jit(solution)/shard_map/ppermute | solution.py:18
  33.7 1.9 %collective-permute-start.5 = (bf16[1,5,64]{2,1,0:T(8,128)(2,1)S(1)}, bf16[1,5,64]{2,1,0:T(8,128)(2,1)S(1)}, u32[]{:S(2)}, u32[]{:S(2)}) collective-permute-start(bf16[1,5,64]{2,1,0:T(8,128)(2,1)S(1)} %dynamic-slice_convert_fusion.1), channel_id=1, source_target_pairs={{0,8},{8,0},{16,24},{24,16},{32,40},{40,32},{48,56},{56,48},{64,72... | collective-permute-start | bytes 1928 | tf_op jit(solution)/shard_map/ppermute | solution.py:18
  35.7 2.4 %collective-permute-start.4 = (bf16[64,1,5,128]{0,3,2,1:T(8,128)(2,1)S(1)}, bf16[64,1,5,128]{0,3,2,1:T(8,128)(2,1)S(1)}, u32[]{:S(2)}, u32[]{:S(2)}) collective-permute-start(bf16[64,1,5,128]{0,3,2,1:T(8,128)(2,1)S(1)} %dynamic-slice_convert_fusion), channel_id=1, source_target_pairs={{0,8},{8,0},{16,24},{24,16},{32,40},{40,32},{48,56},{56,48},{64,72... | collective-permute-start | bytes 245768 | tf_op jit(solution)/shard_map/ppermute | solution.py:18
  38.2 0.9 collective-permute-done.4
  39.3 62.2 %all-gather.2.cloned.1.call-done = bf16[5120,640]{1,0:T(8,128)(2,1)} async-done(((bf16[80,640]{1,0:T(8,128)(2,1)}), bf16[5120,640]{1,0:T(8,128)(2,1)}) %all-gather.2.cloned.1.call-update) | async-done | bytes 6553616 | tf_op jit(solution)/shard_map/all_gather | solution.py:70
  101.5 5.0 %convolution_convert_fusion = bf16[64,5120]{1,0:T(8,128)(2,1)S(1)} fusion(bf16[64,640]{0,1:T(8,128)(2,1)S(1)} %bitcast.154, bf16[5120,640]{1,0:T(8,128)(2,1)} %all-gather.2.cloned.1.call-done), kind=kOutput, calls=%fused_computation.31 | convolution fusion | flops 419758080 | bytes 7290880 | tf_op jit(solution)/shard_map/dot_general | solution.py:156
  106.5 27.3 %all_to_all.5 = bf16[64,8,640]{2,0,1:T(8,128)(2,1)S(1)} all-to-all(bf16[64,8,640]{2,0,1:T(8,128)(2,1)S(1)} %bitcast.150), channel_id=1, replica_groups=mesh['req'=64,'tp'=8] {'tp'}, dimensions={1} | all-to-all | bytes 1310720 | tf_op jit(solution)/shard_map/all_to_all | solution.py:57
  133.9 25.9 %all_gather.7 = bf16[64,5120]{1,0:T(8,128)(2,1)S(1)} all-gather(bf16[64,640]{1,0:T(8,128)(2,1)S(1)} %reduce_sum.36), channel_id=1, replica_groups=mesh['req'=64,'tp'=8] {'tp'}, dimensions={1}, use_global_device_ids=true | all-gather | bytes 737280 | tf_op jit(solution)/shard_map/all_gather | solution.py:59
  159.8 0.8 copy.52
  (54 shorter events, 4.5 us)
Async XLA Ops:
  6.5 13.0 %copy-start = (s32[32,32]{1,0:T(8,128)S(1)}, s32[32,32]{1,0:T(8,128)}, u32[]{:S(2)}) copy-start(s32[32,32]{1,0:T(8,128)} %param.16) | copy-start | bytes 12292
  6.5 94.9 %all-gather.2.cloned.1.call-start = ((), (), s32[]{:S(2)}) async-start(), calls=%async_computation.1 | async-start | bytes 6656000 | tf_op jit(solution)/shard_map/all_gather | solution.py:70
  8.3 8.5 %copy-start.1 = (bf16[64,128]{1,0:T(8,128)(2,1)S(1)}, bf16[64,128]{1,0:T(8,128)(2,1)}, u32[]{:S(2)}) copy-start(bf16[64,128]{1,0:T(8,128)(2,1)} %param.12) | copy-start | bytes 49156
  12.4 7.1 %collective-permute-start.1 = (bf16[64,5,128]{2,1,0:T(8,128)(2,1)S(1)}, bf16[64,5,128]{2,1,0:T(8,128)(2,1)S(1)}, u32[]{:S(2)}, u32[]{:S(2)}) collective-permute-start(bf16[64,5,128]{2,1,0:T(8,128)(2,1)S(1)} %fusion.25), channel_id=1, source_target_pairs={{0,8},{8,0},{16,24},{24,16},{32,40},{40,32},{48,56},{56,48},{64,72... | collective-permute-start | bytes 245768 | tf_op jit(solution)/shard_map/ppermute | solution.py:18
  14.4 5.3 %collective-permute-start = (bf16[64,1,128]{2,0,1:T(8,128)(2,1)S(1)}, bf16[64,1,128]{2,0,1:T(8,128)(2,1)S(1)}, u32[]{:S(2)}, u32[]{:S(2)}) collective-permute-start(bf16[64,1,128]{2,0,1:T(8,128)(2,1)S(1)} %bitcast.156), channel_id=1, source_target_pairs={{0,8},{8,0},{16,24},{24,16},{32,40},{40,32},{48,56},{56,48},{64,72... | collective-permute-start | bytes 49160 | tf_op jit(solution)/shard_map/ppermute | solution.py:18
  16.8 3.4 %collective-permute-start.2 = (bf16[64,1,128]{2,0,1:T(8,128)(2,1)S(1)}, bf16[64,1,128]{2,0,1:T(8,128)(2,1)S(1)}, u32[]{:S(2)}, u32[]{:S(2)}) collective-permute-start(bf16[64,1,128]{2,0,1:T(8,128)(2,1)S(1)} %bitcast.157), channel_id=1, source_target_pairs={{0,8},{8,0},{16,24},{24,16},{32,40},{40,32},{48,56},{56,48},{64,72... | collective-permute-start | bytes 49160 | tf_op jit(solution)/shard_map/ppermute | solution.py:18
  31.2 6.9 %collective-permute-start.3 = (bf16[1,5,64]{2,1,0:T(8,128)(2,1)S(1)}, bf16[1,5,64]{2,1,0:T(8,128)(2,1)S(1)}, u32[]{:S(2)}, u32[]{:S(2)}) collective-permute-start(bf16[1,5,64]{2,1,0:T(8,128)(2,1)S(1)} %dynamic-slice_convert_fusion.2), channel_id=1, source_target_pairs={{0,8},{8,0},{16,24},{24,16},{32,40},{40,32},{48,56},{56,48},{64,72... | collective-permute-start | bytes 1928 | tf_op jit(solution)/shard_map/ppermute | solution.py:18
  33.7 4.5 %collective-permute-start.5 = (bf16[1,5,64]{2,1,0:T(8,128)(2,1)S(1)}, bf16[1,5,64]{2,1,0:T(8,128)(2,1)S(1)}, u32[]{:S(2)}, u32[]{:S(2)}) collective-permute-start(bf16[1,5,64]{2,1,0:T(8,128)(2,1)S(1)} %dynamic-slice_convert_fusion.1), channel_id=1, source_target_pairs={{0,8},{8,0},{16,24},{24,16},{32,40},{40,32},{48,56},{56,48},{64,72... | collective-permute-start | bytes 1928 | tf_op jit(solution)/shard_map/ppermute | solution.py:18
  35.7 3.4 %collective-permute-start.4 = (bf16[64,1,5,128]{0,3,2,1:T(8,128)(2,1)S(1)}, bf16[64,1,5,128]{0,3,2,1:T(8,128)(2,1)S(1)}, u32[]{:S(2)}, u32[]{:S(2)}) collective-permute-start(bf16[64,1,5,128]{0,3,2,1:T(8,128)(2,1)S(1)} %dynamic-slice_convert_fusion), channel_id=1, source_target_pairs={{0,8},{8,0},{16,24},{24,16},{32,40},{40,32},{48,56},{56,48},{64,72... | collective-permute-start | bytes 245768 | tf_op jit(solution)/shard_map/ppermute | solution.py:18
Sparse Core Ops, SparseCore 0:
  10.6 90.7 all-gather.1

commit v3 on v1

--- a/solution.py
+++ b/solution.py
@@ -50,8 +50,13 @@
     return (new_max, running_sum, output)
 
 
-def tensor_total(partial_value):
-    return lax.psum(partial_value.astype(jnp.bfloat16), "tp")
+def output_rows(w_out):
+    parts = lax.axis_size("tp")
+    rows, width = w_out.shape
+    share = rows // parts
+    pieces = lax.all_to_all(w_out.reshape(parts, share, width), "tp", 0, 0, tiled=True)
+    mine = jnp.transpose(pieces, (1, 0, 2)).reshape(share, parts * width)
+    return lax.all_gather(mine, "req", axis=0)
 
 
 def shards(q_new, k_new, v_new, k_cache, v_cache, lengths, page_table, w_out):
@@ -62,7 +67,7 @@
     page_rows = k_cache.shape[1]
     block_rows = BLOCK_PAGES * page_rows
     scale = 1.0 / math.sqrt(HD)
-    weights_all = lax.all_gather(w_out, "req", axis=0, tiled=True)
+    weights_mine = output_rows(w_out)
     device_row = lax.axis_index("req")
     parity = device_row % 2
     request = device_row // 2
@@ -148,13 +153,12 @@
         .reshape(own_rows, local_heads * GROUP * HD)
         .astype(jnp.bfloat16)
     )
-    partial_value = lax.dot_general(
-        attention,
-        weights_all,
-        (((1,), (1,)), ((), ())),
-        preferred_element_type=jnp.float32,
-    )
-    return tensor_total(partial_value)
+    full_rows = lax.all_gather(attention, "tp", axis=1, tiled=True)
+    projected = jnp.einsum(
+        "qc,irc->qir", full_rows, weights_mine, preferred_element_type=jnp.float32
+    ).astype(jnp.bfloat16)
+    gathered = lax.all_gather(projected, "tp", axis=2, tiled=True)
+    return gathered.reshape(own_rows, -1)
 
 
 def solution(mesh):

time: 194 us -> 169 us (0.87)
  waiting for transfers between devices: 146 us -> 41.6 us
  blocking collectives: 0 us -> 71.1 us
  matrix products: 7.14 us -> 12.8 us
  local copies, waits for them, and re-layouts: 7.82 us -> 10.5 us
    psum x1 -> x0, waiting for transfers between devices: 76.8 us -> none  [tensor_total(): return lax.psum(partial_value.astype(jnp.bfloat16), 'tp')]
    all_gather x0 -> x2, blocking collectives: none -> 54.4 us  [the longest x1 28.7 us: shards(): gathered = lax.all_gather(projected, 'tp', axis=2, tiled=True)]
    all_gather x1, waiting for transfers between devices: 67.6 us -> 40.7 us  [output_rows(): return lax.all_gather(mine, 'req', axis=0)]
    all_to_all x0 -> x1, blocking collectives: none -> 16.7 us  [output_rows(): lax.all_to_all(w_out.reshape(parts, share, width), 'tp', 0, 0, tiled=True)]
    dot_general x1, matrix products: 5.84 us -> 11.5 us  [shards(): jnp.einsum('qc,irc->qir', full_rows, weights_mine, preferred_element_type...]
    reshape x0 -> x2, local copies, waits for them, and re-layouts: none -> 3.89 us  [the longest x1 2.92 us: shards(): return gathered.reshape(own_rows, -1)]
    unnamed x5 -> x10, local copies, waits for them, and re-layouts: 1.98 us -> 0.02 us
  transfers between devices with their start and end apart: 8 -> 7, of which waited for: 3 -> 2; matrix products, arithmetic and copies ran while one was open for 6% -> 5% of each run, Pallas kernels for 0% -> 0%
where the time goes in v3:
time: 169 us; the launch traced here: 166 us
  blocking collectives  71.1 us (42%)
  waiting for transfers between devices  41.6 us (25%)
  between operations  15 us (9%)
  starting transfers between devices  13 us (8%)
  matrix products  12.8 us (8%)
  local copies, waits for them, and re-layouts  10.5 us (6%)
  other arithmetic  2.26 us (1%)
    all_gather x1, waiting for transfers between devices, output_rows(): return lax.all_gather(mine, 'req', axis=0)  40.7 us
    all_gather x1, blocking collectives, shards(): gathered = lax.all_gather(projected, 'tp', axis=2, tiled=True)  28.7 us
    all_gather x1, blocking collectives, shards(): full_rows = lax.all_gather(attention, 'tp', axis=1, tiled=True)  25.7 us
    all_to_all x1, blocking collectives, output_rows(): lax.all_to_all(w_out.reshape(parts, share, width), 'tp', 0, 0, tiled=True)  16.7 us
    ppermute x6, starting transfers between devices, from_partner(): lax.ppermute(value, axis, [(i, i ^ 1 << distance) for i in range(lax.axis...  13 us
    dot_general x1, matrix products, shards(): jnp.einsum('qc,irc->qir', full_rows, weights_mine, preferred_element_type...  11.5 us
  transfers between devices with their start and end apart: 7, of which 2 were waited for; matrix products, arithmetic and copies ran while one was open for 5% of the time, Pallas kernels for 0%

profile of v3, /device:TPU:6, one launch (start us, length us, event | category | flops | bytes accessed | tf_op | source)
XLA Modules:
  0.0 166.3 jit_solution(1819094608172669467)
XLA Ops:
  6.6 1.0 reshape.303
  7.6 16.7 %all_to_all.5 = bf16[8,10,640]{2,1,0:T(8,128)(2,1)S(1)} all-to-all(bf16[8,10,640]{2,1,0:T(8,128)(2,1)S(1)} %reshape.303), channel_id=1, replica_groups=mesh['req'=64,'tp'=8] {'tp'}, dimensions={0} | all-to-all | bytes 204800 | tf_op jit(solution)/shard_map/all_to_all | solution.py:57
  24.2 0.7 all_gather_reshape.3
  25.2 0.6 dynamic_slice.27
  27.0 1.9 %collective-permute-start.1 = (bf16[64,5,128]{2,1,0:T(8,128)(2,1)S(1)}, bf16[64,5,128]{2,1,0:T(8,128)(2,1)S(1)}, u32[]{:S(2)}, u32[]{:S(2)}) collective-permute-start(bf16[64,5,128]{2,1,0:T(8,128)(2,1)S(1)} %fusion.31), channel_id=1, source_target_pairs={{0,8},{8,0},{16,24},{24,16},{32,40},{40,32},{48,56},{56,48},{64,72... | collective-permute-start | bytes 245768 | tf_op jit(solution)/shard_map/ppermute | solution.py:18
  29.0 2.4 %collective-permute-start = (bf16[64,1,128]{2,0,1:T(8,128)(2,1)S(1)}, bf16[64,1,128]{2,0,1:T(8,128)(2,1)S(1)}, u32[]{:S(2)}, u32[]{:S(2)}) collective-permute-start(bf16[64,1,128]{2,0,1:T(8,128)(2,1)S(1)} %bitcast.153), channel_id=1, source_target_pairs={{0,8},{8,0},{16,24},{24,16},{32,40},{40,32},{48,56},{56,48},{64,72... | collective-permute-start | bytes 49160 | tf_op jit(solution)/shard_map/ppermute | solution.py:18
  31.4 1.9 %collective-permute-start.2 = (bf16[64,1,128]{2,0,1:T(8,128)(2,1)S(1)}, bf16[64,1,128]{2,0,1:T(8,128)(2,1)S(1)}, u32[]{:S(2)}, u32[]{:S(2)}) collective-permute-start(bf16[64,1,128]{2,0,1:T(8,128)(2,1)S(1)} %bitcast.154), channel_id=1, source_target_pairs={{0,8},{8,0},{16,24},{24,16},{32,40},{40,32},{48,56},{56,48},{64,72... | collective-permute-start | bytes 49160 | tf_op jit(solution)/shard_map/ppermute | solution.py:18
  34.9 5.2 %while.14 = (s32[]{:T(128)}, f32[1,5,128]{2,1,0:T(8,128)S(1)}, f32[1,5,128]{2,1,0:T(8,128)S(1)}, f32[128,1,5,128]{0,3,2,1:T(8,128)S(1)}, s32[]{:T(128)}, /*index...) while((s32[]{:T(128)}, f32[1,5,128]{2,1,0:T(8,128)S(1)}, ...), condition=%wide.region_5.6_spmd, body=%wide.region_2.5_spmd.sunk | while | flops 170889632 | bytes 5585255 | solution.py:127
  35.1 1.6 gather_fusion
  36.7 0.6 fusion.85
  37.3 0.4 bitcast_reduce_fusion.2
  37.7 1.6 gather_fusion.1
  39.3 0.5 fusion.88
  39.8 0.3 fusion.87
  40.2 2.4 %collective-permute-start.3 = (bf16[1,5,64]{2,1,0:T(8,128)(2,1)S(1)}, bf16[1,5,64]{2,1,0:T(8,128)(2,1)S(1)}, u32[]{:S(2)}, u32[]{:S(2)}) collective-permute-start(bf16[1,5,64]{2,1,0:T(8,128)(2,1)S(1)} %dynamic-slice_convert_fusion.2), channel_id=1, source_target_pairs={{0,8},{8,0},{16,24},{24,16},{32,40},{40,32},{48,56},{56,48},{64,72... | collective-permute-start | bytes 1928 | tf_op jit(solution)/shard_map/ppermute | solution.py:18
  42.7 1.9 %collective-permute-start.5 = (bf16[1,5,64]{2,1,0:T(8,128)(2,1)S(1)}, bf16[1,5,64]{2,1,0:T(8,128)(2,1)S(1)}, u32[]{:S(2)}, u32[]{:S(2)}) collective-permute-start(bf16[1,5,64]{2,1,0:T(8,128)(2,1)S(1)} %dynamic-slice_convert_fusion.1), channel_id=1, source_target_pairs={{0,8},{8,0},{16,24},{24,16},{32,40},{40,32},{48,56},{56,48},{64,72... | collective-permute-start | bytes 1928 | tf_op jit(solution)/shard_map/ppermute | solution.py:18
  44.8 2.4 %collective-permute-start.4 = (bf16[64,1,5,128]{0,3,2,1:T(8,128)(2,1)S(1)}, bf16[64,1,5,128]{0,3,2,1:T(8,128)(2,1)S(1)}, u32[]{:S(2)}, u32[]{:S(2)}) collective-permute-start(bf16[64,1,5,128]{0,3,2,1:T(8,128)(2,1)S(1)} %dynamic-slice_convert_fusion), channel_id=1, source_target_pairs={{0,8},{8,0},{16,24},{24,16},{32,40},{40,32},{48,56},{56,48},{64,72... | collective-permute-start | bytes 245768 | tf_op jit(solution)/shard_map/ppermute | solution.py:18
  47.3 0.9 collective-permute-done.4
  48.5 25.7 %all_gather.9 = bf16[64,5120]{1,0:T(8,128)(2,1)S(1)} all-gather(bf16[64,640]{1,0:T(8,128)(2,1)S(1)} %copy.41), channel_id=1, replica_groups=mesh['req'=64,'tp'=8] {'tp'}, dimensions={1}, use_global_device_ids=true | all-gather | bytes 737280 | tf_op jit(solution)/shard_map/all_gather | solution.py:156
  74.2 40.7 %all-gather.2.cloned.1.call-done = bf16[64,10,5120]{2,1,0:T(8,128)(2,1)} async-done(((bf16[1,10,5120]{2,1,0:T(8,128)(2,1)}), bf16[64,10,5120]{2,1,0:T(8,128)(2,1)}) %all-gather.2.cloned.1.call-update) | async-done | bytes 6553616 | tf_op jit(solution)/shard_map/all_gather | solution.py:59
  114.8 11.5 %fusion.23 = bf16[64,64,10]{1,0,2:T(8,128)(2,1)S(1)} fusion(bf16[64,10,5120]{2,1,0:T(8,128)(2,1)} %all-gather.2.cloned.1.call-done, bf16[64,5120]{1,0:T(8,128)(2,1)S(1)} %all_gather.9), kind=kOutput, calls=%fused_computation.37 | convolution fusion | flops 419471360 | bytes 7290880 | tf_op jit(solution)/shard_map/qc,irc->qir/dot_general | solution.py:157
  126.3 28.7 %all_gather.11 = bf16[64,64,80]{1,0,2:T(8,128)(2,1)S(1)} all-gather(bf16[64,64,10]{1,0,2:T(8,128)(2,1)S(1)} %fusion.23), channel_id=1, replica_groups=mesh['req'=64,'tp'=8] {'tp'}, dimensions={2}, use_global_device_ids=true | all-gather | bytes 737280 | tf_op jit(solution)/shard_map/all_gather | solution.py:160
  155.1 1.5 copy.34
  156.5 2.9 %reshape.304 = bf16[64,5120]{1,0:T(8,128)(2,1)} reshape(bf16[64,64,80]{2,1,0:T(8,128)(2,1)S(1)} %copy.34) | data formatting | bytes 1310720 | tf_op jit(solution)/shard_map/reshape | solution.py:161
  (51 shorter events, 2.5 us)
Async XLA Ops:
  6.5 27.4 %copy-start = (s32[32,32]{1,0:T(8,128)S(1)}, s32[32,32]{1,0:T(8,128)}, u32[]{:S(2)}) copy-start(s32[32,32]{1,0:T(8,128)} %param.16) | copy-start | bytes 12292
  6.5 18.5 %copy-start.1 = (bf16[64,640]{1,0:T(8,128)(2,1)S(1)}, bf16[64,640]{1,0:T(8,128)(2,1)}, u32[]{:S(2)}) copy-start(bf16[64,640]{1,0:T(8,128)(2,1)} %param.10) | copy-start | bytes 245764
  6.5 18.6 %copy-start.4 = (s32[32]{0:T(128)S(1)}, s32[32]{0:T(128)}, u32[]{:S(2)}) copy-start(s32[32]{0:T(128)} %param.15) | copy-start | bytes 388
  6.5 19.8 %copy-start.2 = (bf16[64,128]{1,0:T(8,128)(2,1)S(1)}, bf16[64,128]{1,0:T(8,128)(2,1)}, u32[]{:S(2)}) copy-start(bf16[64,128]{1,0:T(8,128)(2,1)} %param.11) | copy-start | bytes 49156
  6.5 108.3 %all-gather.2.cloned.1.call-start = ((), (), s32[]{:S(2)}) async-start(), calls=%async_computation.1 | async-start | bytes 10649600 | tf_op jit(solution)/shard_map/all_gather | solution.py:59
  25.2 6.2 %copy-start.3 = (bf16[64,128]{1,0:T(8,128)(2,1)S(1)}, bf16[64,128]{1,0:T(8,128)(2,1)}, u32[]{:S(2)}) copy-start(bf16[64,128]{1,0:T(8,128)(2,1)} %param.12) | copy-start | bytes 49156
  27.0 7.0 %collective-permute-start.1 = (bf16[64,5,128]{2,1,0:T(8,128)(2,1)S(1)}, bf16[64,5,128]{2,1,0:T(8,128)(2,1)S(1)}, u32[]{:S(2)}, u32[]{:S(2)}) collective-permute-start(bf16[64,5,128]{2,1,0:T(8,128)(2,1)S(1)} %fusion.31), channel_id=1, source_target_pairs={{0,8},{8,0},{16,24},{24,16},{32,40},{40,32},{48,56},{56,48},{64,72... | collective-permute-start | bytes 245768 | tf_op jit(solution)/shard_map/ppermute | solution.py:18
  29.0 5.2 %collective-permute-start = (bf16[64,1,128]{2,0,1:T(8,128)(2,1)S(1)}, bf16[64,1,128]{2,0,1:T(8,128)(2,1)S(1)}, u32[]{:S(2)}, u32[]{:S(2)}) collective-permute-start(bf16[64,1,128]{2,0,1:T(8,128)(2,1)S(1)} %bitcast.153), channel_id=1, source_target_pairs={{0,8},{8,0},{16,24},{24,16},{32,40},{40,32},{48,56},{56,48},{64,72... | collective-permute-start | bytes 49160 | tf_op jit(solution)/shard_map/ppermute | solution.py:18
  31.4 3.3 %collective-permute-start.2 = (bf16[64,1,128]{2,0,1:T(8,128)(2,1)S(1)}, bf16[64,1,128]{2,0,1:T(8,128)(2,1)S(1)}, u32[]{:S(2)}, u32[]{:S(2)}) collective-permute-start(bf16[64,1,128]{2,0,1:T(8,128)(2,1)S(1)} %bitcast.154), channel_id=1, source_target_pairs={{0,8},{8,0},{16,24},{24,16},{32,40},{40,32},{48,56},{56,48},{64,72... | collective-permute-start | bytes 49160 | tf_op jit(solution)/shard_map/ppermute | solution.py:18
  40.2 7.0 %collective-permute-start.3 = (bf16[1,5,64]{2,1,0:T(8,128)(2,1)S(1)}, bf16[1,5,64]{2,1,0:T(8,128)(2,1)S(1)}, u32[]{:S(2)}, u32[]{:S(2)}) collective-permute-start(bf16[1,5,64]{2,1,0:T(8,128)(2,1)S(1)} %dynamic-slice_convert_fusion.2), channel_id=1, source_target_pairs={{0,8},{8,0},{16,24},{24,16},{32,40},{40,32},{48,56},{56,48},{64,72... | collective-permute-start | bytes 1928 | tf_op jit(solution)/shard_map/ppermute | solution.py:18
  42.7 4.5 %collective-permute-start.5 = (bf16[1,5,64]{2,1,0:T(8,128)(2,1)S(1)}, bf16[1,5,64]{2,1,0:T(8,128)(2,1)S(1)}, u32[]{:S(2)}, u32[]{:S(2)}) collective-permute-start(bf16[1,5,64]{2,1,0:T(8,128)(2,1)S(1)} %dynamic-slice_convert_fusion.1), channel_id=1, source_target_pairs={{0,8},{8,0},{16,24},{24,16},{32,40},{40,32},{48,56},{56,48},{64,72... | collective-permute-start | bytes 1928 | tf_op jit(solution)/shard_map/ppermute | solution.py:18
  44.8 3.4 %collective-permute-start.4 = (bf16[64,1,5,128]{0,3,2,1:T(8,128)(2,1)S(1)}, bf16[64,1,5,128]{0,3,2,1:T(8,128)(2,1)S(1)}, u32[]{:S(2)}, u32[]{:S(2)}) collective-permute-start(bf16[64,1,5,128]{0,3,2,1:T(8,128)(2,1)S(1)} %dynamic-slice_convert_fusion), channel_id=1, source_target_pairs={{0,8},{8,0},{16,24},{24,16},{32,40},{40,32},{48,56},{56,48},{64,72... | collective-permute-start | bytes 245768 | tf_op jit(solution)/shard_map/ppermute | solution.py:18
Sparse Core Ops, SparseCore 0:
  25.1 89.6 all-gather.1

commit v4 on v3

--- a/solution.py
+++ b/solution.py
@@ -56,7 +56,9 @@
     share = rows // parts
     pieces = lax.all_to_all(w_out.reshape(parts, share, width), "tp", 0, 0, tiled=True)
     mine = jnp.transpose(pieces, (1, 0, 2)).reshape(share, parts * width)
-    return lax.all_gather(mine, "req", axis=0)
+    padded = -(-share // 8) * 8
+    mine = jnp.pad(mine, ((0, padded - share), (0, 0)))
+    return lax.all_gather(mine, "req", axis=0, tiled=True), share
 
 
 def shards(q_new, k_new, v_new, k_cache, v_cache, lengths, page_table, w_out):
@@ -67,7 +69,7 @@
     page_rows = k_cache.shape[1]
     block_rows = BLOCK_PAGES * page_rows
     scale = 1.0 / math.sqrt(HD)
-    weights_mine = output_rows(w_out)
+    weights_mine, share = output_rows(w_out)
     device_row = lax.axis_index("req")
     parity = device_row % 2
     request = device_row // 2
@@ -154,9 +156,14 @@
         .astype(jnp.bfloat16)
     )
     full_rows = lax.all_gather(attention, "tp", axis=1, tiled=True)
-    projected = jnp.einsum(
-        "qc,irc->qir", full_rows, weights_mine, preferred_element_type=jnp.float32
-    ).astype(jnp.bfloat16)
+    projected = lax.dot_general(
+        full_rows,
+        weights_mine,
+        (((1,), (1,)), ((), ())),
+        preferred_element_type=jnp.float32,
+    )
+    blocks = weights_mine.shape[0] // (-(-share // 8) * 8)
+    projected = projected.reshape(own_rows, blocks, -1)[:, :, :share].astype(jnp.bfloat16)
     gathered = lax.all_gather(projected, "tp", axis=2, tiled=True)
     return gathered.reshape(own_rows, -1)
 

time: 169 us -> 165 us (0.976)
  waiting for transfers between devices: 41.6 us -> 24.1 us
  local copies, waits for them, and re-layouts: 10.5 us -> 20.5 us
  other arithmetic: 2.26 us -> 5.28 us
  blocking collectives: 71.1 us -> 73 us
  matrix products: 12.8 us -> 11.1 us
    all_gather x1, waiting for transfers between devices: 40.7 us -> 23.2 us  [output_rows(): return (lax.all_gather(mine, 'req', axis=0, tiled=True), share)]
    gather x1 -> x4, local copies, waits for them, and re-layouts: 1.61 us -> 6.48 us  [visit(): block_values = v_cache[slots].reshape(block_rows, local_heads, HD)]
    gather x1 -> x4, local copies, waits for them, and re-layouts: 1.61 us -> 6.47 us  [visit(): block_keys = k_cache[slots].reshape(block_rows, local_heads, HD)]
    dot_general x1, matrix products: 11.5 us -> 7.29 us  [shards(): lax.dot_general(full_rows, weights_mine, (((1,), (1,)), ((), ())), prefer...]
    all_gather x1, blocking collectives: 25.7 us -> 27.8 us  [shards(): full_rows = lax.all_gather(attention, 'tp', axis=1, tiled=True)]
    and x1 -> x4, other arithmetic: 0.63 us -> 2.52 us  [visit(): usable = jnp.repeat(logical < last_page, page_rows) & (key_places < length)]
  transfers between devices with their start and end apart: 7 -> 7, of which waited for: 2 -> 2; matrix products, arithmetic and copies ran while one was open for 5% -> 14% of each run, Pallas kernels for 0% -> 0%
where the time goes in v4:
time: 165 us; the launch traced here: 162 us
  blocking collectives  73 us (44%)
  waiting for transfers between devices  24.1 us (15%)
  local copies, waits for them, and re-layouts  20.5 us (12%)
  between operations  15 us (9%)
  starting transfers between devices  13 us (8%)
  matrix products  11.1 us (7%)
  other arithmetic  5.28 us (3%)
    all_gather x1, blocking collectives, shards(): gathered = lax.all_gather(projected, 'tp', axis=2, tiled=True)  28.5 us
    all_gather x1, blocking collectives, shards(): full_rows = lax.all_gather(attention, 'tp', axis=1, tiled=True)  27.8 us
    all_gather x1, waiting for transfers between devices, output_rows(): return (lax.all_gather(mine, 'req', axis=0, tiled=True), share)  23.2 us
    all_to_all x1, blocking collectives, output_rows(): lax.all_to_all(w_out.reshape(parts, share, width), 'tp', 0, 0, tiled=True)  16.7 us
    ppermute x6, starting transfers between devices, from_partner(): lax.ppermute(value, axis, [(i, i ^ 1 << distance) for i in range(lax.axis...  12.9 us
    dot_general x1, matrix products, shards(): lax.dot_general(full_rows, weights_mine, (((1,), (1,)), ((), ())), prefer...  7.29 us
    gather x4, local copies, waits for them, and re-layouts, visit(): block_values = v_cache[slots].reshape(block_rows, local_heads, HD)  6.48 us
    gather x4, local copies, waits for them, and re-layouts, visit(): block_keys = k_cache[slots].reshape(block_rows, local_heads, HD)  6.47 us
  transfers between devices with their start and end apart: 7, of which 2 were waited for; matrix products, arithmetic and copies ran while one was open for 14% of the time, Pallas kernels for 0%

profile of v4, /device:TPU:6, one launch (start us, length us, event | category | flops | bytes accessed | tf_op | source)
XLA Modules:
  0.0 162.3 jit_solution(7969564444890126911)
XLA Ops:
  6.6 1.0 reshape.310
  7.6 16.7 %all_to_all.5 = bf16[8,10,640]{2,1,0:T(8,128)(2,1)S(1)} all-to-all(bf16[8,10,640]{2,1,0:T(8,128)(2,1)S(1)} %reshape.310), channel_id=1, replica_groups=mesh['req'=64,'tp'=8] {'tp'}, dimensions={0} | all-to-all | bytes 204800 | tf_op jit(solution)/shard_map/all_to_all | solution.py:57
  27.0 1.9 %collective-permute-start.1 = (bf16[64,5,128]{2,1,0:T(8,128)(2,1)S(1)}, bf16[64,5,128]{2,1,0:T(8,128)(2,1)S(1)}, u32[]{:S(2)}, u32[]{:S(2)}) collective-permute-start(bf16[64,5,128]{2,1,0:T(8,128)(2,1)S(1)} %fusion.25), channel_id=1, source_target_pairs={{0,8},{8,0},{16,24},{24,16},{32,40},{40,32},{48,56},{56,48},{64,72... | collective-permute-start | bytes 245768 | tf_op jit(solution)/shard_map/ppermute | solution.py:18
  29.0 2.4 %collective-permute-start = (bf16[64,1,128]{2,0,1:T(8,128)(2,1)S(1)}, bf16[64,1,128]{2,0,1:T(8,128)(2,1)S(1)}, u32[]{:S(2)}, u32[]{:S(2)}) collective-permute-start(bf16[64,1,128]{2,0,1:T(8,128)(2,1)S(1)} %bitcast.160), channel_id=1, source_target_pairs={{0,8},{8,0},{16,24},{24,16},{32,40},{40,32},{48,56},{56,48},{64,72... | collective-permute-start | bytes 49160 | tf_op jit(solution)/shard_map/ppermute | solution.py:18
  31.4 1.9 %collective-permute-start.2 = (bf16[64,1,128]{2,0,1:T(8,128)(2,1)S(1)}, bf16[64,1,128]{2,0,1:T(8,128)(2,1)S(1)}, u32[]{:S(2)}, u32[]{:S(2)}) collective-permute-start(bf16[64,1,128]{2,0,1:T(8,128)(2,1)S(1)} %bitcast.161), channel_id=1, source_target_pairs={{0,8},{8,0},{16,24},{24,16},{32,40},{40,32},{48,56},{56,48},{64,72... | collective-permute-start | bytes 49160 | tf_op jit(solution)/shard_map/ppermute | solution.py:18
  34.9 20.8 %while.14 = (s32[]{:T(128)}, f32[1,5,128]{2,1,0:T(8,128)S(1)}, f32[1,5,128]{2,1,0:T(8,128)S(1)}, f32[128,1,5,128]{0,3,2,1:T(8,128)S(1)}, s32[]{:T(128)}, /*index...) while((s32[]{:T(128)}, f32[1,5,128]{2,1,0:T(8,128)S(1)}, ...), condition=%wide.region_5.6_spmd, body=%wide.region_2.5_spmd.sunk | while | flops 170889632 | bytes 5585255 | solution.py:129
  35.1 1.6 gather_fusion
  37.7 1.6 gather_fusion.1
  40.2 1.6 %gather_fusion = bf16[4,128,128]{2,1,0:T(8,128)(2,1)S(1)} fusion(bf16[16,128,128]{2,1,0:T(8,128)(2,1)} %get-tuple-element.297, s32[1024]{0:T(1024)S(1)} %pad_clamp_fusion.2), kind=kCustom, calls=%fused_computation.clone.1 | custom fusion | bytes 262160 | tf_op jit(solution)/shard_map/while/body/gather | solution.py:120
  42.9 1.6 gather_fusion.1
  45.4 1.6 gather_fusion
  48.1 1.6 gather_fusion.1
  50.6 1.6 gather_fusion
  53.3 1.6 %gather_fusion.1 = bf16[4,128,128]{2,1,0:T(8,128)(2,1)S(1)} fusion(bf16[16,128,128]{2,1,0:T(8,128)(2,1)} %get-tuple-element.299, s32[1024]{0:T(1024)S(1)} %pad_clamp_fusion.2), kind=kCustom, calls=%fused_computation.1.clone.1 | custom fusion | bytes 262160 | tf_op jit(solution)/shard_map/while/body/gather | solution.py:121
  55.8 2.4 %collective-permute-start.3 = (bf16[1,5,64]{2,1,0:T(8,128)(2,1)S(1)}, bf16[1,5,64]{2,1,0:T(8,128)(2,1)S(1)}, u32[]{:S(2)}, u32[]{:S(2)}) collective-permute-start(bf16[1,5,64]{2,1,0:T(8,128)(2,1)S(1)} %dynamic-slice_convert_fusion.2), channel_id=1, source_target_pairs={{0,8},{8,0},{16,24},{24,16},{32,40},{40,32},{48,56},{56,48},{64,72... | collective-permute-start | bytes 1928 | tf_op jit(solution)/shard_map/ppermute | solution.py:18
  58.3 1.9 %collective-permute-start.5 = (bf16[1,5,64]{2,1,0:T(8,128)(2,1)S(1)}, bf16[1,5,64]{2,1,0:T(8,128)(2,1)S(1)}, u32[]{:S(2)}, u32[]{:S(2)}) collective-permute-start(bf16[1,5,64]{2,1,0:T(8,128)(2,1)S(1)} %dynamic-slice_convert_fusion.1), channel_id=1, source_target_pairs={{0,8},{8,0},{16,24},{24,16},{32,40},{40,32},{48,56},{56,48},{64,72... | collective-permute-start | bytes 1928 | tf_op jit(solution)/shard_map/ppermute | solution.py:18
  60.3 2.4 %collective-permute-start.4 = (bf16[64,1,5,128]{0,3,2,1:T(8,128)(2,1)S(1)}, bf16[64,1,5,128]{0,3,2,1:T(8,128)(2,1)S(1)}, u32[]{:S(2)}, u32[]{:S(2)}) collective-permute-start(bf16[64,1,5,128]{0,3,2,1:T(8,128)(2,1)S(1)} %dynamic-slice_convert_fusion), channel_id=1, source_target_pairs={{0,8},{8,0},{16,24},{24,16},{32,40},{40,32},{48,56},{56,48},{64,72... | collective-permute-start | bytes 245768 | tf_op jit(solution)/shard_map/ppermute | solution.py:18
  62.8 0.9 collective-permute-done.4
  63.9 27.8 %all_gather.9 = bf16[64,5120]{0,1:T(8,128)(2,1)S(1)} all-gather(bf16[64,640]{0,1:T(8,128)(2,1)S(1)} %bitcast.158), channel_id=1, replica_groups=mesh['req'=64,'tp'=8] {'tp'}, dimensions={1}, use_global_device_ids=true | all-gather | bytes 737280 | tf_op jit(solution)/shard_map/all_gather | solution.py:158
  91.7 23.2 %all-gather.2.cloned.1.call-done = bf16[1024,5120]{1,0:T(8,128)(2,1)} async-done(((bf16[16,5120]{1,0:T(8,128)(2,1)}), bf16[1024,5120]{1,0:T(8,128)(2,1)}) %all-gather.2.cloned.1.call-update) | async-done | bytes 10485776 | tf_op jit(solution)/shard_map/all_gather | solution.py:61
  114.8 7.3 %convolution_convert_fusion = bf16[64,1024]{1,0:T(8,128)(2,1)S(1)} fusion(bf16[64,5120]{0,1:T(8,128)(2,1)S(1)} %all_gather.9, bf16[1024,5120]{1,0:T(8,128)(2,1)} %all-gather.2.cloned.1.call-done), kind=kOutput, calls=%fused_computation.35 | convolution fusion | flops 671154176 | bytes 11272192 | tf_op jit(solution)/shard_map/dot_general | solution.py:159
  122.5 28.5 %all_gather.11 = bf16[64,64,80]{1,0,2:T(8,128)(2,1)S(1)} all-gather(bf16[64,64,10]{1,0,2:T(8,128)(2,1)S(1)} %copy.39), channel_id=1, replica_groups=mesh['req'=64,'tp'=8] {'tp'}, dimensions={2}, use_global_device_ids=true | all-gather | bytes 737280 | tf_op jit(solution)/shard_map/all_gather | solution.py:167
  151.1 1.5 copy.40
  152.5 2.9 %reshape.313 = bf16[64,5120]{1,0:T(8,128)(2,1)} reshape(bf16[64,64,80]{2,1,0:T(8,128)(2,1)S(1)} %copy.40) | data formatting | bytes 1310720 | tf_op jit(solution)/shard_map/reshape | solution.py:168
  (93 shorter events, 11.4 us)
Async XLA Ops:
  6.5 27.4 %copy-start = (s32[32,32]{1,0:T(8,128)S(1)}, s32[32,32]{1,0:T(8,128)}, u32[]{:S(2)}) copy-start(s32[32,32]{1,0:T(8,128)} %param.16) | copy-start | bytes 12292
  6.5 18.5 %copy-start.1 = (bf16[64,640]{1,0:T(8,128)(2,1)S(1)}, bf16[64,640]{1,0:T(8,128)(2,1)}, u32[]{:S(2)}) copy-start(bf16[64,640]{1,0:T(8,128)(2,1)} %param.10) | copy-start | bytes 245764
  6.5 18.6 %copy-start.4 = (s32[32]{0:T(128)S(1)}, s32[32]{0:T(128)}, u32[]{:S(2)}) copy-start(s32[32]{0:T(128)} %param.15) | copy-start | bytes 388
  6.5 19.8 %copy-start.2 = (bf16[64,128]{1,0:T(8,128)(2,1)S(1)}, bf16[64,128]{1,0:T(8,128)(2,1)}, u32[]{:S(2)}) copy-start(bf16[64,128]{1,0:T(8,128)(2,1)} %param.11) | copy-start | bytes 49156
  6.5 108.3 %all-gather.2.cloned.1.call-start = ((), (), s32[]{:S(2)}) async-start(), calls=%async_computation.1 | async-start | bytes 10649600 | tf_op jit(solution)/shard_map/all_gather | solution.py:61
  25.2 6.2 %copy-start.3 = (bf16[64,128]{1,0:T(8,128)(2,1)S(1)}, bf16[64,128]{1,0:T(8,128)(2,1)}, u32[]{:S(2)}) copy-start(bf16[64,128]{1,0:T(8,128)(2,1)} %param.12) | copy-start | bytes 49156
  27.0 7.0 %collective-permute-start.1 = (bf16[64,5,128]{2,1,0:T(8,128)(2,1)S(1)}, bf16[64,5,128]{2,1,0:T(8,128)(2,1)S(1)}, u32[]{:S(2)}, u32[]{:S(2)}) collective-permute-start(bf16[64,5,128]{2,1,0:T(8,128)(2,1)S(1)} %fusion.25), channel_id=1, source_target_pairs={{0,8},{8,0},{16,24},{24,16},{32,40},{40,32},{48,56},{56,48},{64,72... | collective-permute-start | bytes 245768 | tf_op jit(solution)/shard_map/ppermute | solution.py:18
  29.0 5.2 %collective-permute-start = (bf16[64,1,128]{2,0,1:T(8,128)(2,1)S(1)}, bf16[64,1,128]{2,0,1:T(8,128)(2,1)S(1)}, u32[]{:S(2)}, u32[]{:S(2)}) collective-permute-start(bf16[64,1,128]{2,0,1:T(8,128)(2,1)S(1)} %bitcast.160), channel_id=1, source_target_pairs={{0,8},{8,0},{16,24},{24,16},{32,40},{40,32},{48,56},{56,48},{64,72... | collective-permute-start | bytes 49160 | tf_op jit(solution)/shard_map/ppermute | solution.py:18
  31.4 3.3 %collective-permute-start.2 = (bf16[64,1,128]{2,0,1:T(8,128)(2,1)S(1)}, bf16[64,1,128]{2,0,1:T(8,128)(2,1)S(1)}, u32[]{:S(2)}, u32[]{:S(2)}) collective-permute-start(bf16[64,1,128]{2,0,1:T(8,128)(2,1)S(1)} %bitcast.161), channel_id=1, source_target_pairs={{0,8},{8,0},{16,24},{24,16},{32,40},{40,32},{48,56},{56,48},{64,72... | collective-permute-start | bytes 49160 | tf_op jit(solution)/shard_map/ppermute | solution.py:18
  55.8 6.9 %collective-permute-start.3 = (bf16[1,5,64]{2,1,0:T(8,128)(2,1)S(1)}, bf16[1,5,64]{2,1,0:T(8,128)(2,1)S(1)}, u32[]{:S(2)}, u32[]{:S(2)}) collective-permute-start(bf16[1,5,64]{2,1,0:T(8,128)(2,1)S(1)} %dynamic-slice_convert_fusion.2), channel_id=1, source_target_pairs={{0,8},{8,0},{16,24},{24,16},{32,40},{40,32},{48,56},{56,48},{64,72... | collective-permute-start | bytes 1928 | tf_op jit(solution)/shard_map/ppermute | solution.py:18
  58.3 4.5 %collective-permute-start.5 = (bf16[1,5,64]{2,1,0:T(8,128)(2,1)S(1)}, bf16[1,5,64]{2,1,0:T(8,128)(2,1)S(1)}, u32[]{:S(2)}, u32[]{:S(2)}) collective-permute-start(bf16[1,5,64]{2,1,0:T(8,128)(2,1)S(1)} %dynamic-slice_convert_fusion.1), channel_id=1, source_target_pairs={{0,8},{8,0},{16,24},{24,16},{32,40},{40,32},{48,56},{56,48},{64,72... | collective-permute-start | bytes 1928 | tf_op jit(solution)/shard_map/ppermute | solution.py:18
  60.3 3.4 %collective-permute-start.4 = (bf16[64,1,5,128]{0,3,2,1:T(8,128)(2,1)S(1)}, bf16[64,1,5,128]{0,3,2,1:T(8,128)(2,1)S(1)}, u32[]{:S(2)}, u32[]{:S(2)}) collective-permute-start(bf16[64,1,5,128]{0,3,2,1:T(8,128)(2,1)S(1)} %dynamic-slice_convert_fusion), channel_id=1, source_target_pairs={{0,8},{8,0},{16,24},{24,16},{32,40},{40,32},{48,56},{56,48},{64,72... | collective-permute-start | bytes 245768 | tf_op jit(solution)/shard_map/ppermute | solution.py:18
Sparse Core Ops, SparseCore 0:
  25.1 89.6 all-gather.1

commit v5 on v4

--- a/solution.py
+++ b/solution.py
@@ -16,6 +16,13 @@
 
 def from_partner(value, axis, distance):
     return lax.ppermute(value, axis, [(i, i ^ 1 << distance) for i in range(lax.axis_size(axis))])
+
+
+def from_tp(value, shift):
+    if shift == 0:
+        return value
+    size = lax.axis_size("tp")
+    return lax.ppermute(value, "tp", [(i, (i + shift) % size) for i in range(size)])
 
 
 def rotate(values, places):
@@ -155,6 +162,7 @@
         .reshape(own_rows, local_heads * GROUP * HD)
         .astype(jnp.bfloat16)
     )
+    parts = lax.axis_size("tp")
     full_rows = lax.all_gather(attention, "tp", axis=1, tiled=True)
     projected = lax.dot_general(
         full_rows,
@@ -164,8 +172,10 @@
     )
     blocks = weights_mine.shape[0] // (-(-share // 8) * 8)
     projected = projected.reshape(own_rows, blocks, -1)[:, :, :share].astype(jnp.bfloat16)
-    gathered = lax.all_gather(projected, "tp", axis=2, tiled=True)
-    return gathered.reshape(own_rows, -1)
+    gathered = jnp.stack([from_tp(projected, shift) for shift in range(parts)])
+    sources = (lax.axis_index("tp") - jnp.arange(parts)) % parts
+    gathered = jnp.take(gathered, sources, axis=0)
+    return jnp.transpose(gathered, (1, 2, 0, 3)).reshape(own_rows, -1)
 
 
 def solution(mesh):

time: 165 us -> 203 us (1.23)
  the two profiles are of different devices: /device:TPU:6 before, /device:TPU:9 now
where the time goes in v5:
time: 203 us; the launch traced here: 202 us
  waiting for transfers between devices  74.6 us (37%)
  starting transfers between devices  42.6 us (21%)
  blocking collectives  35.6 us (18%)
  local copies, waits for them, and re-layouts  21.2 us (10%)
  between operations  15.1 us (7%)
  matrix products  9.42 us (5%)
  other arithmetic  3.57 us (2%)
    all_gather x1, waiting for transfers between devices, output_rows(): return (lax.all_gather(mine, 'req', axis=0, tiled=True), share)  40.9 us
    ppermute x7, waiting for transfers between devices, from_tp(): lax.ppermute(value, 'tp', [(i, (i + shift) % size) for i in range(size)])  32.5 us
    ppermute x7, starting transfers between devices, from_tp(): lax.ppermute(value, 'tp', [(i, (i + shift) % size) for i in range(size)])  27.1 us
    all_gather x1, blocking collectives, shards(): full_rows = lax.all_gather(attention, 'tp', axis=1, tiled=True)  21.7 us
    ppermute x6, starting transfers between devices, from_partner(): lax.ppermute(value, axis, [(i, i ^ 1 << distance) for i in range(lax.axis...  15.4 us
    all_to_all x1, blocking collectives, output_rows(): lax.all_to_all(w_out.reshape(parts, share, width), 'tp', 0, 0, tiled=True)  13.9 us
    dot_general x1, matrix products, shards(): lax.dot_general(full_rows, weights_mine, (((1,), (1,)), ((), ())), prefer...  7.29 us
    unnamed x17, local copies, waits for them, and re-layouts  5.08 us
  transfers between devices with their start and end apart: 14, of which 6 were waited for; matrix products, arithmetic and copies ran while one was open for 9% of the time, Pallas kernels for 0%

profile of v5, /device:TPU:9, one launch (start us, length us, event | category | flops | bytes accessed | tf_op | source)
XLA Modules:
  0.0 202.3 jit_solution(11156302024861886297)
XLA Ops:
  7.5 13.9 %all_to_all.5 = bf16[8,10,640]{2,1,0:T(8,128)(2,1)S(1)} all-to-all(bf16[8,10,640]{2,1,0:T(8,128)(2,1)S(1)} %reshape.364), channel_id=1, replica_groups=mesh['req'=64,'tp'=8] {'tp'}, dimensions={0} | all-to-all | bytes 204800 | tf_op jit(solution)/shard_map/all_to_all | solution.py:64
  25.1 4.9 %collective-permute-start.1 = (bf16[64,5,128]{2,1,0:T(8,128)(2,1)S(1)}, bf16[64,5,128]{2,1,0:T(8,128)(2,1)S(1)}, u32[]{:S(2)}, u32[]{:S(2)}) collective-permute-start(bf16[64,5,128]{2,1,0:T(8,128)(2,1)S(1)} %fusion.25), channel_id=1, source_target_pairs={{0,8},{8,0},{16,24},{24,16},{32,40},{40,32},{48,56},{56,48},{64,72... | collective-permute-start | bytes 245768 | tf_op jit(solution)/shard_map/ppermute | solution.py:18
  30.0 1.9 collective-permute-start
  31.9 2.4 %collective-permute-start.2 = (bf16[64,1,128]{2,0,1:T(8,128)(2,1)S(1)}, bf16[64,1,128]{2,0,1:T(8,128)(2,1)S(1)}, u32[]{:S(2)}, u32[]{:S(2)}) collective-permute-start(bf16[64,1,128]{2,0,1:T(8,128)(2,1)S(1)} %bitcast.190), channel_id=1, source_target_pairs={{0,8},{8,0},{16,24},{24,16},{32,40},{40,32},{48,56},{56,48},{64,72... | collective-permute-start | bytes 49160 | tf_op jit(solution)/shard_map/ppermute | solution.py:18
  36.0 10.4 %while.14 = (s32[]{:T(128)}, f32[1,5,128]{2,1,0:T(8,128)S(1)}, f32[1,5,128]{2,1,0:T(8,128)S(1)}, f32[128,1,5,128]{0,3,2,1:T(8,128)S(1)}, s32[]{:T(128)}, /*index...) while((s32[]{:T(128)}, f32[1,5,128]{2,1,0:T(8,128)S(1)}, ...), condition=%wide.region_5.6_spmd, body=%wide.region_2.5_spmd.sunk | while | flops 170889632 | bytes 5585255 | solution.py:136
  38.8 1.6 gather_fusion.1
  46.5 1.9 collective-permute-start.3
  48.5 2.4 %collective-permute-start.5 = (bf16[1,5,64]{2,1,0:T(8,128)(2,1)S(1)}, bf16[1,5,64]{2,1,0:T(8,128)(2,1)S(1)}, u32[]{:S(2)}, u32[]{:S(2)}) collective-permute-start(bf16[1,5,64]{2,1,0:T(8,128)(2,1)S(1)} %dynamic-slice_convert_fusion.1), channel_id=1, source_target_pairs={{0,8},{8,0},{16,24},{24,16},{32,40},{40,32},{48,56},{56,48},{64,72... | collective-permute-start | bytes 1928 | tf_op jit(solution)/shard_map/ppermute | solution.py:18
  51.0 1.9 collective-permute-start.4
  54.4 21.7 %all_gather.6 = bf16[64,5120]{0,1:T(8,128)(2,1)S(1)} all-gather(bf16[64,640]{0,1:T(8,128)(2,1)S(1)} %bitcast.187), channel_id=1, replica_groups=mesh['req'=64,'tp'=8] {'tp'}, dimensions={1}, use_global_device_ids=true | all-gather | bytes 737280 | tf_op jit(solution)/shard_map/all_gather | solution.py:166
  76.1 40.9 %all-gather.2.cloned.1.call-done = bf16[1024,5120]{1,0:T(8,128)(2,1)} async-done(((bf16[16,5120]{1,0:T(8,128)(2,1)}), bf16[1024,5120]{1,0:T(8,128)(2,1)}) %all-gather.2.cloned.1.call-update) | async-done | bytes 10485776 | tf_op jit(solution)/shard_map/all_gather | solution.py:68
  117.0 7.3 %convolution_convert_fusion = bf16[64,1024]{1,0:T(8,128)(2,1)S(1)} fusion(bf16[64,5120]{0,1:T(8,128)(2,1)S(1)} %all_gather.6, bf16[1024,5120]{1,0:T(8,128)(2,1)} %all-gather.2.cloned.1.call-done), kind=kOutput, calls=%fused_computation.37 | convolution fusion | flops 671154176 | bytes 11272192 | tf_op jit(solution)/shard_map/dot_general | solution.py:167
  124.5 3.1 %collective-permute-start.6 = (bf16[64,64,10]{0,2,1:T(8,128)(2,1)S(1)}, bf16[64,64,10]{0,2,1:T(8,128)(2,1)S(1)}, u32[]{:S(2)}, u32[]{:S(2)}) collective-permute-start(bf16[64,64,10]{0,2,1:T(8,128)(2,1)S(1)} %bitcast.176), channel_id=1, source_target_pairs={{0,1},{1,2},{2,3},{3,4},{4,5},{5,6},{6,7},{7,0},{8,9},{9,10},{10,1... | collective-permute-start | bytes 245768 | tf_op jit(solution)/shard_map/ppermute | solution.py:25
  128.3 5.2 %collective-permute-start.7 = (bf16[64,64,10]{0,2,1:T(8,128)(2,1)S(1)}, bf16[64,64,10]{0,2,1:T(8,128)(2,1)S(1)}, u32[]{:S(2)}, u32[]{:S(2)}) collective-permute-start(bf16[64,64,10]{0,2,1:T(8,128)(2,1)S(1)} %bitcast.178), channel_id=1, source_target_pairs={{0,2},{1,3},{2,4},{3,5},{4,6},{5,7},{6,0},{7,1},{8,10},{9,11},{10,... | collective-permute-start | bytes 245768 | tf_op jit(solution)/shard_map/ppermute | solution.py:25
  133.6 2.3 %collective-permute-start.8 = (bf16[64,64,10]{0,2,1:T(8,128)(2,1)S(1)}, bf16[64,64,10]{0,2,1:T(8,128)(2,1)S(1)}, u32[]{:S(2)}, u32[]{:S(2)}) collective-permute-start(bf16[64,64,10]{0,2,1:T(8,128)(2,1)S(1)} %bitcast.179), channel_id=1, source_target_pairs={{0,3},{1,4},{2,5},{3,6},{4,7},{5,0},{6,1},{7,2},{8,11},{9,12},{10,... | collective-permute-start | bytes 245768 | tf_op jit(solution)/shard_map/ppermute | solution.py:25
  135.8 4.8 %collective-permute-start.9 = (bf16[64,64,10]{0,2,1:T(8,128)(2,1)S(1)}, bf16[64,64,10]{0,2,1:T(8,128)(2,1)S(1)}, u32[]{:S(2)}, u32[]{:S(2)}) collective-permute-start(bf16[64,64,10]{0,2,1:T(8,128)(2,1)S(1)} %bitcast.180), channel_id=1, source_target_pairs={{0,4},{1,5},{2,6},{3,7},{4,0},{5,1},{6,2},{7,3},{8,12},{9,13},{10,... | collective-permute-start | bytes 245768 | tf_op jit(solution)/shard_map/ppermute | solution.py:25
  140.6 3.3 %collective-permute-start.10 = (bf16[64,64,10]{0,2,1:T(8,128)(2,1)S(1)}, bf16[64,64,10]{0,2,1:T(8,128)(2,1)S(1)}, u32[]{:S(2)}, u32[]{:S(2)}) collective-permute-start(bf16[64,64,10]{0,2,1:T(8,128)(2,1)S(1)} %bitcast.181), channel_id=1, source_target_pairs={{0,5},{1,6},{2,7},{3,0},{4,1},{5,2},{6,3},{7,4},{8,13},{9,14},{10,... | collective-permute-start | bytes 245768 | tf_op jit(solution)/shard_map/ppermute | solution.py:25
  144.0 4.1 %collective-permute-start.11 = (bf16[64,64,10]{0,2,1:T(8,128)(2,1)S(1)}, bf16[64,64,10]{0,2,1:T(8,128)(2,1)S(1)}, u32[]{:S(2)}, u32[]{:S(2)}) collective-permute-start(bf16[64,64,10]{0,2,1:T(8,128)(2,1)S(1)} %bitcast.182), channel_id=1, source_target_pairs={{0,6},{1,7},{2,0},{3,1},{4,2},{5,3},{6,4},{7,5},{8,14},{9,15},{10,... | collective-permute-start | bytes 245768 | tf_op jit(solution)/shard_map/ppermute | solution.py:25
  148.8 4.3 %collective-permute-start.12 = (bf16[64,64,10]{0,2,1:T(8,128)(2,1)S(1)}, bf16[64,64,10]{0,2,1:T(8,128)(2,1)S(1)}, u32[]{:S(2)}, u32[]{:S(2)}) collective-permute-start(bf16[64,64,10]{0,2,1:T(8,128)(2,1)S(1)} %bitcast.183), channel_id=1, source_target_pairs={{0,7},{1,0},{2,1},{3,2},{4,3},{5,4},{6,5},{7,6},{8,15},{9,8},{10,9... | collective-permute-start | bytes 245768 | tf_op jit(solution)/shard_map/ppermute | solution.py:25
  153.8 8.7 %collective-permute-done.8 = bf16[64,64,10]{0,2,1:T(8,128)(2,1)S(1)} collective-permute-done((bf16[64,64,10]{0,2,1:T(8,128)(2,1)S(1)}, bf16[64,64,10]{0,2,1:T(8,128)(2,1)S(1)}, u32[]{:S(2)}, u32[]{:S(2)}) %collective-permute-start.8) | collective-permute-done | bytes 81952 | tf_op jit(solution)/shard_map/ppermute | solution.py:25
  164.0 9.0 %collective-permute-done.10 = bf16[64,64,10]{0,2,1:T(8,128)(2,1)S(1)} collective-permute-done((bf16[64,64,10]{0,2,1:T(8,128)(2,1)S(1)}, bf16[64,64,10]{0,2,1:T(8,128)(2,1)S(1)}, u32[]{:S(2)}, u32[]{:S(2)}) %collective-permute-start.10) | collective-permute-done | bytes 81952 | tf_op jit(solution)/shard_map/ppermute | solution.py:25
  173.8 4.1 %collective-permute-done.11 = bf16[64,64,10]{0,2,1:T(8,128)(2,1)S(1)} collective-permute-done((bf16[64,64,10]{0,2,1:T(8,128)(2,1)S(1)}, bf16[64,64,10]{0,2,1:T(8,128)(2,1)S(1)}, u32[]{:S(2)}, u32[]{:S(2)}) %collective-permute-start.11) | collective-permute-done | bytes 81952 | tf_op jit(solution)/shard_map/ppermute | solution.py:25
  178.6 10.6 %collective-permute-done.12 = bf16[64,64,10]{0,2,1:T(8,128)(2,1)S(1)} collective-permute-done((bf16[64,64,10]{0,2,1:T(8,128)(2,1)S(1)}, bf16[64,64,10]{0,2,1:T(8,128)(2,1)S(1)}, u32[]{:S(2)}, u32[]{:S(2)}) %collective-permute-start.12) | collective-permute-done | bytes 81952 | tf_op jit(solution)/shard_map/ppermute | solution.py:25
  189.9 2.5 %gather_fusion.2 = bf16[8,64,64,10]{1,3,2,0:T(8,128)(2,1)S(1)} fusion(bf16[8,64,64,10]{1,3,2,0:T(8,128)(2,1)} %bitcast_dynamic-update-slice_fusion, s32[1024]{0:T(1024)S(1)} %pad_clamp_fusion.1), kind=kCustom, calls=%fused_computation.2 | custom fusion | bytes 1310752 | tf_op jit(solution)/shard_map/jit(_take)/gather | solution.py:177
  (91 shorter events, 24.1 us)
Async XLA Ops:
  6.5 28.4 %copy-start = (s32[32,32]{1,0:T(8,128)S(1)}, s32[32,32]{1,0:T(8,128)}, u32[]{:S(2)}) copy-start(s32[32,32]{1,0:T(8,128)} %param.16) | copy-start | bytes 12292
  6.5 16.7 %copy-start.3 = (s32[32]{0:T(128)S(1)}, s32[32]{0:T(128)}, u32[]{:S(2)}) copy-start(s32[32]{0:T(128)} %param.15) | copy-start | bytes 388
  6.5 17.9 %copy-start.1 = (bf16[64,128]{1,0:T(8,128)(2,1)S(1)}, bf16[64,128]{1,0:T(8,128)(2,1)}, u32[]{:S(2)}) copy-start(bf16[64,128]{1,0:T(8,128)(2,1)} %param.11) | copy-start | bytes 49156
  6.5 110.5 %all-gather.2.cloned.1.call-start = ((), (), s32[]{:S(2)}) async-start(), calls=%async_computation.1 | async-start | bytes 10649600 | tf_op jit(solution)/shard_map/all_gather | solution.py:68
  21.4 10.5 %copy-start.2 = (bf16[64,128]{1,0:T(8,128)(2,1)S(1)}, bf16[64,128]{1,0:T(8,128)(2,1)}, u32[]{:S(2)}) copy-start(bf16[64,128]{1,0:T(8,128)(2,1)} %param.12) | copy-start | bytes 49156
  25.1 10.0 %collective-permute-start.1 = (bf16[64,5,128]{2,1,0:T(8,128)(2,1)S(1)}, bf16[64,5,128]{2,1,0:T(8,128)(2,1)S(1)}, u32[]{:S(2)}, u32[]{:S(2)}) collective-permute-start(bf16[64,5,128]{2,1,0:T(8,128)(2,1)S(1)} %fusion.25), channel_id=1, source_target_pairs={{0,8},{8,0},{16,24},{24,16},{32,40},{40,32},{48,56},{56,48},{64,72... | collective-permute-start | bytes 245768 | tf_op jit(solution)/shard_map/ppermute | solution.py:18
  30.0 5.3 %collective-permute-start = (bf16[64,1,128]{2,0,1:T(8,128)(2,1)S(1)}, bf16[64,1,128]{2,0,1:T(8,128)(2,1)S(1)}, u32[]{:S(2)}, u32[]{:S(2)}) collective-permute-start(bf16[64,1,128]{2,0,1:T(8,128)(2,1)S(1)} %bitcast.189), channel_id=1, source_target_pairs={{0,8},{8,0},{16,24},{24,16},{32,40},{40,32},{48,56},{56,48},{64,72... | collective-permute-start | bytes 49160 | tf_op jit(solution)/shard_map/ppermute | solution.py:18
  31.9 3.8 %collective-permute-start.2 = (bf16[64,1,128]{2,0,1:T(8,128)(2,1)S(1)}, bf16[64,1,128]{2,0,1:T(8,128)(2,1)S(1)}, u32[]{:S(2)}, u32[]{:S(2)}) collective-permute-start(bf16[64,1,128]{2,0,1:T(8,128)(2,1)S(1)} %bitcast.190), channel_id=1, source_target_pairs={{0,8},{8,0},{16,24},{24,16},{32,40},{40,32},{48,56},{56,48},{64,72... | collective-permute-start | bytes 49160 | tf_op jit(solution)/shard_map/ppermute | solution.py:18
  46.5 6.4 %collective-permute-start.3 = (bf16[1,5,64]{2,1,0:T(8,128)(2,1)S(1)}, bf16[1,5,64]{2,1,0:T(8,128)(2,1)S(1)}, u32[]{:S(2)}, u32[]{:S(2)}) collective-permute-start(bf16[1,5,64]{2,1,0:T(8,128)(2,1)S(1)} %dynamic-slice_convert_fusion.2), channel_id=1, source_target_pairs={{0,8},{8,0},{16,24},{24,16},{32,40},{40,32},{48,56},{56,48},{64,72... | collective-permute-start | bytes 1928 | tf_op jit(solution)/shard_map/ppermute | solution.py:18
  48.5 4.5 %collective-permute-start.5 = (bf16[1,5,64]{2,1,0:T(8,128)(2,1)S(1)}, bf16[1,5,64]{2,1,0:T(8,128)(2,1)S(1)}, u32[]{:S(2)}, u32[]{:S(2)}) collective-permute-start(bf16[1,5,64]{2,1,0:T(8,128)(2,1)S(1)} %dynamic-slice_convert_fusion.1), channel_id=1, source_target_pairs={{0,8},{8,0},{16,24},{24,16},{32,40},{40,32},{48,56},{56,48},{64,72... | collective-permute-start | bytes 1928 | tf_op jit(solution)/shard_map/ppermute | solution.py:18
  51.0 3.3 %collective-permute-start.4 = (bf16[64,1,5,128]{0,3,2,1:T(8,128)(2,1)S(1)}, bf16[64,1,5,128]{0,3,2,1:T(8,128)(2,1)S(1)}, u32[]{:S(2)}, u32[]{:S(2)}) collective-permute-start(bf16[64,1,5,128]{0,3,2,1:T(8,128)(2,1)S(1)} %dynamic-slice_convert_fusion), channel_id=1, source_target_pairs={{0,8},{8,0},{16,24},{24,16},{32,40},{40,32},{48,56},{56,48},{64,72... | collective-permute-start | bytes 245768 | tf_op jit(solution)/shard_map/ppermute | solution.py:18
  124.5 19.5 %collective-permute-start.6 = (bf16[64,64,10]{0,2,1:T(8,128)(2,1)S(1)}, bf16[64,64,10]{0,2,1:T(8,128)(2,1)S(1)}, u32[]{:S(2)}, u32[]{:S(2)}) collective-permute-start(bf16[64,64,10]{0,2,1:T(8,128)(2,1)S(1)} %bitcast.176), channel_id=1, source_target_pairs={{0,1},{1,2},{2,3},{3,4},{4,5},{5,6},{6,7},{7,0},{8,9},{9,10},{10,1... | collective-permute-start | bytes 245768 | tf_op jit(solution)/shard_map/ppermute | solution.py:25
  128.3 20.5 %collective-permute-start.7 = (bf16[64,64,10]{0,2,1:T(8,128)(2,1)S(1)}, bf16[64,64,10]{0,2,1:T(8,128)(2,1)S(1)}, u32[]{:S(2)}, u32[]{:S(2)}) collective-permute-start(bf16[64,64,10]{0,2,1:T(8,128)(2,1)S(1)} %bitcast.178), channel_id=1, source_target_pairs={{0,2},{1,3},{2,4},{3,5},{4,6},{5,7},{6,0},{7,1},{8,10},{9,11},{10,... | collective-permute-start | bytes 245768 | tf_op jit(solution)/shard_map/ppermute | solution.py:25
  133.6 29.0 %collective-permute-start.8 = (bf16[64,64,10]{0,2,1:T(8,128)(2,1)S(1)}, bf16[64,64,10]{0,2,1:T(8,128)(2,1)S(1)}, u32[]{:S(2)}, u32[]{:S(2)}) collective-permute-start(bf16[64,64,10]{0,2,1:T(8,128)(2,1)S(1)} %bitcast.179), channel_id=1, source_target_pairs={{0,3},{1,4},{2,5},{3,6},{4,7},{5,0},{6,1},{7,2},{8,11},{9,12},{10,... | collective-permute-start | bytes 245768 | tf_op jit(solution)/shard_map/ppermute | solution.py:25
  135.8 27.5 %collective-permute-start.9 = (bf16[64,64,10]{0,2,1:T(8,128)(2,1)S(1)}, bf16[64,64,10]{0,2,1:T(8,128)(2,1)S(1)}, u32[]{:S(2)}, u32[]{:S(2)}) collective-permute-start(bf16[64,64,10]{0,2,1:T(8,128)(2,1)S(1)} %bitcast.180), channel_id=1, source_target_pairs={{0,4},{1,5},{2,6},{3,7},{4,0},{5,1},{6,2},{7,3},{8,12},{9,13},{10,... | collective-permute-start | bytes 245768 | tf_op jit(solution)/shard_map/ppermute | solution.py:25
  140.6 32.4 %collective-permute-start.10 = (bf16[64,64,10]{0,2,1:T(8,128)(2,1)S(1)}, bf16[64,64,10]{0,2,1:T(8,128)(2,1)S(1)}, u32[]{:S(2)}, u32[]{:S(2)}) collective-permute-start(bf16[64,64,10]{0,2,1:T(8,128)(2,1)S(1)} %bitcast.181), channel_id=1, source_target_pairs={{0,5},{1,6},{2,7},{3,0},{4,1},{5,2},{6,3},{7,4},{8,13},{9,14},{10,... | collective-permute-start | bytes 245768 | tf_op jit(solution)/shard_map/ppermute | solution.py:25
  144.0 33.9 %collective-permute-start.11 = (bf16[64,64,10]{0,2,1:T(8,128)(2,1)S(1)}, bf16[64,64,10]{0,2,1:T(8,128)(2,1)S(1)}, u32[]{:S(2)}, u32[]{:S(2)}) collective-permute-start(bf16[64,64,10]{0,2,1:T(8,128)(2,1)S(1)} %bitcast.182), channel_id=1, source_target_pairs={{0,6},{1,7},{2,0},{3,1},{4,2},{5,3},{6,4},{7,5},{8,14},{9,15},{10,... | collective-permute-start | bytes 245768 | tf_op jit(solution)/shard_map/ppermute | solution.py:25
  148.8 40.4 %collective-permute-start.12 = (bf16[64,64,10]{0,2,1:T(8,128)(2,1)S(1)}, bf16[64,64,10]{0,2,1:T(8,128)(2,1)S(1)}, u32[]{:S(2)}, u32[]{:S(2)}) collective-permute-start(bf16[64,64,10]{0,2,1:T(8,128)(2,1)S(1)} %bitcast.183), channel_id=1, source_target_pairs={{0,7},{1,0},{2,1},{3,2},{4,3},{5,4},{6,5},{7,6},{8,15},{9,8},{10,9... | collective-permute-start | bytes 245768 | tf_op jit(solution)/shard_map/ppermute | solution.py:25
Sparse Core Ops, SparseCore 0:
  22.3 94.6 all-gather.1

commit v6 on v4

--- a/solution.py
+++ b/solution.py
@@ -164,7 +164,10 @@
     )
     blocks = weights_mine.shape[0] // (-(-share // 8) * 8)
     projected = projected.reshape(own_rows, blocks, -1)[:, :, :share].astype(jnp.bfloat16)
-    gathered = lax.all_gather(projected, "tp", axis=2, tiled=True)
+    parts = lax.axis_size("tp")
+    rows, blocks, share = projected.shape
+    copies = jnp.broadcast_to(projected[:, :, None], (rows, blocks, parts, share))
+    gathered = lax.all_to_all(copies, "tp", 2, 2, tiled=True)
     return gathered.reshape(own_rows, -1)
 
 

time: 165 us -> 167 us (1.012)
  waiting for transfers between devices: 24.1 us -> 34.8 us
  local copies, waits for them, and re-layouts: 20.5 us -> 16.9 us
  other arithmetic: 5.28 us -> 3.26 us
  matrix products: 11.1 us -> 9.43 us
    all_gather x1 -> x0, blocking collectives: 28.5 us -> none  [shards(): gathered = lax.all_gather(projected, 'tp', axis=2, tiled=True)]
    all_to_all x0 -> x1, blocking collectives: none -> 27.3 us  [shards(): gathered = lax.all_to_all(copies, 'tp', 2, 2, tiled=True)]
    all_gather x1, waiting for transfers between devices: 23.2 us -> 33.9 us  [output_rows(): return (lax.all_gather(mine, 'req', axis=0, tiled=True), share)]
    all_to_all x0 -> x1, local copies, waits for them, and re-layouts: none -> 3.25 us  [shards(): gathered = lax.all_to_all(copies, 'tp', 2, 2, tiled=True)]
    gather x4 -> x2, local copies, waits for them, and re-layouts: 6.48 us -> 3.23 us  [visit(): block_values = v_cache[slots].reshape(block_rows, local_heads, HD)]
    gather x4 -> x2, local copies, waits for them, and re-layouts: 6.47 us -> 3.25 us  [visit(): block_keys = k_cache[slots].reshape(block_rows, local_heads, HD)]
    unnamed x12 -> x15, local copies, waits for them, and re-layouts: 0.06 us -> 2.08 us
  transfers between devices with their start and end apart: 7 -> 7, of which waited for: 2 -> 2; matrix products, arithmetic and copies ran while one was open for 14% -> 8% of each run, Pallas kernels for 0% -> 0%
where the time goes in v6:
time: 167 us; the launch traced here: 164 us
  blocking collectives  71.4 us (43%)
  waiting for transfers between devices  34.8 us (21%)
  local copies, waits for them, and re-layouts  16.9 us (10%)
  between operations  15 us (9%)
  starting transfers between devices  13 us (8%)
  matrix products  9.43 us (6%)
  other arithmetic  3.26 us (2%)
    all_gather x1, waiting for transfers between devices, output_rows(): return (lax.all_gather(mine, 'req', axis=0, tiled=True), share)  33.9 us
    all_gather x1, blocking collectives, shards(): full_rows = lax.all_gather(attention, 'tp', axis=1, tiled=True)  27.5 us
    all_to_all x1, blocking collectives, shards(): gathered = lax.all_to_all(copies, 'tp', 2, 2, tiled=True)  27.3 us
    all_to_all x1, blocking collectives, output_rows(): lax.all_to_all(w_out.reshape(parts, share, width), 'tp', 0, 0, tiled=True)  16.7 us
    ppermute x6, starting transfers between devices, from_partner(): lax.ppermute(value, axis, [(i, i ^ 1 << distance) for i in range(lax.axis...  12.9 us
    dot_general x1, matrix products, shards(): lax.dot_general(full_rows, weights_mine, (((1,), (1,)), ((), ())), prefer...  7.29 us
  transfers between devices with their start and end apart: 7, of which 2 were waited for; matrix products, arithmetic and copies ran while one was open for 8% of the time, Pallas kernels for 0%

profile of v6, /device:TPU:6, one launch (start us, length us, event | category | flops | bytes accessed | tf_op | source)
XLA Modules:
  0.0 164.0 jit_solution(3711295148073159485)
XLA Ops:
  6.6 1.0 reshape.311
  7.6 16.7 %all_to_all.10 = bf16[8,10,640]{2,1,0:T(8,128)(2,1)S(1)} all-to-all(bf16[8,10,640]{2,1,0:T(8,128)(2,1)S(1)} %reshape.311), channel_id=1, replica_groups=mesh['req'=64,'tp'=8] {'tp'}, dimensions={0} | all-to-all | bytes 204800 | tf_op jit(solution)/shard_map/all_to_all | solution.py:57
  24.3 0.7 pad.5
  27.0 1.9 %collective-permute-start.1 = (bf16[64,5,128]{2,1,0:T(8,128)(2,1)S(1)}, bf16[64,5,128]{2,1,0:T(8,128)(2,1)S(1)}, u32[]{:S(2)}, u32[]{:S(2)}) collective-permute-start(bf16[64,5,128]{2,1,0:T(8,128)(2,1)S(1)} %fusion.25), channel_id=1, source_target_pairs={{0,8},{8,0},{16,24},{24,16},{32,40},{40,32},{48,56},{56,48},{64,72... | collective-permute-start | bytes 245768 | tf_op jit(solution)/shard_map/ppermute | solution.py:18
  29.0 2.4 %collective-permute-start = (bf16[64,1,128]{2,0,1:T(8,128)(2,1)S(1)}, bf16[64,1,128]{2,0,1:T(8,128)(2,1)S(1)}, u32[]{:S(2)}, u32[]{:S(2)}) collective-permute-start(bf16[64,1,128]{2,0,1:T(8,128)(2,1)S(1)} %bitcast.166), channel_id=1, source_target_pairs={{0,8},{8,0},{16,24},{24,16},{32,40},{40,32},{48,56},{56,48},{64,72... | collective-permute-start | bytes 49160 | tf_op jit(solution)/shard_map/ppermute | solution.py:18
  31.4 1.9 %collective-permute-start.2 = (bf16[64,1,128]{2,0,1:T(8,128)(2,1)S(1)}, bf16[64,1,128]{2,0,1:T(8,128)(2,1)S(1)}, u32[]{:S(2)}, u32[]{:S(2)}) collective-permute-start(bf16[64,1,128]{2,0,1:T(8,128)(2,1)S(1)} %bitcast.167), channel_id=1, source_target_pairs={{0,8},{8,0},{16,24},{24,16},{32,40},{40,32},{48,56},{56,48},{64,72... | collective-permute-start | bytes 49160 | tf_op jit(solution)/shard_map/ppermute | solution.py:18
  34.9 10.4 %while.14 = (s32[]{:T(128)}, f32[1,5,128]{2,1,0:T(8,128)S(1)}, f32[1,5,128]{2,1,0:T(8,128)S(1)}, f32[128,1,5,128]{0,3,2,1:T(8,128)S(1)}, s32[]{:T(128)}, /*index...) while((s32[]{:T(128)}, f32[1,5,128]{2,1,0:T(8,128)S(1)}, ...), condition=%wide.region_5.6_spmd, body=%wide.region_2.5_spmd.sunk | while | flops 170889632 | bytes 5585255 | solution.py:129
  35.1 1.6 gather_fusion
  37.7 1.6 gather_fusion.1
  40.2 1.6 gather_fusion
  42.9 1.6 gather_fusion.1
  45.4 2.4 %collective-permute-start.3 = (bf16[1,5,64]{2,1,0:T(8,128)(2,1)S(1)}, bf16[1,5,64]{2,1,0:T(8,128)(2,1)S(1)}, u32[]{:S(2)}, u32[]{:S(2)}) collective-permute-start(bf16[1,5,64]{2,1,0:T(8,128)(2,1)S(1)} %dynamic-slice_convert_fusion.2), channel_id=1, source_target_pairs={{0,8},{8,0},{16,24},{24,16},{32,40},{40,32},{48,56},{56,48},{64,72... | collective-permute-start | bytes 1928 | tf_op jit(solution)/shard_map/ppermute | solution.py:18
  47.9 1.9 %collective-permute-start.5 = (bf16[1,5,64]{2,1,0:T(8,128)(2,1)S(1)}, bf16[1,5,64]{2,1,0:T(8,128)(2,1)S(1)}, u32[]{:S(2)}, u32[]{:S(2)}) collective-permute-start(bf16[1,5,64]{2,1,0:T(8,128)(2,1)S(1)} %dynamic-slice_convert_fusion.1), channel_id=1, source_target_pairs={{0,8},{8,0},{16,24},{24,16},{32,40},{40,32},{48,56},{56,48},{64,72... | collective-permute-start | bytes 1928 | tf_op jit(solution)/shard_map/ppermute | solution.py:18
  49.9 2.4 %collective-permute-start.4 = (bf16[64,1,5,128]{0,3,2,1:T(8,128)(2,1)S(1)}, bf16[64,1,5,128]{0,3,2,1:T(8,128)(2,1)S(1)}, u32[]{:S(2)}, u32[]{:S(2)}) collective-permute-start(bf16[64,1,5,128]{0,3,2,1:T(8,128)(2,1)S(1)} %dynamic-slice_convert_fusion), channel_id=1, source_target_pairs={{0,8},{8,0},{16,24},{24,16},{32,40},{40,32},{48,56},{56,48},{64,72... | collective-permute-start | bytes 245768 | tf_op jit(solution)/shard_map/ppermute | solution.py:18
  52.4 0.9 collective-permute-done.4
  53.5 27.5 %all_gather.6 = bf16[64,5120]{0,1:T(8,128)(2,1)S(1)} all-gather(bf16[64,640]{0,1:T(8,128)(2,1)S(1)} %bitcast.164), channel_id=1, replica_groups=mesh['req'=64,'tp'=8] {'tp'}, dimensions={1}, use_global_device_ids=true | all-gather | bytes 737280 | tf_op jit(solution)/shard_map/all_gather | solution.py:158
  81.0 33.9 %all-gather.2.cloned.1.call-done = bf16[1024,5120]{1,0:T(8,128)(2,1)} async-done(((bf16[16,5120]{1,0:T(8,128)(2,1)}), bf16[1024,5120]{1,0:T(8,128)(2,1)}) %all-gather.2.cloned.1.call-update) | async-done | bytes 10485776 | tf_op jit(solution)/shard_map/all_gather | solution.py:61
  114.9 7.3 %convolution_convert_fusion = bf16[64,1024]{1,0:T(8,128)(2,1)S(1)} fusion(bf16[64,5120]{0,1:T(8,128)(2,1)S(1)} %all_gather.6, bf16[1024,5120]{1,0:T(8,128)(2,1)} %all-gather.2.cloned.1.call-done), kind=kOutput, calls=%fused_computation.35 | convolution fusion | flops 671154176 | bytes 11272192 | tf_op jit(solution)/shard_map/dot_general | solution.py:159
  122.9 0.9 reshape.338
  123.8 27.3 %all_to_all.11 = bf16[8,2,20480]{2,1,0:T(2,128)(2,1)S(1)} all-to-all(bf16[8,2,20480]{2,1,0:T(2,128)(2,1)S(1)} %reshape.338), channel_id=1, replica_groups=mesh['req'=64,'tp'=8] {'tp'}, dimensions={0} | all-to-all | bytes 1310720 | tf_op jit(solution)/shard_map/all_to_all | solution.py:170
  151.0 0.8 reshape.339
  151.9 3.2 %copy.31 = bf16[64,64,8,10]{0,3,2,1:T(8,128)(2,1)S(1)} copy(bf16[64,64,8,10]{1,0,3,2:T(8,128)(2,1)S(1)} %bitcast.156) | data formatting | bytes 1310720 | tf_op jit(solution)/shard_map/all_to_all | solution.py:170
  155.1 0.8 reshape.314
  155.9 1.3 copy.32
  (71 shorter events, 7.3 us)
Async XLA Ops:
  6.5 27.4 %copy-start = (s32[32,32]{1,0:T(8,128)S(1)}, s32[32,32]{1,0:T(8,128)}, u32[]{:S(2)}) copy-start(s32[32,32]{1,0:T(8,128)} %param.16) | copy-start | bytes 12292
  6.5 18.5 %copy-start.1 = (bf16[64,640]{1,0:T(8,128)(2,1)S(1)}, bf16[64,640]{1,0:T(8,128)(2,1)}, u32[]{:S(2)}) copy-start(bf16[64,640]{1,0:T(8,128)(2,1)} %param.10) | copy-start | bytes 245764
  6.5 18.6 %copy-start.4 = (s32[32]{0:T(128)S(1)}, s32[32]{0:T(128)}, u32[]{:S(2)}) copy-start(s32[32]{0:T(128)} %param.15) | copy-start | bytes 388
  6.5 19.8 %copy-start.2 = (bf16[64,128]{1,0:T(8,128)(2,1)S(1)}, bf16[64,128]{1,0:T(8,128)(2,1)}, u32[]{:S(2)}) copy-start(bf16[64,128]{1,0:T(8,128)(2,1)} %param.11) | copy-start | bytes 49156
  6.5 108.3 %all-gather.2.cloned.1.call-start = ((), (), s32[]{:S(2)}) async-start(), calls=%async_computation.2 | async-start | bytes 10649600 | tf_op jit(solution)/shard_map/all_gather | solution.py:61
  25.2 6.2 %copy-start.3 = (bf16[64,128]{1,0:T(8,128)(2,1)S(1)}, bf16[64,128]{1,0:T(8,128)(2,1)}, u32[]{:S(2)}) copy-start(bf16[64,128]{1,0:T(8,128)(2,1)} %param.12) | copy-start | bytes 49156
  27.0 7.0 %collective-permute-start.1 = (bf16[64,5,128]{2,1,0:T(8,128)(2,1)S(1)}, bf16[64,5,128]{2,1,0:T(8,128)(2,1)S(1)}, u32[]{:S(2)}, u32[]{:S(2)}) collective-permute-start(bf16[64,5,128]{2,1,0:T(8,128)(2,1)S(1)} %fusion.25), channel_id=1, source_target_pairs={{0,8},{8,0},{16,24},{24,16},{32,40},{40,32},{48,56},{56,48},{64,72... | collective-permute-start | bytes 245768 | tf_op jit(solution)/shard_map/ppermute | solution.py:18
  29.0 5.2 %collective-permute-start = (bf16[64,1,128]{2,0,1:T(8,128)(2,1)S(1)}, bf16[64,1,128]{2,0,1:T(8,128)(2,1)S(1)}, u32[]{:S(2)}, u32[]{:S(2)}) collective-permute-start(bf16[64,1,128]{2,0,1:T(8,128)(2,1)S(1)} %bitcast.166), channel_id=1, source_target_pairs={{0,8},{8,0},{16,24},{24,16},{32,40},{40,32},{48,56},{56,48},{64,72... | collective-permute-start | bytes 49160 | tf_op jit(solution)/shard_map/ppermute | solution.py:18
  31.4 3.3 %collective-permute-start.2 = (bf16[64,1,128]{2,0,1:T(8,128)(2,1)S(1)}, bf16[64,1,128]{2,0,1:T(8,128)(2,1)S(1)}, u32[]{:S(2)}, u32[]{:S(2)}) collective-permute-start(bf16[64,1,128]{2,0,1:T(8,128)(2,1)S(1)} %bitcast.167), channel_id=1, source_target_pairs={{0,8},{8,0},{16,24},{24,16},{32,40},{40,32},{48,56},{56,48},{64,72... | collective-permute-start | bytes 49160 | tf_op jit(solution)/shard_map/ppermute | solution.py:18
  45.4 6.9 %collective-permute-start.3 = (bf16[1,5,64]{2,1,0:T(8,128)(2,1)S(1)}, bf16[1,5,64]{2,1,0:T(8,128)(2,1)S(1)}, u32[]{:S(2)}, u32[]{:S(2)}) collective-permute-start(bf16[1,5,64]{2,1,0:T(8,128)(2,1)S(1)} %dynamic-slice_convert_fusion.2), channel_id=1, source_target_pairs={{0,8},{8,0},{16,24},{24,16},{32,40},{40,32},{48,56},{56,48},{64,72... | collective-permute-start | bytes 1928 | tf_op jit(solution)/shard_map/ppermute | solution.py:18
  47.9 4.5 %collective-permute-start.5 = (bf16[1,5,64]{2,1,0:T(8,128)(2,1)S(1)}, bf16[1,5,64]{2,1,0:T(8,128)(2,1)S(1)}, u32[]{:S(2)}, u32[]{:S(2)}) collective-permute-start(bf16[1,5,64]{2,1,0:T(8,128)(2,1)S(1)} %dynamic-slice_convert_fusion.1), channel_id=1, source_target_pairs={{0,8},{8,0},{16,24},{24,16},{32,40},{40,32},{48,56},{56,48},{64,72... | collective-permute-start | bytes 1928 | tf_op jit(solution)/shard_map/ppermute | solution.py:18
  49.9 3.4 %collective-permute-start.4 = (bf16[64,1,5,128]{0,3,2,1:T(8,128)(2,1)S(1)}, bf16[64,1,5,128]{0,3,2,1:T(8,128)(2,1)S(1)}, u32[]{:S(2)}, u32[]{:S(2)}) collective-permute-start(bf16[64,1,5,128]{0,3,2,1:T(8,128)(2,1)S(1)} %dynamic-slice_convert_fusion), channel_id=1, source_target_pairs={{0,8},{8,0},{16,24},{24,16},{32,40},{40,32},{48,56},{56,48},{64,72... | collective-permute-start | bytes 245768 | tf_op jit(solution)/shard_map/ppermute | solution.py:18
Sparse Core Ops, SparseCore 0:
  25.1 89.6 all-gather.1

commit v7 on v4

--- a/solution.py
+++ b/solution.py
@@ -55,9 +55,7 @@
     rows, width = w_out.shape
     share = rows // parts
     pieces = lax.all_to_all(w_out.reshape(parts, share, width), "tp", 0, 0, tiled=True)
-    mine = jnp.transpose(pieces, (1, 0, 2)).reshape(share, parts * width)
-    padded = -(-share // 8) * 8
-    mine = jnp.pad(mine, ((0, padded - share), (0, 0)))
+    mine = jnp.transpose(pieces, (1, 0, 2))
     return lax.all_gather(mine, "req", axis=0, tiled=True), share
 
 
@@ -155,15 +153,14 @@
         .reshape(own_rows, local_heads * GROUP * HD)
         .astype(jnp.bfloat16)
     )
-    full_rows = lax.all_gather(attention, "tp", axis=1, tiled=True)
+    full_rows = lax.all_gather(attention[:, None], "tp", axis=1, tiled=True)
     projected = lax.dot_general(
         full_rows,
         weights_mine,
-        (((1,), (1,)), ((), ())),
+        (((1, 2), (1, 2)), ((), ())),
         preferred_element_type=jnp.float32,
     )
-    blocks = weights_mine.shape[0] // (-(-share // 8) * 8)
-    projected = projected.reshape(own_rows, blocks, -1)[:, :, :share].astype(jnp.bfloat16)
+    projected = projected.reshape(own_rows, -1, share).astype(jnp.bfloat16)
     gathered = lax.all_gather(projected, "tp", axis=2, tiled=True)
     return gathered.reshape(own_rows, -1)
 

time: 165 us -> 158 us (0.958)
  waiting for transfers between devices: 24.1 us -> 20.2 us
  matrix products: 11.1 us -> 8.88 us
  blocking collectives: 73 us -> 71 us
    all_gather x1, waiting for transfers between devices: 23.2 us -> 19.2 us  [output_rows(): return (lax.all_gather(mine, 'req', axis=0, tiled=True), share)]
    dot_general x1, matrix products: 7.29 us -> 4.99 us  [shards(): lax.dot_general(full_rows, weights_mine, (((1, 2), (1, 2)), ((), ())), pr...]
    all_gather x1, blocking collectives: 27.8 us -> 25.8 us  [shards(): full_rows = lax.all_gather(attention[:, None], 'tp', axis=1, tiled=True)]
  transfers between devices with their start and end apart: 7 -> 7, of which waited for: 2 -> 2; matrix products, arithmetic and copies ran while one was open for 14% -> 16% of each run, Pallas kernels for 0% -> 0%
where the time goes in v7:
time: 158 us; the launch traced here: 156 us
  blocking collectives  71 us (45%)
  local copies, waits for them, and re-layouts  21.5 us (14%)
  waiting for transfers between devices  20.2 us (13%)
  between operations  15.2 us (10%)
  starting transfers between devices  13 us (8%)
  matrix products  8.88 us (6%)
  other arithmetic  5.77 us (4%)
    all_gather x1, blocking collectives, shards(): gathered = lax.all_gather(projected, 'tp', axis=2, tiled=True)  28.5 us
    all_gather x1, blocking collectives, shards(): full_rows = lax.all_gather(attention[:, None], 'tp', axis=1, tiled=True)  25.8 us
    all_gather x1, waiting for transfers between devices, output_rows(): return (lax.all_gather(mine, 'req', axis=0, tiled=True), share)  19.2 us
    all_to_all x1, blocking collectives, output_rows(): lax.all_to_all(w_out.reshape(parts, share, width), 'tp', 0, 0, tiled=True)  16.7 us
    ppermute x6, starting transfers between devices, from_partner(): lax.ppermute(value, axis, [(i, i ^ 1 << distance) for i in range(lax.axis...  12.9 us
    gather x4, local copies, waits for them, and re-layouts, visit(): block_values = v_cache[slots].reshape(block_rows, local_heads, HD)  6.47 us
    gather x4, local copies, waits for them, and re-layouts, visit(): block_keys = k_cache[slots].reshape(block_rows, local_heads, HD)  6.46 us
    dot_general x1, matrix products, shards(): lax.dot_general(full_rows, weights_mine, (((1, 2), (1, 2)), ((), ())), pr...  4.99 us
  transfers between devices with their start and end apart: 7, of which 2 were waited for; matrix products, arithmetic and copies ran while one was open for 16% of the time, Pallas kernels for 0%

profile of v7, /device:TPU:6, one launch (start us, length us, event | category | flops | bytes accessed | tf_op | source)
XLA Modules:
  0.0 155.8 jit_solution(15833743976615498956)
XLA Ops:
  6.5 1.0 reshape.315
  7.5 16.7 %all_to_all.5 = bf16[8,10,640]{2,1,0:T(8,128)(2,1)S(1)} all-to-all(bf16[8,10,640]{2,1,0:T(8,128)(2,1)S(1)} %reshape.315), channel_id=1, replica_groups=mesh['req'=64,'tp'=8] {'tp'}, dimensions={0} | all-to-all | bytes 204800 | tf_op jit(solution)/shard_map/all_to_all | solution.py:57
  24.9 1.0 reshape.317
  28.0 1.9 %collective-permute-start.1 = (bf16[64,5,128]{2,1,0:T(8,128)(2,1)S(1)}, bf16[64,5,128]{2,1,0:T(8,128)(2,1)S(1)}, u32[]{:S(2)}, u32[]{:S(2)}) collective-permute-start(bf16[64,5,128]{2,1,0:T(8,128)(2,1)S(1)} %fusion.33), channel_id=1, source_target_pairs={{0,8},{8,0},{16,24},{24,16},{32,40},{40,32},{48,56},{56,48},{64,72... | collective-permute-start | bytes 245768 | tf_op jit(solution)/shard_map/ppermute | solution.py:18
  29.9 2.4 %collective-permute-start = (bf16[64,1,128]{2,0,1:T(8,128)(2,1)S(1)}, bf16[64,1,128]{2,0,1:T(8,128)(2,1)S(1)}, u32[]{:S(2)}, u32[]{:S(2)}) collective-permute-start(bf16[64,1,128]{2,0,1:T(8,128)(2,1)S(1)} %bitcast.157), channel_id=1, source_target_pairs={{0,8},{8,0},{16,24},{24,16},{32,40},{40,32},{48,56},{56,48},{64,72... | collective-permute-start | bytes 49160 | tf_op jit(solution)/shard_map/ppermute | solution.py:18
  32.3 1.9 %collective-permute-start.2 = (bf16[64,1,128]{2,0,1:T(8,128)(2,1)S(1)}, bf16[64,1,128]{2,0,1:T(8,128)(2,1)S(1)}, u32[]{:S(2)}, u32[]{:S(2)}) collective-permute-start(bf16[64,1,128]{2,0,1:T(8,128)(2,1)S(1)} %bitcast.158), channel_id=1, source_target_pairs={{0,8},{8,0},{16,24},{24,16},{32,40},{40,32},{48,56},{56,48},{64,72... | collective-permute-start | bytes 49160 | tf_op jit(solution)/shard_map/ppermute | solution.py:18
  36.0 21.3 %while.14 = (s32[]{:T(128)}, f32[1,5,128]{2,1,0:T(8,128)S(1)}, f32[1,5,128]{2,1,0:T(8,128)S(1)}, f32[128,1,5,128]{0,3,2,1:T(8,128)S(1)}, s32[]{:T(128)}, /*index...) while((s32[]{:T(128)}, f32[1,5,128]{2,1,0:T(8,128)S(1)}, ...), condition=%wide.region_5.6_spmd, body=%wide.region_2.5_spmd.sunk | while | flops 170889632 | bytes 5585255 | solution.py:127
  36.1 1.6 %gather_fusion = bf16[4,128,128]{2,1,0:T(8,128)(2,1)S(1)} fusion(bf16[16,128,128]{2,1,0:T(8,128)(2,1)} %get-tuple-element.297, s32[1024]{0:T(1024)S(1)} %pad_clamp_fusion.2), kind=kCustom, calls=%fused_computation.clone.1 | custom fusion | bytes 262160 | tf_op jit(solution)/shard_map/while/body/gather | solution.py:118
  38.9 1.6 %gather_fusion.1 = bf16[4,128,128]{2,1,0:T(8,128)(2,1)S(1)} fusion(bf16[16,128,128]{2,1,0:T(8,128)(2,1)} %get-tuple-element.299, s32[1024]{0:T(1024)S(1)} %pad_clamp_fusion.2), kind=kCustom, calls=%fused_computation.1.clone.1 | custom fusion | bytes 262160 | tf_op jit(solution)/shard_map/while/body/gather | solution.py:119
  41.4 1.6 %gather_fusion = bf16[4,128,128]{2,1,0:T(8,128)(2,1)S(1)} fusion(bf16[16,128,128]{2,1,0:T(8,128)(2,1)} %get-tuple-element.297, s32[1024]{0:T(1024)S(1)} %pad_clamp_fusion.2), kind=kCustom, calls=%fused_computation.clone.1 | custom fusion | bytes 262160 | tf_op jit(solution)/shard_map/while/body/gather | solution.py:118
  44.2 1.6 %gather_fusion.1 = bf16[4,128,128]{2,1,0:T(8,128)(2,1)S(1)} fusion(bf16[16,128,128]{2,1,0:T(8,128)(2,1)} %get-tuple-element.299, s32[1024]{0:T(1024)S(1)} %pad_clamp_fusion.2), kind=kCustom, calls=%fused_computation.1.clone.1 | custom fusion | bytes 262160 | tf_op jit(solution)/shard_map/while/body/gather | solution.py:119
  46.7 1.6 %gather_fusion = bf16[4,128,128]{2,1,0:T(8,128)(2,1)S(1)} fusion(bf16[16,128,128]{2,1,0:T(8,128)(2,1)} %get-tuple-element.297, s32[1024]{0:T(1024)S(1)} %pad_clamp_fusion.2), kind=kCustom, calls=%fused_computation.clone.1 | custom fusion | bytes 262160 | tf_op jit(solution)/shard_map/while/body/gather | solution.py:118
  49.5 1.6 %gather_fusion.1 = bf16[4,128,128]{2,1,0:T(8,128)(2,1)S(1)} fusion(bf16[16,128,128]{2,1,0:T(8,128)(2,1)} %get-tuple-element.299, s32[1024]{0:T(1024)S(1)} %pad_clamp_fusion.2), kind=kCustom, calls=%fused_computation.1.clone.1 | custom fusion | bytes 262160 | tf_op jit(solution)/shard_map/while/body/gather | solution.py:119
  52.1 1.6 %gather_fusion = bf16[4,128,128]{2,1,0:T(8,128)(2,1)S(1)} fusion(bf16[16,128,128]{2,1,0:T(8,128)(2,1)} %get-tuple-element.297, s32[1024]{0:T(1024)S(1)} %pad_clamp_fusion.2), kind=kCustom, calls=%fused_computation.clone.1 | custom fusion | bytes 262160 | tf_op jit(solution)/shard_map/while/body/gather | solution.py:118
  54.8 1.6 %gather_fusion.1 = bf16[4,128,128]{2,1,0:T(8,128)(2,1)S(1)} fusion(bf16[16,128,128]{2,1,0:T(8,128)(2,1)} %get-tuple-element.299, s32[1024]{0:T(1024)S(1)} %pad_clamp_fusion.2), kind=kCustom, calls=%fused_computation.1.clone.1 | custom fusion | bytes 262160 | tf_op jit(solution)/shard_map/while/body/gather | solution.py:119
  57.3 2.4 %collective-permute-start.3 = (bf16[1,5,64]{2,1,0:T(8,128)(2,1)S(1)}, bf16[1,5,64]{2,1,0:T(8,128)(2,1)S(1)}, u32[]{:S(2)}, u32[]{:S(2)}) collective-permute-start(bf16[1,5,64]{2,1,0:T(8,128)(2,1)S(1)} %dynamic-slice_convert_fusion.2), channel_id=1, source_target_pairs={{0,8},{8,0},{16,24},{24,16},{32,40},{40,32},{48,56},{56,48},{64,72... | collective-permute-start | bytes 1928 | tf_op jit(solution)/shard_map/ppermute | solution.py:18
  59.8 1.9 %collective-permute-start.5 = (bf16[1,5,64]{2,1,0:T(8,128)(2,1)S(1)}, bf16[1,5,64]{2,1,0:T(8,128)(2,1)S(1)}, u32[]{:S(2)}, u32[]{:S(2)}) collective-permute-start(bf16[1,5,64]{2,1,0:T(8,128)(2,1)S(1)} %dynamic-slice_convert_fusion.1), channel_id=1, source_target_pairs={{0,8},{8,0},{16,24},{24,16},{32,40},{40,32},{48,56},{56,48},{64,72... | collective-permute-start | bytes 1928 | tf_op jit(solution)/shard_map/ppermute | solution.py:18
  61.9 2.4 %collective-permute-start.4 = (bf16[64,1,5,128]{0,3,2,1:T(8,128)(2,1)S(1)}, bf16[64,1,5,128]{0,3,2,1:T(8,128)(2,1)S(1)}, u32[]{:S(2)}, u32[]{:S(2)}) collective-permute-start(bf16[64,1,5,128]{0,3,2,1:T(8,128)(2,1)S(1)} %dynamic-slice_convert_fusion), channel_id=1, source_target_pairs={{0,8},{8,0},{16,24},{24,16},{32,40},{40,32},{48,56},{56,48},{64,72... | collective-permute-start | bytes 245768 | tf_op jit(solution)/shard_map/ppermute | solution.py:18
  65.6 25.8 %all_gather.9 = bf16[64,8,640]{2,0,1:T(8,128)(2,1)S(1)} all-gather(bf16[64,1,640]{2,0,1:T(8,128)(2,1)S(1)} %copy.52), channel_id=1, replica_groups=mesh['req'=64,'tp'=8] {'tp'}, dimensions={1}, use_global_device_ids=true | all-gather | bytes 737280 | tf_op jit(solution)/shard_map/all_gather | solution.py:156
  91.3 19.2 %all-gather.2.cloned.1.call-done = bf16[640,8,640]{2,1,0:T(8,128)(2,1)} async-done(((bf16[10,8,640]{2,1,0:T(8,128)(2,1)}), bf16[640,8,640]{2,1,0:T(8,128)(2,1)}) %all-gather.2.cloned.1.call-update) | async-done | bytes 6553616 | tf_op jit(solution)/shard_map/all_gather | solution.py:59
  110.6 5.0 %fusion.27 = bf16[64,640]{1,0:T(8,128)(2,1)S(1)} fusion(bf16[64,8,640]{2,0,1:T(8,128)(2,1)S(1)} %all_gather.9, bf16[640,8,640]{2,1,0:T(8,128)(2,1)} %all-gather.2.cloned.1.call-done), kind=kOutput, calls=%fused_computation.39 | convolution fusion | flops 419471360 | bytes 7290880 | tf_op jit(solution)/shard_map/dot_general | solution.py:157
  116.0 28.5 %all_gather.11 = bf16[64,64,80]{1,0,2:T(8,128)(2,1)S(1)} all-gather(bf16[64,64,10]{1,0,2:T(8,128)(2,1)S(1)} %copy.44), channel_id=1, replica_groups=mesh['req'=64,'tp'=8] {'tp'}, dimensions={2}, use_global_device_ids=true | all-gather | bytes 737280 | tf_op jit(solution)/shard_map/all_gather | solution.py:164
  144.6 1.5 copy.45
  146.1 2.9 %reshape.316 = bf16[64,5120]{1,0:T(8,128)(2,1)} reshape(bf16[64,64,80]{2,1,0:T(8,128)(2,1)S(1)} %copy.45) | data formatting | bytes 1310720 | tf_op jit(solution)/shard_map/reshape | solution.py:165
  (90 shorter events, 12.9 us)
Async XLA Ops:
  6.5 28.5 %copy-start = (s32[32,32]{1,0:T(8,128)S(1)}, s32[32,32]{1,0:T(8,128)}, u32[]{:S(2)}) copy-start(s32[32,32]{1,0:T(8,128)} %param.16) | copy-start | bytes 12292
  6.5 19.4 %copy-start.3 = (s32[32]{0:T(128)S(1)}, s32[32]{0:T(128)}, u32[]{:S(2)}) copy-start(s32[32]{0:T(128)} %param.15) | copy-start | bytes 388
  6.5 20.7 %copy-start.1 = (bf16[64,128]{1,0:T(8,128)(2,1)S(1)}, bf16[64,128]{1,0:T(8,128)(2,1)}, u32[]{:S(2)}) copy-start(bf16[64,128]{1,0:T(8,128)(2,1)} %param.11) | copy-start | bytes 49156
  6.5 104.0 %all-gather.2.cloned.1.call-start = ((), (), s32[]{:S(2)}) async-start(), calls=%async_computation.1 | async-start | bytes 6656000 | tf_op jit(solution)/shard_map/all_gather | solution.py:59
  25.9 6.4 %copy-start.2 = (bf16[64,128]{1,0:T(8,128)(2,1)S(1)}, bf16[64,128]{1,0:T(8,128)(2,1)}, u32[]{:S(2)}) copy-start(bf16[64,128]{1,0:T(8,128)(2,1)} %param.12) | copy-start | bytes 49156
  28.0 7.1 %collective-permute-start.1 = (bf16[64,5,128]{2,1,0:T(8,128)(2,1)S(1)}, bf16[64,5,128]{2,1,0:T(8,128)(2,1)S(1)}, u32[]{:S(2)}, u32[]{:S(2)}) collective-permute-start(bf16[64,5,128]{2,1,0:T(8,128)(2,1)S(1)} %fusion.33), channel_id=1, source_target_pairs={{0,8},{8,0},{16,24},{24,16},{32,40},{40,32},{48,56},{56,48},{64,72... | collective-permute-start | bytes 245768 | tf_op jit(solution)/shard_map/ppermute | solution.py:18
  29.9 5.3 %collective-permute-start = (bf16[64,1,128]{2,0,1:T(8,128)(2,1)S(1)}, bf16[64,1,128]{2,0,1:T(8,128)(2,1)S(1)}, u32[]{:S(2)}, u32[]{:S(2)}) collective-permute-start(bf16[64,1,128]{2,0,1:T(8,128)(2,1)S(1)} %bitcast.157), channel_id=1, source_target_pairs={{0,8},{8,0},{16,24},{24,16},{32,40},{40,32},{48,56},{56,48},{64,72... | collective-permute-start | bytes 49160 | tf_op jit(solution)/shard_map/ppermute | solution.py:18
  32.3 3.4 %collective-permute-start.2 = (bf16[64,1,128]{2,0,1:T(8,128)(2,1)S(1)}, bf16[64,1,128]{2,0,1:T(8,128)(2,1)S(1)}, u32[]{:S(2)}, u32[]{:S(2)}) collective-permute-start(bf16[64,1,128]{2,0,1:T(8,128)(2,1)S(1)} %bitcast.158), channel_id=1, source_target_pairs={{0,8},{8,0},{16,24},{24,16},{32,40},{40,32},{48,56},{56,48},{64,72... | collective-permute-start | bytes 49160 | tf_op jit(solution)/shard_map/ppermute | solution.py:18
  57.3 6.9 %collective-permute-start.3 = (bf16[1,5,64]{2,1,0:T(8,128)(2,1)S(1)}, bf16[1,5,64]{2,1,0:T(8,128)(2,1)S(1)}, u32[]{:S(2)}, u32[]{:S(2)}) collective-permute-start(bf16[1,5,64]{2,1,0:T(8,128)(2,1)S(1)} %dynamic-slice_convert_fusion.2), channel_id=1, source_target_pairs={{0,8},{8,0},{16,24},{24,16},{32,40},{40,32},{48,56},{56,48},{64,72... | collective-permute-start | bytes 1928 | tf_op jit(solution)/shard_map/ppermute | solution.py:18
  59.8 4.5 %collective-permute-start.5 = (bf16[1,5,64]{2,1,0:T(8,128)(2,1)S(1)}, bf16[1,5,64]{2,1,0:T(8,128)(2,1)S(1)}, u32[]{:S(2)}, u32[]{:S(2)}) collective-permute-start(bf16[1,5,64]{2,1,0:T(8,128)(2,1)S(1)} %dynamic-slice_convert_fusion.1), channel_id=1, source_target_pairs={{0,8},{8,0},{16,24},{24,16},{32,40},{40,32},{48,56},{56,48},{64,72... | collective-permute-start | bytes 1928 | tf_op jit(solution)/shard_map/ppermute | solution.py:18
  61.9 3.4 %collective-permute-start.4 = (bf16[64,1,5,128]{0,3,2,1:T(8,128)(2,1)S(1)}, bf16[64,1,5,128]{0,3,2,1:T(8,128)(2,1)S(1)}, u32[]{:S(2)}, u32[]{:S(2)}) collective-permute-start(bf16[64,1,5,128]{0,3,2,1:T(8,128)(2,1)S(1)} %dynamic-slice_convert_fusion), channel_id=1, source_target_pairs={{0,8},{8,0},{16,24},{24,16},{32,40},{40,32},{48,56},{56,48},{64,72... | collective-permute-start | bytes 245768 | tf_op jit(solution)/shard_map/ppermute | solution.py:18
Sparse Core Ops, SparseCore 0:
  25.0 85.5 all-gather.1

commit v8 on v7

--- a/solution.py
+++ b/solution.py
@@ -3,11 +3,13 @@
 import jax
 import jax.numpy as jnp
 from jax import lax
+from jax.sharding import Mesh
 from jax.sharding import PartitionSpec as P
 
 HD = 128
 GROUP = 5
 BLOCK_PAGES = 4
+ROWS = ("z", "x", "core")
 
 
 ROPE_BASE = 1000000.0
@@ -56,7 +58,8 @@
     share = rows // parts
     pieces = lax.all_to_all(w_out.reshape(parts, share, width), "tp", 0, 0, tiled=True)
     mine = jnp.transpose(pieces, (1, 0, 2))
-    return lax.all_gather(mine, "req", axis=0, tiled=True), share
+    near = lax.all_gather(mine, "z", axis=0, tiled=True)
+    return lax.all_gather(near, ("x", "core"), axis=0, tiled=True), share
 
 
 def shards(q_new, k_new, v_new, k_cache, v_cache, lengths, page_table, w_out):
@@ -68,7 +71,9 @@
     block_rows = BLOCK_PAGES * page_rows
     scale = 1.0 / math.sqrt(HD)
     weights_mine, share = output_rows(w_out)
-    device_row = lax.axis_index("req")
+    device_row = (lax.axis_index("z") * lax.axis_size("x") + lax.axis_index("x")) * lax.axis_size(
+        "core"
+    ) + lax.axis_index("core")
     parity = device_row % 2
     request = device_row // 2
     length = lengths[request]
@@ -81,7 +86,7 @@
     ).astype(jnp.bfloat16)
     own_values = v_new.reshape(own_rows, local_heads, HD)
     peer_queries, peer_keys, peer_values = from_partner(
-        (own_queries, own_keys, own_values), "req", 0
+        (own_queries, own_keys, own_values), "core", 0
     )
 
     def ordered(mine, theirs):
@@ -133,9 +138,9 @@
         lax.dynamic_slice_in_dim(running_sum, peer_start, own_rows, 2),
     )
     other_output, other_max, other_sum = (
-        from_partner(outgoing[0].astype(jnp.bfloat16), "req", 0).astype(jnp.float32),
-        from_partner(outgoing[1].astype(jnp.bfloat16), "req", 0).astype(jnp.float32),
-        from_partner(outgoing[2].astype(jnp.bfloat16), "req", 0).astype(jnp.float32),
+        from_partner(outgoing[0].astype(jnp.bfloat16), "core", 0).astype(jnp.float32),
+        from_partner(outgoing[1].astype(jnp.bfloat16), "core", 0).astype(jnp.float32),
+        from_partner(outgoing[2].astype(jnp.bfloat16), "core", 0).astype(jnp.float32),
     )
     mine_output = lax.dynamic_slice_in_dim(output, own_start, own_rows, 0)
     mine_max = lax.dynamic_slice_in_dim(running_max, own_start, own_rows, 2)
@@ -160,21 +165,28 @@
         (((1, 2), (1, 2)), ((), ())),
         preferred_element_type=jnp.float32,
     )
-    projected = projected.reshape(own_rows, -1, share).astype(jnp.bfloat16)
+    depth = lax.axis_size("z")
+    projected = projected.reshape(own_rows, -1, depth, share)
+    projected = jnp.transpose(projected, (0, 2, 1, 3)).reshape(own_rows, -1, share)
+    projected = projected.astype(jnp.bfloat16)
     gathered = lax.all_gather(projected, "tp", axis=2, tiled=True)
     return gathered.reshape(own_rows, -1)
 
 
 def solution(mesh):
     in_specs = (
-        P("req", "tp"),
-        P("req", "tp"),
-        P("req", "tp"),
-        P("req", None, "tp"),
-        P("req", None, "tp"),
+        P(ROWS, "tp"),
+        P(ROWS, "tp"),
+        P(ROWS, "tp"),
+        P(ROWS, None, "tp"),
+        P(ROWS, None, "tp"),
         P(),
         P(),
-        P("req", "tp"),
+        P(ROWS, "tp"),
     )
-    out_specs = P("req", None)
-    return jax.shard_map(shards, mesh=mesh, in_specs=in_specs, out_specs=out_specs, check_vma=False)
+    out_specs = P(ROWS, None)
+    rows, parts = mesh.devices.shape
+    cores = 2
+    depth = 4 if rows % (4 * cores) == 0 else 1
+    split = Mesh(mesh.devices.reshape(depth, rows // (depth * cores), cores, parts), ROWS + ("tp",))
+    return jax.shard_map(shards, mesh=split, in_specs=in_specs, out_specs=out_specs, check_vma=False)

time: 158 us -> 156 us (0.987)
  the two profiles are of different devices: /device:TPU:6 before, /device:TPU:68 now
where the time goes in v8:
time: 156 us; the launch traced here: 155 us
  blocking collectives  90.5 us (58%)
  local copies, waits for them, and re-layouts  20.8 us (13%)
  between operations  15.1 us (10%)
  starting transfers between devices  13 us (8%)
  matrix products  8.76 us (6%)
  other arithmetic  5.57 us (4%)
    all_gather x1, blocking collectives, shards(): gathered = lax.all_gather(projected, 'tp', axis=2, tiled=True)  27.4 us
    all_gather x1, blocking collectives, shards(): full_rows = lax.all_gather(attention[:, None], 'tp', axis=1, tiled=True)  25.7 us
    all_gather x1, blocking collectives, output_rows(): near = lax.all_gather(mine, 'z', axis=0, tiled=True)  20.7 us
    all_to_all x1, blocking collectives, output_rows(): lax.all_to_all(w_out.reshape(parts, share, width), 'tp', 0, 0, tiled=True)  16.7 us
    ppermute x6, starting transfers between devices, from_partner(): lax.ppermute(value, axis, [(i, i ^ 1 << distance) for i in range(lax.axis...  13 us
    gather x4, local copies, waits for them, and re-layouts, visit(): block_values = v_cache[slots].reshape(block_rows, local_heads, HD)  6.48 us
    gather x4, local copies, waits for them, and re-layouts, visit(): block_keys = k_cache[slots].reshape(block_rows, local_heads, HD)  6.47 us
    dot_general x1, matrix products, shards(): lax.dot_general(full_rows, weights_mine, (((1, 2), (1, 2)), ((), ())), pr...  4.94 us
  transfers between devices with their start and end apart: 7, of which 1 were waited for; matrix products, arithmetic and copies ran while one was open for 15% of the time, Pallas kernels for 0%

profile of v8, /device:TPU:68, one launch (start us, length us, event | category | flops | bytes accessed | tf_op | source)
XLA Modules:
  0.0 155.1 jit_solution(3614957007625193306)
XLA Ops:
  6.5 1.0 reshape.317
  7.5 16.7 %all_to_all.5 = bf16[8,10,640]{2,1,0:T(8,128)(2,1)S(1)} all-to-all(bf16[8,10,640]{2,1,0:T(8,128)(2,1)S(1)} %reshape.317), channel_id=1, replica_groups=mesh['z'=4,'x'=8,'core'=2,'tp'=8] {'tp'}, dimensions={0} | all-to-all | bytes 204800 | tf_op jit(solution)/shard_map/all_to_all | solution.py:59
  24.2 20.7 %all_gather.13 = bf16[40,8,640]{2,1,0:T(8,128)(2,1)S(1)} all-gather(bf16[10,8,640]{2,1,0:T(8,128)(2,1)S(1)} %copy.40), channel_id=1, replica_groups=mesh['z'=4,'x'=8,'core'=2,'tp'=8] {'z'}, dimensions={0}, use_global_device_ids=true | all-gather | bytes 512000 | tf_op jit(solution)/shard_map/all_gather | solution.py:61
  47.9 1.9 %collective-permute-start.1 = (bf16[64,5,128]{2,1,0:T(8,128)(2,1)S(1)}, bf16[64,5,128]{2,1,0:T(8,128)(2,1)S(1)}, u32[]{:S(2)}, u32[]{:S(2)}) collective-permute-start(bf16[64,5,128]{2,1,0:T(8,128)(2,1)S(1)} %fusion.26), channel_id=1, source_target_pairs={{0,8},{8,0},{1,9},{9,1},{2,10},{10,2},{3,11},{11,3},{4,12},{12,4},... | collective-permute-start | bytes 245768 | tf_op jit(solution)/shard_map/ppermute | solution.py:20
  49.9 2.4 %collective-permute-start = (bf16[64,1,128]{2,0,1:T(8,128)(2,1)S(1)}, bf16[64,1,128]{2,0,1:T(8,128)(2,1)S(1)}, u32[]{:S(2)}, u32[]{:S(2)}) collective-permute-start(bf16[64,1,128]{2,0,1:T(8,128)(2,1)S(1)} %bitcast.162), channel_id=1, source_target_pairs={{0,8},{8,0},{1,9},{9,1},{2,10},{10,2},{3,11},{11,3},{4,12},{12,4},... | collective-permute-start | bytes 49160 | tf_op jit(solution)/shard_map/ppermute | solution.py:20
  52.3 1.9 %collective-permute-start.2 = (bf16[64,1,128]{2,0,1:T(8,128)(2,1)S(1)}, bf16[64,1,128]{2,0,1:T(8,128)(2,1)S(1)}, u32[]{:S(2)}, u32[]{:S(2)}) collective-permute-start(bf16[64,1,128]{2,0,1:T(8,128)(2,1)S(1)} %bitcast.163), channel_id=1, source_target_pairs={{0,8},{8,0},{1,9},{9,1},{2,10},{10,2},{3,11},{11,3},{4,12},{12,4},... | collective-permute-start | bytes 49160 | tf_op jit(solution)/shard_map/ppermute | solution.py:20
  55.9 21.1 %while.14 = (s32[]{:T(128)}, f32[1,5,128]{2,1,0:T(8,128)S(1)}, f32[1,5,128]{2,1,0:T(8,128)S(1)}, f32[128,1,5,128]{0,3,2,1:T(8,128)S(1)}, s32[]{:T(128)}, /*index...) while((s32[]{:T(128)}, f32[1,5,128]{2,1,0:T(8,128)S(1)}, ...), condition=%wide.region_5.6_spmd, body=%wide.region_2.5_spmd.sunk | while | flops 170889632 | bytes 5585255 | solution.py:132
  56.0 1.6 %gather_fusion = bf16[4,128,128]{2,1,0:T(8,128)(2,1)S(1)} fusion(bf16[16,128,128]{2,1,0:T(8,128)(2,1)} %get-tuple-element.297, s32[1024]{0:T(1024)S(1)} %pad_clamp_fusion.2), kind=kCustom, calls=%fused_computation.clone.1 | custom fusion | bytes 262160 | tf_op jit(solution)/shard_map/while/body/gather | solution.py:123
  58.8 1.6 %gather_fusion.1 = bf16[4,128,128]{2,1,0:T(8,128)(2,1)S(1)} fusion(bf16[16,128,128]{2,1,0:T(8,128)(2,1)} %get-tuple-element.299, s32[1024]{0:T(1024)S(1)} %pad_clamp_fusion.2), kind=kCustom, calls=%fused_computation.1.clone.1 | custom fusion | bytes 262160 | tf_op jit(solution)/shard_map/while/body/gather | solution.py:124
  61.3 1.6 %gather_fusion = bf16[4,128,128]{2,1,0:T(8,128)(2,1)S(1)} fusion(bf16[16,128,128]{2,1,0:T(8,128)(2,1)} %get-tuple-element.297, s32[1024]{0:T(1024)S(1)} %pad_clamp_fusion.2), kind=kCustom, calls=%fused_computation.clone.1 | custom fusion | bytes 262160 | tf_op jit(solution)/shard_map/while/body/gather | solution.py:123
  64.0 1.6 %gather_fusion.1 = bf16[4,128,128]{2,1,0:T(8,128)(2,1)S(1)} fusion(bf16[16,128,128]{2,1,0:T(8,128)(2,1)} %get-tuple-element.299, s32[1024]{0:T(1024)S(1)} %pad_clamp_fusion.2), kind=kCustom, calls=%fused_computation.1.clone.1 | custom fusion | bytes 262160 | tf_op jit(solution)/shard_map/while/body/gather | solution.py:124
  66.5 1.6 %gather_fusion = bf16[4,128,128]{2,1,0:T(8,128)(2,1)S(1)} fusion(bf16[16,128,128]{2,1,0:T(8,128)(2,1)} %get-tuple-element.297, s32[1024]{0:T(1024)S(1)} %pad_clamp_fusion.2), kind=kCustom, calls=%fused_computation.clone.1 | custom fusion | bytes 262160 | tf_op jit(solution)/shard_map/while/body/gather | solution.py:123
  69.3 1.6 %gather_fusion.1 = bf16[4,128,128]{2,1,0:T(8,128)(2,1)S(1)} fusion(bf16[16,128,128]{2,1,0:T(8,128)(2,1)} %get-tuple-element.299, s32[1024]{0:T(1024)S(1)} %pad_clamp_fusion.2), kind=kCustom, calls=%fused_computation.1.clone.1 | custom fusion | bytes 262160 | tf_op jit(solution)/shard_map/while/body/gather | solution.py:124
  71.8 1.6 %gather_fusion = bf16[4,128,128]{2,1,0:T(8,128)(2,1)S(1)} fusion(bf16[16,128,128]{2,1,0:T(8,128)(2,1)} %get-tuple-element.297, s32[1024]{0:T(1024)S(1)} %pad_clamp_fusion.2), kind=kCustom, calls=%fused_computation.clone.1 | custom fusion | bytes 262160 | tf_op jit(solution)/shard_map/while/body/gather | solution.py:123
  74.5 1.6 %gather_fusion.1 = bf16[4,128,128]{2,1,0:T(8,128)(2,1)S(1)} fusion(bf16[16,128,128]{2,1,0:T(8,128)(2,1)} %get-tuple-element.299, s32[1024]{0:T(1024)S(1)} %pad_clamp_fusion.2), kind=kCustom, calls=%fused_computation.1.clone.1 | custom fusion | bytes 262160 | tf_op jit(solution)/shard_map/while/body/gather | solution.py:124
  77.0 2.5 %collective-permute-start.5 = (bf16[1,5,64]{2,1,0:T(8,128)(2,1)S(1)}, bf16[1,5,64]{2,1,0:T(8,128)(2,1)S(1)}, u32[]{:S(2)}, u32[]{:S(2)}) collective-permute-start(bf16[1,5,64]{2,1,0:T(8,128)(2,1)S(1)} %dynamic-slice_convert_fusion.1), channel_id=1, source_target_pairs={{0,8},{8,0},{1,9},{9,1},{2,10},{10,2},{3,11},{11,3},{4,12},{12,4},... | collective-permute-start | bytes 1928 | tf_op jit(solution)/shard_map/ppermute | solution.py:20
  79.6 1.9 %collective-permute-start.3 = (bf16[1,5,64]{2,1,0:T(8,128)(2,1)S(1)}, bf16[1,5,64]{2,1,0:T(8,128)(2,1)S(1)}, u32[]{:S(2)}, u32[]{:S(2)}) collective-permute-start(bf16[1,5,64]{2,1,0:T(8,128)(2,1)S(1)} %dynamic-slice_convert_fusion.2), channel_id=1, source_target_pairs={{0,8},{8,0},{1,9},{9,1},{2,10},{10,2},{3,11},{11,3},{4,12},{12,4},... | collective-permute-start | bytes 1928 | tf_op jit(solution)/shard_map/ppermute | solution.py:20
  81.6 2.4 %collective-permute-start.4 = (bf16[64,1,5,128]{0,3,2,1:T(8,128)(2,1)S(1)}, bf16[64,1,5,128]{0,3,2,1:T(8,128)(2,1)S(1)}, u32[]{:S(2)}, u32[]{:S(2)}) collective-permute-start(bf16[64,1,5,128]{0,3,2,1:T(8,128)(2,1)S(1)} %dynamic-slice_convert_fusion), channel_id=1, source_target_pairs={{0,8},{8,0},{1,9},{9,1},{2,10},{10,2},{3,11},{11,3},{4,12},{12,4},... | collective-permute-start | bytes 245768 | tf_op jit(solution)/shard_map/ppermute | solution.py:20
  84.1 0.9 collective-permute-done.4
  85.3 25.7 %all_gather.12 = bf16[64,8,640]{2,0,1:T(8,128)(2,1)S(1)} all-gather(bf16[64,1,640]{2,0,1:T(8,128)(2,1)S(1)} %copy.52), channel_id=1, replica_groups=mesh['z'=4,'x'=8,'core'=2,'tp'=8] {'tp'}, dimensions={1}, use_global_device_ids=true | all-gather | bytes 737280 | tf_op jit(solution)/shard_map/all_gather | solution.py:161
  111.0 4.9 %fusion.22 = bf16[64,640]{1,0:T(8,128)(2,1)S(1)} fusion(bf16[64,8,640]{2,0,1:T(8,128)(2,1)S(1)} %all_gather.12, bf16[640,8,640]{2,0,1:T(8,128)(2,1)} %all-gather.2.cloned.1.call-done), kind=kOutput, calls=%fused_computation.37 | convolution fusion | flops 419471360 | bytes 7290880 | tf_op jit(solution)/shard_map/dot_general | solution.py:162
  116.5 27.4 %all_gather.15 = bf16[64,64,80]{1,0,2:T(8,128)(2,1)S(1)} all-gather(bf16[64,64,10]{1,0,2:T(8,128)(2,1)S(1)} %copy.44), channel_id=1, replica_groups=mesh['z'=4,'x'=8,'core'=2,'tp'=8] {'tp'}, dimensions={2}, use_global_device_ids=true | all-gather | bytes 737280 | tf_op jit(solution)/shard_map/all_gather | solution.py:172
  143.9 1.5 copy.45
  145.4 2.9 %reshape.318 = bf16[64,5120]{1,0:T(8,128)(2,1)} reshape(bf16[64,64,80]{2,1,0:T(8,128)(2,1)S(1)} %copy.45) | data formatting | bytes 1310720 | tf_op jit(solution)/shard_map/reshape | solution.py:173
  (95 shorter events, 11.9 us)
Async XLA Ops:
  6.5 48.4 %copy-start = (s32[32,32]{1,0:T(8,128)S(1)}, s32[32,32]{1,0:T(8,128)}, u32[]{:S(2)}) copy-start(s32[32,32]{1,0:T(8,128)} %param.16) | copy-start | bytes 12292
  6.5 39.3 %copy-start.1 = (bf16[64,640]{1,0:T(8,128)(2,1)S(1)}, bf16[64,640]{1,0:T(8,128)(2,1)}, u32[]{:S(2)}) copy-start(bf16[64,640]{1,0:T(8,128)(2,1)} %param.10) | copy-start | bytes 245764
  6.5 104.5 %all-gather.2.cloned.1.call-start = ((), (), s32[]{:S(2)}) async-start(), calls=%async_computation.1 | async-start | bytes 6963200 | tf_op jit(solution)/shard_map/all_gather | solution.py:62
  7.5 38.4 %copy-start.4 = (s32[32]{0:T(128)S(1)}, s32[32]{0:T(128)}, u32[]{:S(2)}) copy-start(s32[32]{0:T(128)} %param.15) | copy-start | bytes 388
  7.5 39.7 %copy-start.2 = (bf16[64,128]{1,0:T(8,128)(2,1)S(1)}, bf16[64,128]{1,0:T(8,128)(2,1)}, u32[]{:S(2)}) copy-start(bf16[64,128]{1,0:T(8,128)(2,1)} %param.11) | copy-start | bytes 49156
  45.9 6.4 %copy-start.3 = (bf16[64,128]{1,0:T(8,128)(2,1)S(1)}, bf16[64,128]{1,0:T(8,128)(2,1)}, u32[]{:S(2)}) copy-start(bf16[64,128]{1,0:T(8,128)(2,1)} %param.12) | copy-start | bytes 49156
  47.9 7.1 %collective-permute-start.1 = (bf16[64,5,128]{2,1,0:T(8,128)(2,1)S(1)}, bf16[64,5,128]{2,1,0:T(8,128)(2,1)S(1)}, u32[]{:S(2)}, u32[]{:S(2)}) collective-permute-start(bf16[64,5,128]{2,1,0:T(8,128)(2,1)S(1)} %fusion.26), channel_id=1, source_target_pairs={{0,8},{8,0},{1,9},{9,1},{2,10},{10,2},{3,11},{11,3},{4,12},{12,4},... | collective-permute-start | bytes 245768 | tf_op jit(solution)/shard_map/ppermute | solution.py:20
  49.9 5.3 %collective-permute-start = (bf16[64,1,128]{2,0,1:T(8,128)(2,1)S(1)}, bf16[64,1,128]{2,0,1:T(8,128)(2,1)S(1)}, u32[]{:S(2)}, u32[]{:S(2)}) collective-permute-start(bf16[64,1,128]{2,0,1:T(8,128)(2,1)S(1)} %bitcast.162), channel_id=1, source_target_pairs={{0,8},{8,0},{1,9},{9,1},{2,10},{10,2},{3,11},{11,3},{4,12},{12,4},... | collective-permute-start | bytes 49160 | tf_op jit(solution)/shard_map/ppermute | solution.py:20
  52.3 3.4 %collective-permute-start.2 = (bf16[64,1,128]{2,0,1:T(8,128)(2,1)S(1)}, bf16[64,1,128]{2,0,1:T(8,128)(2,1)S(1)}, u32[]{:S(2)}, u32[]{:S(2)}) collective-permute-start(bf16[64,1,128]{2,0,1:T(8,128)(2,1)S(1)} %bitcast.163), channel_id=1, source_target_pairs={{0,8},{8,0},{1,9},{9,1},{2,10},{10,2},{3,11},{11,3},{4,12},{12,4},... | collective-permute-start | bytes 49160 | tf_op jit(solution)/shard_map/ppermute | solution.py:20
  77.0 7.0 %collective-permute-start.5 = (bf16[1,5,64]{2,1,0:T(8,128)(2,1)S(1)}, bf16[1,5,64]{2,1,0:T(8,128)(2,1)S(1)}, u32[]{:S(2)}, u32[]{:S(2)}) collective-permute-start(bf16[1,5,64]{2,1,0:T(8,128)(2,1)S(1)} %dynamic-slice_convert_fusion.1), channel_id=1, source_target_pairs={{0,8},{8,0},{1,9},{9,1},{2,10},{10,2},{3,11},{11,3},{4,12},{12,4},... | collective-permute-start | bytes 1928 | tf_op jit(solution)/shard_map/ppermute | solution.py:20
  79.6 4.5 %collective-permute-start.3 = (bf16[1,5,64]{2,1,0:T(8,128)(2,1)S(1)}, bf16[1,5,64]{2,1,0:T(8,128)(2,1)S(1)}, u32[]{:S(2)}, u32[]{:S(2)}) collective-permute-start(bf16[1,5,64]{2,1,0:T(8,128)(2,1)S(1)} %dynamic-slice_convert_fusion.2), channel_id=1, source_target_pairs={{0,8},{8,0},{1,9},{9,1},{2,10},{10,2},{3,11},{11,3},{4,12},{12,4},... | collective-permute-start | bytes 1928 | tf_op jit(solution)/shard_map/ppermute | solution.py:20
  81.6 3.4 %collective-permute-start.4 = (bf16[64,1,5,128]{0,3,2,1:T(8,128)(2,1)S(1)}, bf16[64,1,5,128]{0,3,2,1:T(8,128)(2,1)S(1)}, u32[]{:S(2)}, u32[]{:S(2)}) collective-permute-start(bf16[64,1,5,128]{0,3,2,1:T(8,128)(2,1)S(1)} %dynamic-slice_convert_fusion), channel_id=1, source_target_pairs={{0,8},{8,0},{1,9},{9,1},{2,10},{10,2},{3,11},{11,3},{4,12},{12,4},... | collective-permute-start | bytes 245768 | tf_op jit(solution)/shard_map/ppermute | solution.py:20
Sparse Core Ops, SparseCore 0:
  45.9 42.5 all-gather.1

commit v9 on v8

--- a/solution.py
+++ b/solution.py
@@ -8,7 +8,6 @@
 
 HD = 128
 GROUP = 5
-BLOCK_PAGES = 4
 ROWS = ("z", "x", "core")
 
 
@@ -68,7 +67,6 @@
     local_heads = k_new.shape[1] // HD
     pages_local = k_cache.shape[0]
     page_rows = k_cache.shape[1]
-    block_rows = BLOCK_PAGES * page_rows
     scale = 1.0 / math.sqrt(HD)
     weights_mine, share = output_rows(w_out)
     device_row = (lax.axis_index("z") * lax.axis_size("x") + lax.axis_index("x")) * lax.axis_size(
@@ -111,25 +109,22 @@
     even_pages = (page_count + 1) // 2
     first_page = jnp.where(parity == 0, 0, even_pages)
     last_page = jnp.where(parity == 0, even_pages, page_count)
-    table_row = jnp.concatenate([page_table[request], jnp.full((BLOCK_PAGES,), -1, jnp.int32)])
+    table_row = page_table[request]
+    logical = jnp.arange(table_row.shape[0])
+    in_range = (logical >= first_page) & (logical < last_page)
     offset = device_row * pages_local
-    block_count = (last_page - first_page + BLOCK_PAGES - 1) // BLOCK_PAGES
-
-    def visit(block, carry):
-        block_first = first_page + block * BLOCK_PAGES
-        logical = block_first + jnp.arange(BLOCK_PAGES)
-        physical = lax.dynamic_slice(table_row, (block_first,), (BLOCK_PAGES,))
-        slots = jnp.clip(physical - offset, 0, pages_local - 1)
-        block_keys = k_cache[slots].reshape(block_rows, local_heads, HD)
-        block_values = v_cache[slots].reshape(block_rows, local_heads, HD)
-        key_places = (logical[:, None] * page_rows + jnp.arange(page_rows)[None, :]).reshape(
-            block_rows
-        )
-        usable = jnp.repeat(logical < last_page, page_rows) & (key_places < length)
-        allowed = jnp.broadcast_to(usable[None, :], (all_rows, block_rows))
-        return absorb(carry, queries, block_keys, block_values, allowed, scale)
-
-    running_max, running_sum, output = lax.fori_loop(0, block_count, visit, state)
+    slot_ids = jnp.arange(pages_local)
+    match = in_range[:, None] & (table_row[:, None] - offset == slot_ids[None, :])
+    used = jnp.any(match, axis=0)
+    base = jnp.sum(jnp.where(match, logical[:, None], 0), axis=0) * page_rows
+    key_places = (base[:, None] + jnp.arange(page_rows)[None, :]).reshape(-1)
+    usable = jnp.repeat(used, page_rows) & (key_places < length)
+    allowed = jnp.broadcast_to(usable[None, :], (all_rows, pages_local * page_rows))
+    pool_keys = k_cache.reshape(pages_local * page_rows, local_heads, HD)
+    pool_values = v_cache.reshape(pages_local * page_rows, local_heads, HD)
+    running_max, running_sum, output = absorb(
+        state, queries, pool_keys, pool_values, allowed, scale
+    )
     peer_start = (1 - parity) * own_rows
     own_start = parity * own_rows
     outgoing = (

time: 156 us -> 142 us (0.910)
  the two profiles are of different devices: /device:TPU:68 before, /device:TPU:6 now
where the time goes in v9:
time: 142 us
  blocking collectives  90.4 us (64%)
  between operations  15 us (11%)
  starting transfers between devices  13 us (9%)
  local copies, waits for them, and re-layouts  9.14 us (6%)
  matrix products  7.8 us (5%)
  other arithmetic  5.59 us (4%)
    all_gather x1, blocking collectives, shards(): gathered = lax.all_gather(projected, 'tp', axis=2, tiled=True)  27.3 us
    all_gather x1, blocking collectives, shards(): full_rows = lax.all_gather(attention[:, None], 'tp', axis=1, tiled=True)  25.6 us
    all_gather x1, blocking collectives, output_rows(): near = lax.all_gather(mine, 'z', axis=0, tiled=True)  20.9 us
    all_to_all x1, blocking collectives, output_rows(): lax.all_to_all(w_out.reshape(parts, share, width), 'tp', 0, 0, tiled=True)  16.7 us
    ppermute x6, starting transfers between devices, from_partner(): lax.ppermute(value, axis, [(i, i ^ 1 << distance) for i in range(lax.axis...  13 us
    dot_general x1, matrix products, shards(): lax.dot_general(full_rows, weights_mine, (((1, 2), (1, 2)), ((), ())), pr...  4.94 us
    reshape x1, local copies, waits for them, and re-layouts, shards(): return gathered.reshape(own_rows, -1)  2.92 us
  transfers between devices with their start and end apart: 7, of which 1 were waited for; matrix products, arithmetic and copies ran while one was open for 8% of the time, Pallas kernels for 0%

profile of v9, /device:TPU:6, one launch (start us, length us, event | category | flops | bytes accessed | tf_op | source)
XLA Modules:
  0.0 141.8 jit_solution(468860128449095324)
XLA Ops:
  6.5 1.0 reshape.304
  7.5 16.7 %all_to_all.5 = bf16[8,10,640]{2,1,0:T(8,128)(2,1)S(1)} all-to-all(bf16[8,10,640]{2,1,0:T(8,128)(2,1)S(1)} %reshape.304), channel_id=1, replica_groups=mesh['z'=4,'x'=8,'core'=2,'tp'=8] {'tp'}, dimensions={0} | all-to-all | bytes 204800 | tf_op jit(solution)/shard_map/all_to_all | solution.py:58
  24.2 20.9 %all_gather.13 = bf16[40,8,640]{2,1,0:T(8,128)(2,1)S(1)} all-gather(bf16[10,8,640]{2,1,0:T(8,128)(2,1)S(1)} %copy.40), channel_id=1, replica_groups=mesh['z'=4,'x'=8,'core'=2,'tp'=8] {'z'}, dimensions={0}, use_global_device_ids=true | all-gather | bytes 512000 | tf_op jit(solution)/shard_map/all_gather | solution.py:60
  45.1 0.8 copy.41
  45.9 1.0 reshape.306
  46.9 1.3 dynamic_slice.24
  48.9 0.7 convert_bitcast_fusion
  49.9 0.8 fusion.35
  51.0 1.9 %collective-permute-start.1 = (bf16[64,5,128]{2,1,0:T(8,128)(2,1)S(1)}, bf16[64,5,128]{2,1,0:T(8,128)(2,1)S(1)}, u32[]{:S(2)}, u32[]{:S(2)}) collective-permute-start(bf16[64,5,128]{2,1,0:T(8,128)(2,1)S(1)} %fusion.23), channel_id=1, source_target_pairs={{0,8},{8,0},{1,9},{9,1},{2,10},{10,2},{3,11},{11,3},{4,12},{12,4},... | collective-permute-start | bytes 245768 | tf_op jit(solution)/shard_map/ppermute | solution.py:19
  52.9 2.4 %collective-permute-start = (bf16[64,1,128]{2,0,1:T(8,128)(2,1)S(1)}, bf16[64,1,128]{2,0,1:T(8,128)(2,1)S(1)}, u32[]{:S(2)}, u32[]{:S(2)}) collective-permute-start(bf16[64,1,128]{2,0,1:T(8,128)(2,1)S(1)} %bitcast.177), channel_id=1, source_target_pairs={{0,8},{8,0},{1,9},{9,1},{2,10},{10,2},{3,11},{11,3},{4,12},{12,4},... | collective-permute-start | bytes 49160 | tf_op jit(solution)/shard_map/ppermute | solution.py:19
  55.3 1.9 %collective-permute-start.2 = (bf16[64,1,128]{2,0,1:T(8,128)(2,1)S(1)}, bf16[64,1,128]{2,0,1:T(8,128)(2,1)S(1)}, u32[]{:S(2)}, u32[]{:S(2)}) collective-permute-start(bf16[64,1,128]{2,0,1:T(8,128)(2,1)S(1)} %bitcast.178), channel_id=1, source_target_pairs={{0,8},{8,0},{1,9},{9,1},{2,10},{10,2},{3,11},{11,3},{4,12},{12,4},... | collective-permute-start | bytes 49160 | tf_op jit(solution)/shard_map/ppermute | solution.py:19
  58.9 0.7 fusion.56
  60.0 1.0 fusion.1
  61.2 1.3 fusion.2
  62.6 2.4 %collective-permute-start.5 = (bf16[1,5,64]{2,1,0:T(8,128)(2,1)S(1)}, bf16[1,5,64]{2,1,0:T(8,128)(2,1)S(1)}, u32[]{:S(2)}, u32[]{:S(2)}) collective-permute-start(bf16[1,5,64]{2,1,0:T(8,128)(2,1)S(1)} %dynamic-slice_convert_fusion.1), channel_id=1, source_target_pairs={{0,8},{8,0},{1,9},{9,1},{2,10},{10,2},{3,11},{11,3},{4,12},{12,4},... | collective-permute-start | bytes 1928 | tf_op jit(solution)/shard_map/ppermute | solution.py:19
  65.1 1.9 %collective-permute-start.3 = (bf16[1,5,64]{2,1,0:T(8,128)(2,1)S(1)}, bf16[1,5,64]{2,1,0:T(8,128)(2,1)S(1)}, u32[]{:S(2)}, u32[]{:S(2)}) collective-permute-start(bf16[1,5,64]{2,1,0:T(8,128)(2,1)S(1)} %dynamic-slice_convert_fusion.2), channel_id=1, source_target_pairs={{0,8},{8,0},{1,9},{9,1},{2,10},{10,2},{3,11},{11,3},{4,12},{12,4},... | collective-permute-start | bytes 1928 | tf_op jit(solution)/shard_map/ppermute | solution.py:19
  67.3 1.3 fusion.13
  68.6 2.4 %collective-permute-start.4 = (bf16[64,1,5,128]{3,0,2,1:T(8,128)(2,1)S(1)}, bf16[64,1,5,128]{3,0,2,1:T(8,128)(2,1)S(1)}, u32[]{:S(2)}, u32[]{:S(2)}) collective-permute-start(bf16[64,1,5,128]{3,0,2,1:T(8,128)(2,1)S(1)} %dynamic-slice_convert_fusion), channel_id=1, source_target_pairs={{0,8},{8,0},{1,9},{9,1},{2,10},{10,2},{3,11},{11,3},{4,12},{12,4},... | collective-permute-start | bytes 245768 | tf_op jit(solution)/shard_map/ppermute | solution.py:19
  71.2 0.8 collective-permute-done.4
  72.2 25.6 %all_gather.12 = bf16[64,8,640]{2,0,1:T(8,128)(2,1)S(1)} all-gather(bf16[64,1,640]{2,0,1:T(8,128)(2,1)S(1)} %copy_bitcast_fusion), channel_id=1, replica_groups=mesh['z'=4,'x'=8,'core'=2,'tp'=8] {'tp'}, dimensions={1}, use_global_device_ids=true | all-gather | bytes 737280 | tf_op jit(solution)/shard_map/all_gather | solution.py:156
  97.8 4.9 %fusion.19 = bf16[64,640]{1,0:T(8,128)(2,1)S(1)} fusion(bf16[64,8,640]{2,0,1:T(8,128)(2,1)S(1)} %all_gather.12, bf16[640,8,640]{2,0,1:T(8,128)(2,1)} %all-gather.2.cloned.1.call-done), kind=kOutput, calls=%fused_computation.19 | convolution fusion | flops 419471360 | bytes 7290880 | tf_op jit(solution)/shard_map/dot_general | solution.py:157
  103.3 27.3 %all_gather.15 = bf16[64,64,80]{1,0,2:T(8,128)(2,1)S(1)} all-gather(bf16[64,64,10]{1,0,2:T(8,128)(2,1)S(1)} %copy.44), channel_id=1, replica_groups=mesh['z'=4,'x'=8,'core'=2,'tp'=8] {'tp'}, dimensions={2}, use_global_device_ids=true | all-gather | bytes 737280 | tf_op jit(solution)/shard_map/all_gather | solution.py:167
  130.5 1.5 %copy.45 = bf16[64,64,80]{2,1,0:T(8,128)(2,1)S(1)} copy(bf16[64,64,80]{1,0,2:T(8,128)(2,1)S(1)} %all_gather.15) | data formatting | bytes 1310720 | tf_op jit(solution)/shard_map/all_gather | solution.py:167
  132.0 2.9 %reshape.305 = bf16[64,5120]{1,0:T(8,128)(2,1)} reshape(bf16[64,64,80]{2,1,0:T(8,128)(2,1)S(1)} %copy.45) | data formatting | bytes 1310720 | tf_op jit(solution)/shard_map/reshape | solution.py:168
  (42 shorter events, 3.3 us)
Async XLA Ops:
  6.5 53.5 %copy-start = (bf16[16,128,128]{2,1,0:T(8,128)(2,1)S(1)}, bf16[16,128,128]{2,1,0:T(8,128)(2,1)}, u32[]{:S(2)}) copy-start(bf16[16,128,128]{2,1,0:T(8,128)(2,1)} %param.11) | copy-start | bytes 1572868
  6.5 48.8 %copy-start.1 = (bf16[64,128]{1,0:T(8,128)(2,1)S(1)}, bf16[64,128]{1,0:T(8,128)(2,1)}, u32[]{:S(2)}) copy-start(bf16[64,128]{1,0:T(8,128)(2,1)} %param.10) | copy-start | bytes 49156
  6.5 91.3 %all-gather.2.cloned.1.call-start = ((), (), s32[]{:S(2)}) async-start(), calls=%async_computation.1 | async-start | bytes 6963200 | tf_op jit(solution)/shard_map/all_gather | solution.py:61
  51.0 8.7 %collective-permute-start.1 = (bf16[64,5,128]{2,1,0:T(8,128)(2,1)S(1)}, bf16[64,5,128]{2,1,0:T(8,128)(2,1)S(1)}, u32[]{:S(2)}, u32[]{:S(2)}) collective-permute-start(bf16[64,5,128]{2,1,0:T(8,128)(2,1)S(1)} %fusion.23), channel_id=1, source_target_pairs={{0,8},{8,0},{1,9},{9,1},{2,10},{10,2},{3,11},{11,3},{4,12},{12,4},... | collective-permute-start | bytes 245768 | tf_op jit(solution)/shard_map/ppermute | solution.py:19
  52.9 6.9 %collective-permute-start = (bf16[64,1,128]{2,0,1:T(8,128)(2,1)S(1)}, bf16[64,1,128]{2,0,1:T(8,128)(2,1)S(1)}, u32[]{:S(2)}, u32[]{:S(2)}) collective-permute-start(bf16[64,1,128]{2,0,1:T(8,128)(2,1)S(1)} %bitcast.177), channel_id=1, source_target_pairs={{0,8},{8,0},{1,9},{9,1},{2,10},{10,2},{3,11},{11,3},{4,12},{12,4},... | collective-permute-start | bytes 49160 | tf_op jit(solution)/shard_map/ppermute | solution.py:19
  55.3 11.7 %collective-permute-start.2 = (bf16[64,1,128]{2,0,1:T(8,128)(2,1)S(1)}, bf16[64,1,128]{2,0,1:T(8,128)(2,1)S(1)}, u32[]{:S(2)}, u32[]{:S(2)}) collective-permute-start(bf16[64,1,128]{2,0,1:T(8,128)(2,1)S(1)} %bitcast.178), channel_id=1, source_target_pairs={{0,8},{8,0},{1,9},{9,1},{2,10},{10,2},{3,11},{11,3},{4,12},{12,4},... | collective-permute-start | bytes 49160 | tf_op jit(solution)/shard_map/ppermute | solution.py:19
  60.0 7.3 %copy-start.2 = (bf16[16,128,128]{2,1,0:T(8,128)(2,1)S(1)}, bf16[16,128,128]{2,1,0:T(8,128)(2,1)}, u32[]{:S(2)}) copy-start(bf16[16,128,128]{2,1,0:T(8,128)(2,1)} %param.12) | copy-start | bytes 1572868
  62.6 8.5 %collective-permute-start.5 = (bf16[1,5,64]{2,1,0:T(8,128)(2,1)S(1)}, bf16[1,5,64]{2,1,0:T(8,128)(2,1)S(1)}, u32[]{:S(2)}, u32[]{:S(2)}) collective-permute-start(bf16[1,5,64]{2,1,0:T(8,128)(2,1)S(1)} %dynamic-slice_convert_fusion.1), channel_id=1, source_target_pairs={{0,8},{8,0},{1,9},{9,1},{2,10},{10,2},{3,11},{11,3},{4,12},{12,4},... | collective-permute-start | bytes 1928 | tf_op jit(solution)/shard_map/ppermute | solution.py:19
  65.1 6.0 %collective-permute-start.3 = (bf16[1,5,64]{2,1,0:T(8,128)(2,1)S(1)}, bf16[1,5,64]{2,1,0:T(8,128)(2,1)S(1)}, u32[]{:S(2)}, u32[]{:S(2)}) collective-permute-start(bf16[1,5,64]{2,1,0:T(8,128)(2,1)S(1)} %dynamic-slice_convert_fusion.2), channel_id=1, source_target_pairs={{0,8},{8,0},{1,9},{9,1},{2,10},{10,2},{3,11},{11,3},{4,12},{12,4},... | collective-permute-start | bytes 1928 | tf_op jit(solution)/shard_map/ppermute | solution.py:19
  68.6 3.3 %collective-permute-start.4 = (bf16[64,1,5,128]{3,0,2,1:T(8,128)(2,1)S(1)}, bf16[64,1,5,128]{3,0,2,1:T(8,128)(2,1)S(1)}, u32[]{:S(2)}, u32[]{:S(2)}) collective-permute-start(bf16[64,1,5,128]{3,0,2,1:T(8,128)(2,1)S(1)} %dynamic-slice_convert_fusion), channel_id=1, source_target_pairs={{0,8},{8,0},{1,9},{9,1},{2,10},{10,2},{3,11},{11,3},{4,12},{12,4},... | collective-permute-start | bytes 245768 | tf_op jit(solution)/shard_map/ppermute | solution.py:19
Sparse Core Ops, SparseCore 0:
  46.0 43.5 all-gather.1

commit v10 on v9

--- a/solution.py
+++ b/solution.py
@@ -83,9 +83,13 @@
         k_new.reshape(own_rows, local_heads, HD).astype(jnp.float32), own_places
     ).astype(jnp.bfloat16)
     own_values = v_new.reshape(own_rows, local_heads, HD)
-    peer_queries, peer_keys, peer_values = from_partner(
-        (own_queries, own_keys, own_values), "core", 0
+    query_heads = own_queries.shape[1]
+    peer_pack = from_partner(
+        jnp.concatenate([own_queries, own_keys, own_values], axis=1), "core", 0
     )
+    peer_queries = peer_pack[:, :query_heads]
+    peer_keys = peer_pack[:, query_heads : query_heads + local_heads]
+    peer_values = peer_pack[:, query_heads + local_heads :]
 
     def ordered(mine, theirs):
         return jnp.where(
@@ -132,11 +136,18 @@
         lax.dynamic_slice_in_dim(running_max, peer_start, own_rows, 2),
         lax.dynamic_slice_in_dim(running_sum, peer_start, own_rows, 2),
     )
-    other_output, other_max, other_sum = (
-        from_partner(outgoing[0].astype(jnp.bfloat16), "core", 0).astype(jnp.float32),
-        from_partner(outgoing[1].astype(jnp.bfloat16), "core", 0).astype(jnp.float32),
-        from_partner(outgoing[2].astype(jnp.bfloat16), "core", 0).astype(jnp.float32),
+    outgoing = jnp.concatenate(
+        [
+            outgoing[0].astype(jnp.bfloat16),
+            jnp.transpose(outgoing[1], (2, 0, 1))[..., None].astype(jnp.bfloat16),
+            jnp.transpose(outgoing[2], (2, 0, 1))[..., None].astype(jnp.bfloat16),
+        ],
+        axis=-1,
     )
+    incoming = from_partner(outgoing, "core", 0).astype(jnp.float32)
+    other_output = incoming[..., :HD]
+    other_max = jnp.transpose(incoming[..., HD], (1, 2, 0))
+    other_sum = jnp.transpose(incoming[..., HD + 1], (1, 2, 0))
     mine_output = lax.dynamic_slice_in_dim(output, own_start, own_rows, 0)
     mine_max = lax.dynamic_slice_in_dim(running_max, own_start, own_rows, 2)
     mine_sum = lax.dynamic_slice_in_dim(running_sum, own_start, own_rows, 2)

time: 142 us -> 140 us (0.986)
  starting transfers between devices: 13 us -> 4.31 us
  local copies, waits for them, and re-layouts: 9.14 us -> 12.8 us
  matrix products: 7.8 us -> 10.4 us
    ppermute x6 -> x2, starting transfers between devices: 13 us -> 4.31 us  [from_partner(): lax.ppermute(value, axis, [(i, i ^ 1 << distance) for i in range(lax.axis...]
    dot_general x2, matrix products: 1.59 us -> 4.19 us  [absorb(): jnp.einsum('cgqk,kcd->qcgd', weights.astype(jnp.bfloat16), block_values,...]
    unnamed x6 -> x9, local copies, waits for them, and re-layouts: 0.01 us -> 2.31 us
  transfers between devices with their start and end apart: 7 -> 3, of which waited for: 1 -> 1; matrix products, arithmetic and copies ran while one was open for 8% -> 11% of each run, Pallas kernels for 0% -> 0%
where the time goes in v10:
time: 140 us
  blocking collectives  90.4 us (65%)
  between operations  15 us (11%)
  local copies, waits for them, and re-layouts  12.8 us (9%)
  matrix products  10.4 us (7%)
  other arithmetic  5.84 us (4%)
  starting transfers between devices  4.31 us (3%)
    all_gather x1, blocking collectives, shards(): gathered = lax.all_gather(projected, 'tp', axis=2, tiled=True)  27.2 us
    all_gather x1, blocking collectives, shards(): full_rows = lax.all_gather(attention[:, None], 'tp', axis=1, tiled=True)  25.7 us
    all_gather x1, blocking collectives, output_rows(): near = lax.all_gather(mine, 'z', axis=0, tiled=True)  20.9 us
    all_to_all x1, blocking collectives, output_rows(): lax.all_to_all(w_out.reshape(parts, share, width), 'tp', 0, 0, tiled=True)  16.7 us
    dot_general x1, matrix products, shards(): lax.dot_general(full_rows, weights_mine, (((1, 2), (1, 2)), ((), ())), pr...  4.94 us
    ppermute x2, starting transfers between devices, from_partner(): lax.ppermute(value, axis, [(i, i ^ 1 << distance) for i in range(lax.axis...  4.31 us
    dot_general x2, matrix products, absorb(): jnp.einsum('cgqk,kcd->qcgd', weights.astype(jnp.bfloat16), block_values,...  4.19 us
    reshape x1, local copies, waits for them, and re-layouts, shards(): return gathered.reshape(own_rows, -1)  2.92 us
  transfers between devices with their start and end apart: 3, of which 1 were waited for; matrix products, arithmetic and copies ran while one was open for 11% of the time, Pallas kernels for 0%

profile of v10, /device:TPU:6, one launch (start us, length us, event | category | flops | bytes accessed | tf_op | source)
XLA Modules:
  0.0 139.7 jit_solution(10730181127734676627)
XLA Ops:
  6.5 1.0 reshape.330
  7.5 16.7 %all_to_all.5 = bf16[8,10,640]{2,1,0:T(8,128)(2,1)S(1)} all-to-all(bf16[8,10,640]{2,1,0:T(8,128)(2,1)S(1)} %reshape.330), channel_id=1, replica_groups=mesh['z'=4,'x'=8,'core'=2,'tp'=8] {'tp'}, dimensions={0} | all-to-all | bytes 204800 | tf_op jit(solution)/shard_map/all_to_all | solution.py:58
  24.2 20.9 %all_gather.13 = bf16[40,8,640]{2,1,0:T(8,128)(2,1)S(1)} all-gather(bf16[10,8,640]{2,1,0:T(8,128)(2,1)S(1)} %copy.86), channel_id=1, replica_groups=mesh['z'=4,'x'=8,'core'=2,'tp'=8] {'z'}, dimensions={0}, use_global_device_ids=true | all-gather | bytes 512000 | tf_op jit(solution)/shard_map/all_gather | solution.py:60
  45.1 0.8 copy.87
  45.9 1.0 reshape.332
  46.9 1.3 dynamic_slice.24
  48.9 0.7 convert_bitcast_fusion
  49.9 0.8 pad_maximum_fusion.2
  50.7 0.7 copy.77
  51.9 1.9 %collective-permute-start = (bf16[64,7,128]{2,1,0:T(8,128)(2,1)S(1)}, bf16[64,7,128]{2,1,0:T(8,128)(2,1)S(1)}, u32[]{:S(2)}, u32[]{:S(2)}) collective-permute-start(bf16[64,7,128]{2,1,0:T(8,128)(2,1)S(1)} %pad_maximum_fusion.1), channel_id=1, source_target_pairs={{0,8},{8,0},{1,9},{9,1},{2,10},{10,2},{3,11},{11,3},{4,12},{12,4},... | collective-permute-start | bytes 344072 | tf_op jit(solution)/shard_map/ppermute | solution.py:19
  54.5 0.7 fusion.75
  55.5 0.7 fusion.59
  56.7 1.0 fusion.1
  57.8 2.3 %copy-done.1 = f32[128,5,2048]{2,0,1:T(8,128)} copy-done((f32[128,5,2048]{2,0,1:T(8,128)}, f32[128,5,2048]{2,0,1:T(8,128)S(1)}, u32[]{:S(2)}) %copy-start.1) | copy-done | bytes 5242904
  60.1 1.3 fusion.2
  61.9 0.3 fusion.17
  62.2 3.9 %fusion.13 = f32[128,1,5,128]{3,0,2,1:T(8,128)S(1)} fusion(f32[128,1,5,128]{3,0,2,1:T(8,128)S(1)} %fusion.17, bf16[2048,128,1]{1,0,2:T(8,128)(2,1)S(1)} %bitcast.212, f32[128,5,2048]{2,0,1:T(8,128)} %copy-done.1, f32[5,128]{1,0:T(8,128)S(1)} %get-tuple-element.24, pred[2048]{0:T(1024)(128)(4,1)S(1)} %fusion.59), kind=kOutput, calls=%fused_computation.14 | convolution fusion | flops 342179840 | bytes 6427136 | tf_op jit(solution)/shard_map/cgqk,kcd->qcgd/dot_general | solution.py:44
  66.2 2.4 %collective-permute-start.1 = (bf16[64,1,5,130]{3,0,2,1:T(8,128)(2,1)S(1)}, bf16[64,1,5,130]{3,0,2,1:T(8,128)(2,1)S(1)}, u32[]{:S(2)}, u32[]{:S(2)}) collective-permute-start(bf16[64,1,5,130]{3,0,2,1:T(8,128)(2,1)S(1)} %pad_maximum_fusion), channel_id=1, source_target_pairs={{0,8},{8,0},{1,9},{9,1},{2,10},{10,2},{3,11},{11,3},{4,12},{12,4},... | collective-permute-start | bytes 249608 | tf_op jit(solution)/shard_map/ppermute | solution.py:19
  68.6 1.0 collective-permute-done.1
  70.2 25.7 %all_gather.12 = bf16[64,8,640]{2,0,1:T(8,128)(2,1)S(1)} all-gather(bf16[64,1,640]{2,0,1:T(8,128)(2,1)S(1)} %copy_bitcast_fusion), channel_id=1, replica_groups=mesh['z'=4,'x'=8,'core'=2,'tp'=8] {'tp'}, dimensions={1}, use_global_device_ids=true | all-gather | bytes 737280 | tf_op jit(solution)/shard_map/all_gather | solution.py:167
  95.9 4.9 %fusion.19 = bf16[64,640]{1,0:T(8,128)(2,1)S(1)} fusion(bf16[64,8,640]{2,0,1:T(8,128)(2,1)S(1)} %all_gather.12, bf16[640,8,640]{2,0,1:T(8,128)(2,1)} %all-gather.2.cloned.1.call-done), kind=kOutput, calls=%fused_computation.19 | convolution fusion | flops 419471360 | bytes 7290880 | tf_op jit(solution)/shard_map/dot_general | solution.py:168
  101.3 27.2 %all_gather.15 = bf16[64,64,80]{1,0,2:T(8,128)(2,1)S(1)} all-gather(bf16[64,64,10]{1,0,2:T(8,128)(2,1)S(1)} %copy.90), channel_id=1, replica_groups=mesh['z'=4,'x'=8,'core'=2,'tp'=8] {'tp'}, dimensions={2}, use_global_device_ids=true | all-gather | bytes 737280 | tf_op jit(solution)/shard_map/all_gather | solution.py:178
  128.5 1.5 %copy.91 = bf16[64,64,80]{2,1,0:T(8,128)(2,1)S(1)} copy(bf16[64,64,80]{1,0,2:T(8,128)(2,1)S(1)} %all_gather.15) | data formatting | bytes 1310720 | tf_op jit(solution)/shard_map/all_gather | solution.py:178
  130.0 2.9 %reshape.331 = bf16[64,5120]{1,0:T(8,128)(2,1)} reshape(bf16[64,64,80]{2,1,0:T(8,128)(2,1)S(1)} %copy.91) | data formatting | bytes 1310720 | tf_op jit(solution)/shard_map/reshape | solution.py:179
  (46 shorter events, 3.1 us)
Async XLA Ops:
  6.5 50.1 %copy-start = (bf16[16,128,128]{2,1,0:T(8,128)(2,1)S(1)}, bf16[16,128,128]{2,1,0:T(8,128)(2,1)}, u32[]{:S(2)}) copy-start(bf16[16,128,128]{2,1,0:T(8,128)(2,1)} %param.11) | copy-start | bytes 1572868
  6.5 89.3 %all-gather.2.cloned.1.call-start = ((), (), s32[]{:S(2)}) async-start(), calls=%async_computation.1 | async-start | bytes 6963200 | tf_op jit(solution)/shard_map/all_gather | solution.py:61
  51.9 4.3 %collective-permute-start = (bf16[64,7,128]{2,1,0:T(8,128)(2,1)S(1)}, bf16[64,7,128]{2,1,0:T(8,128)(2,1)S(1)}, u32[]{:S(2)}, u32[]{:S(2)}) collective-permute-start(bf16[64,7,128]{2,1,0:T(8,128)(2,1)S(1)} %pad_maximum_fusion.1), channel_id=1, source_target_pairs={{0,8},{8,0},{1,9},{9,1},{2,10},{10,2},{3,11},{11,3},{4,12},{12,4},... | collective-permute-start | bytes 344072 | tf_op jit(solution)/shard_map/ppermute | solution.py:19
  56.6 5.2 %copy-start.2 = (bf16[64,128]{1,0:T(8,128)(2,1)S(1)}, bf16[64,128]{1,0:T(8,128)(2,1)}, u32[]{:S(2)}) copy-start(bf16[64,128]{1,0:T(8,128)(2,1)} %param.10) | copy-start | bytes 49156
  56.7 5.6 %copy-start.3 = (bf16[16,128,128]{2,1,0:T(8,128)(2,1)S(1)}, bf16[16,128,128]{2,1,0:T(8,128)(2,1)}, u32[]{:S(2)}) copy-start(bf16[16,128,128]{2,1,0:T(8,128)(2,1)} %param.12) | copy-start | bytes 1572868
  57.7 2.4 %copy-start.1 = (f32[128,5,2048]{2,0,1:T(8,128)}, f32[128,5,2048]{2,0,1:T(8,128)S(1)}, u32[]{:S(2)}) copy-start(f32[128,5,2048]{2,0,1:T(8,128)S(1)} %get-tuple-element.30) | copy-start | bytes 15728644
  66.2 3.4 %collective-permute-start.1 = (bf16[64,1,5,130]{3,0,2,1:T(8,128)(2,1)S(1)}, bf16[64,1,5,130]{3,0,2,1:T(8,128)(2,1)S(1)}, u32[]{:S(2)}, u32[]{:S(2)}) collective-permute-start(bf16[64,1,5,130]{3,0,2,1:T(8,128)(2,1)S(1)} %pad_maximum_fusion), channel_id=1, source_target_pairs={{0,8},{8,0},{1,9},{9,1},{2,10},{10,2},{3,11},{11,3},{4,12},{12,4},... | collective-permute-start | bytes 249608 | tf_op jit(solution)/shard_map/ppermute | solution.py:19
Sparse Core Ops, SparseCore 0:
  46.0 43.5 all-gather.1

commit v11 on v10

--- a/solution.py
+++ b/solution.py
@@ -53,11 +53,15 @@
 
 def output_rows(w_out):
     parts = lax.axis_size("tp")
+    depth = lax.axis_size("z")
     rows, width = w_out.shape
     share = rows // parts
-    pieces = lax.all_to_all(w_out.reshape(parts, share, width), "tp", 0, 0, tiled=True)
-    mine = jnp.transpose(pieces, (1, 0, 2))
-    near = lax.all_gather(mine, "z", axis=0, tiled=True)
+    chunks = jnp.broadcast_to(w_out.reshape(1, parts, share, width), (depth, parts, share, width))
+    pieces = lax.all_to_all(
+        chunks.reshape(depth * parts, share, width), ("z", "tp"), 0, 0, tiled=True
+    )
+    near = jnp.transpose(pieces.reshape(depth, parts, share, width), (0, 2, 1, 3))
+    near = near.reshape(depth * share, parts, width)
     return lax.all_gather(near, ("x", "core"), axis=0, tiled=True), share
 
 

time: 140 us -> 140 us (level)
    all_gather x1 -> x0, blocking collectives: 20.9 us -> none  [output_rows(): near = lax.all_gather(mine, 'z', axis=0, tiled=True)]
    all_to_all x1, blocking collectives: 16.7 us -> 37.4 us  [output_rows(): lax.all_to_all(chunks.reshape(depth * parts, share, width), ('z', 'tp'),...]
  transfers between devices with their start and end apart: 3 -> 3, of which waited for: 1 -> 1; matrix products, arithmetic and copies ran while one was open for 11% -> 10% of each run, Pallas kernels for 0% -> 0%
where the time goes in v11:
time: 140 us; the launch traced here: 139 us
  blocking collectives  91.1 us (65%)
  between operations  15 us (11%)
  local copies, waits for them, and re-layouts  12.2 us (9%)
  matrix products  10.4 us (7%)
  other arithmetic  5.13 us (4%)
  starting transfers between devices  4.32 us (3%)
    all_to_all x1, blocking collectives, output_rows(): lax.all_to_all(chunks.reshape(depth * parts, share, width), ('z', 'tp'),...  37.4 us
    all_gather x1, blocking collectives, shards(): gathered = lax.all_gather(projected, 'tp', axis=2, tiled=True)  27.3 us
    all_gather x1, blocking collectives, shards(): full_rows = lax.all_gather(attention[:, None], 'tp', axis=1, tiled=True)  26.4 us
    dot_general x1, matrix products, shards(): lax.dot_general(full_rows, weights_mine, (((1, 2), (1, 2)), ((), ())), pr...  4.94 us
    ppermute x2, starting transfers between devices, from_partner(): lax.ppermute(value, axis, [(i, i ^ 1 << distance) for i in range(lax.axis...  4.32 us
    dot_general x2, matrix products, absorb(): jnp.einsum('cgqk,kcd->qcgd', weights.astype(jnp.bfloat16), block_values,...  4.16 us
    reshape x1, local copies, waits for them, and re-layouts, shards(): return gathered.reshape(own_rows, -1)  2.92 us
  transfers between devices with their start and end apart: 3, of which 1 were waited for; matrix products, arithmetic and copies ran while one was open for 10% of the time, Pallas kernels for 0%

profile of v11, /device:TPU:6, one launch (start us, length us, event | category | flops | bytes accessed | tf_op | source)
XLA Modules:
  0.0 139.1 jit_solution(9211877861156886975)
XLA Ops:
  6.5 1.0 broadcast_in_dim.110
  7.6 37.4 %all_to_all.5 = bf16[32,10,640]{2,1,0:T(8,128)(2,1)S(1)} all-to-all(bf16[32,10,640]{2,1,0:T(8,128)(2,1)S(1)} %bitcast.210), channel_id=1, replica_groups=mesh['z'=4,'x'=8,'core'=2,'tp'=8] {'z','tp'}, dimensions={0} | all-to-all | bytes 819200 | tf_op jit(solution)/shard_map/all_to_all | solution.py:60
  45.1 0.8 copy.101
  45.9 1.0 reshape.342
  46.9 1.3 dynamic_slice.24
  48.9 0.7 convert_bitcast_fusion
  50.5 1.9 %collective-permute-start = (bf16[64,7,128]{2,1,0:T(8,128)(2,1)S(1)}, bf16[64,7,128]{2,1,0:T(8,128)(2,1)S(1)}, u32[]{:S(2)}, u32[]{:S(2)}) collective-permute-start(bf16[64,7,128]{2,1,0:T(8,128)(2,1)S(1)} %pad_maximum_fusion.1), channel_id=1, source_target_pairs={{0,8},{8,0},{1,9},{9,1},{2,10},{10,2},{3,11},{11,3},{4,12},{12,4},... | collective-permute-start | bytes 344072 | tf_op jit(solution)/shard_map/ppermute | solution.py:19
  53.1 0.7 fusion.75
  54.0 0.7 fusion.59
  55.0 0.2 fusion.84
  55.2 1.1 fusion.1
  56.4 2.3 %copy-done.1 = f32[128,5,2048]{2,0,1:T(8,128)} copy-done((f32[128,5,2048]{2,0,1:T(8,128)}, f32[128,5,2048]{2,0,1:T(8,128)S(1)}, u32[]{:S(2)}) %copy-start.1) | copy-done | bytes 5242904
  58.7 1.3 fusion.2
  60.5 0.3 fusion.17
  60.8 3.8 %fusion.13 = f32[128,1,5,128]{3,0,2,1:T(8,128)S(1)} fusion(f32[128,1,5,128]{3,0,2,1:T(8,128)S(1)} %fusion.17, bf16[2048,128,1]{1,0,2:T(8,128)(2,1)S(1)} %bitcast.218, f32[128,5,2048]{2,0,1:T(8,128)} %copy-done.1, f32[5,128]{1,0:T(8,128)S(1)} %get-tuple-element.24, pred[2048]{0:T(1024)(128)(4,1)S(1)} %fusion.59), kind=kOutput, calls=%fused_computation.14 | convolution fusion | flops 342179840 | bytes 6427136 | tf_op jit(solution)/shard_map/cgqk,kcd->qcgd/dot_general | solution.py:44
  64.8 2.4 %collective-permute-start.1 = (bf16[64,1,5,130]{3,0,2,1:T(8,128)(2,1)S(1)}, bf16[64,1,5,130]{3,0,2,1:T(8,128)(2,1)S(1)}, u32[]{:S(2)}, u32[]{:S(2)}) collective-permute-start(bf16[64,1,5,130]{3,0,2,1:T(8,128)(2,1)S(1)} %pad_maximum_fusion), channel_id=1, source_target_pairs={{0,8},{8,0},{1,9},{9,1},{2,10},{10,2},{3,11},{11,3},{4,12},{12,4},... | collective-permute-start | bytes 249608 | tf_op jit(solution)/shard_map/ppermute | solution.py:19
  67.2 1.0 collective-permute-done.1
  68.2 0.2 slice_reduce_fusion.1
  68.5 0.2 copy_bitcast_fusion
  68.7 26.4 %all_gather.9 = bf16[64,8,640]{2,0,1:T(8,128)(2,1)S(1)} all-gather(bf16[64,1,640]{2,0,1:T(8,128)(2,1)S(1)} %copy_bitcast_fusion), channel_id=1, replica_groups=mesh['z'=4,'x'=8,'core'=2,'tp'=8] {'tp'}, dimensions={1}, use_global_device_ids=true | all-gather | bytes 737280 | tf_op jit(solution)/shard_map/all_gather | solution.py:171
  95.2 4.9 %fusion.19 = bf16[64,640]{1,0:T(8,128)(2,1)S(1)} fusion(bf16[64,8,640]{2,0,1:T(8,128)(2,1)S(1)} %all_gather.9, bf16[640,8,640]{2,0,1:T(8,128)(2,1)} %all-gather.2.cloned.1.call-done), kind=kOutput, calls=%fused_computation.19 | convolution fusion | flops 419471360 | bytes 7290880 | tf_op jit(solution)/shard_map/dot_general | solution.py:172
  100.6 27.3 %all_gather.11 = bf16[64,64,80]{1,0,2:T(8,128)(2,1)S(1)} all-gather(bf16[64,64,10]{1,0,2:T(8,128)(2,1)S(1)} %copy.104), channel_id=1, replica_groups=mesh['z'=4,'x'=8,'core'=2,'tp'=8] {'tp'}, dimensions={2}, use_global_device_ids=true | all-gather | bytes 737280 | tf_op jit(solution)/shard_map/all_gather | solution.py:182
  127.9 1.5 %copy.105 = bf16[64,64,80]{2,1,0:T(8,128)(2,1)S(1)} copy(bf16[64,64,80]{1,0,2:T(8,128)(2,1)S(1)} %all_gather.11) | data formatting | bytes 1310720 | tf_op jit(solution)/shard_map/all_gather | solution.py:182
  129.4 2.9 %reshape.341 = bf16[64,5120]{1,0:T(8,128)(2,1)} reshape(bf16[64,64,80]{2,1,0:T(8,128)(2,1)S(1)} %copy.105) | data formatting | bytes 1310720 | tf_op jit(solution)/shard_map/reshape | solution.py:183
  (48 shorter events, 2.7 us)
Async XLA Ops:
  6.5 48.7 %copy-start = (bf16[16,128,128]{2,1,0:T(8,128)(2,1)S(1)}, bf16[16,128,128]{2,1,0:T(8,128)(2,1)}, u32[]{:S(2)}) copy-start(bf16[16,128,128]{2,1,0:T(8,128)(2,1)} %param.11) | copy-start | bytes 1572868
  6.5 43.3 %copy-start.2 = (bf16[64,128]{1,0:T(8,128)(2,1)S(1)}, bf16[64,128]{1,0:T(8,128)(2,1)}, u32[]{:S(2)}) copy-start(bf16[64,128]{1,0:T(8,128)(2,1)} %param.9) | copy-start | bytes 49156
  6.5 43.5 %copy-start.3 = (bf16[64,128]{1,0:T(8,128)(2,1)S(1)}, bf16[64,128]{1,0:T(8,128)(2,1)}, u32[]{:S(2)}) copy-start(bf16[64,128]{1,0:T(8,128)(2,1)} %param.10) | copy-start | bytes 49156
  6.5 88.6 %all-gather.2.cloned.1.call-start = ((), (), s32[]{:S(2)}) async-start(), calls=%async_computation.1 | async-start | bytes 6963200 | tf_op jit(solution)/shard_map/all_gather | solution.py:65
  50.5 4.3 %collective-permute-start = (bf16[64,7,128]{2,1,0:T(8,128)(2,1)S(1)}, bf16[64,7,128]{2,1,0:T(8,128)(2,1)S(1)}, u32[]{:S(2)}, u32[]{:S(2)}) collective-permute-start(bf16[64,7,128]{2,1,0:T(8,128)(2,1)S(1)} %pad_maximum_fusion.1), channel_id=1, source_target_pairs={{0,8},{8,0},{1,9},{9,1},{2,10},{10,2},{3,11},{11,3},{4,12},{12,4},... | collective-permute-start | bytes 344072 | tf_op jit(solution)/shard_map/ppermute | solution.py:19
  55.2 5.6 %copy-start.4 = (bf16[16,128,128]{2,1,0:T(8,128)(2,1)S(1)}, bf16[16,128,128]{2,1,0:T(8,128)(2,1)}, u32[]{:S(2)}) copy-start(bf16[16,128,128]{2,1,0:T(8,128)(2,1)} %param.12) | copy-start | bytes 1572868
  56.3 2.4 %copy-start.1 = (f32[128,5,2048]{2,0,1:T(8,128)}, f32[128,5,2048]{2,0,1:T(8,128)S(1)}, u32[]{:S(2)}) copy-start(f32[128,5,2048]{2,0,1:T(8,128)S(1)} %get-tuple-element.30) | copy-start | bytes 15728644
  64.8 3.4 %collective-permute-start.1 = (bf16[64,1,5,130]{3,0,2,1:T(8,128)(2,1)S(1)}, bf16[64,1,5,130]{3,0,2,1:T(8,128)(2,1)S(1)}, u32[]{:S(2)}, u32[]{:S(2)}) collective-permute-start(bf16[64,1,5,130]{3,0,2,1:T(8,128)(2,1)S(1)} %pad_maximum_fusion), channel_id=1, source_target_pairs={{0,8},{8,0},{1,9},{9,1},{2,10},{10,2},{3,11},{11,3},{4,12},{12,4},... | collective-permute-start | bytes 249608 | tf_op jit(solution)/shard_map/ppermute | solution.py:19
Sparse Core Ops, SparseCore 0:
  46.0 44.6 all-gather.1

commit v12 on v10

--- a/solution.py
+++ b/solution.py
@@ -56,8 +56,18 @@
     rows, width = w_out.shape
     share = rows // parts
     pieces = lax.all_to_all(w_out.reshape(parts, share, width), "tp", 0, 0, tiled=True)
-    mine = jnp.transpose(pieces, (1, 0, 2))
-    near = lax.all_gather(mine, "z", axis=0, tiled=True)
+    near = jnp.transpose(pieces, (1, 0, 2))
+    depth = lax.axis_size("z")
+    place = lax.axis_index("z")
+    step = 1
+    while step < depth:
+        other = lax.ppermute(near, "z", [(i, i ^ step) for i in range(depth)])
+        near = jnp.where(
+            (place & step) == 0,
+            jnp.concatenate([near, other], axis=0),
+            jnp.concatenate([other, near], axis=0),
+        )
+        step *= 2
     return lax.all_gather(near, ("x", "core"), axis=0, tiled=True), share
 
 

time: 140 us -> 151 us (1.079)
  blocking collectives: 90.4 us -> 70.8 us
  starting transfers between devices: 4.31 us -> 19.7 us
  waiting for transfers between devices: 1.02 us -> 15.1 us
    all_gather x1 -> x0, blocking collectives: 20.9 us -> none  [output_rows(): near = lax.all_gather(mine, 'z', axis=0, tiled=True)]
    ppermute x0 -> x2, starting transfers between devices: none -> 15.4 us  [output_rows(): other = lax.ppermute(near, 'z', [(i, i ^ step) for i in range(depth)])]
    ppermute x0 -> x2, waiting for transfers between devices: none -> 14.1 us  [output_rows(): other = lax.ppermute(near, 'z', [(i, i ^ step) for i in range(depth)])]
  transfers between devices with their start and end apart: 3 -> 5, of which waited for: 1 -> 3; matrix products, arithmetic and copies ran while one was open for 11% -> 10% of each run, Pallas kernels for 0% -> 0%
where the time goes in v12:
time: 151 us; the launch traced here: 150 us
  blocking collectives  70.8 us (47%)
  starting transfers between devices  19.7 us (13%)
  waiting for transfers between devices  15.1 us (10%)
  between operations  15 us (10%)
  local copies, waits for them, and re-layouts  12 us (8%)
  matrix products  10.4 us (7%)
  other arithmetic  6.92 us (5%)
    all_gather x1, blocking collectives, shards(): gathered = lax.all_gather(projected, 'tp', axis=2, tiled=True)  27.3 us
    all_gather x1, blocking collectives, shards(): full_rows = lax.all_gather(attention[:, None], 'tp', axis=1, tiled=True)  26.9 us
    all_to_all x1, blocking collectives, output_rows(): lax.all_to_all(w_out.reshape(parts, share, width), 'tp', 0, 0, tiled=True)  16.7 us
    ppermute x2, starting transfers between devices, output_rows(): other = lax.ppermute(near, 'z', [(i, i ^ step) for i in range(depth)])  15.4 us
    ppermute x2, waiting for transfers between devices, output_rows(): other = lax.ppermute(near, 'z', [(i, i ^ step) for i in range(depth)])  14.1 us
    dot_general x1, matrix products, shards(): lax.dot_general(full_rows, weights_mine, (((1, 2), (1, 2)), ((), ())), pr...  4.94 us
    ppermute x2, starting transfers between devices, from_partner(): lax.ppermute(value, axis, [(i, i ^ 1 << distance) for i in range(lax.axis...  4.32 us
    dot_general x2, matrix products, absorb(): jnp.einsum('cgqk,kcd->qcgd', weights.astype(jnp.bfloat16), block_values,...  4.2 us
  transfers between devices with their start and end apart: 5, of which 3 were waited for; matrix products, arithmetic and copies ran while one was open for 10% of the time, Pallas kernels for 0%

profile of v12, /device:TPU:6, one launch (start us, length us, event | category | flops | bytes accessed | tf_op | source)
XLA Modules:
  0.0 150.0 jit_solution(303925151527423309)
XLA Ops:
  6.5 1.0 reshape.330
  7.5 16.7 %all_to_all.5 = bf16[8,10,640]{2,1,0:T(8,128)(2,1)S(1)} all-to-all(bf16[8,10,640]{2,1,0:T(8,128)(2,1)S(1)} %reshape.330), channel_id=1, replica_groups=mesh['z'=4,'x'=8,'core'=2,'tp'=8] {'tp'}, dimensions={0} | all-to-all | bytes 204800 | tf_op jit(solution)/shard_map/all_to_all | solution.py:58
  24.2 6.1 %collective-permute-start.2 = (bf16[10,8,640]{2,0,1:T(8,128)(2,1)S(1)}, bf16[10,8,640]{2,0,1:T(8,128)(2,1)S(1)}, u32[]{:S(2)}, u32[]{:S(2)}) collective-permute-start(bf16[10,8,640]{2,0,1:T(8,128)(2,1)S(1)} %bitcast.208), channel_id=1, source_target_pairs={{0,128},{128,0},{256,384},{384,256},{1,129},{129,1},{257,385},{385... | collective-permute-start | bytes 307208 | tf_op jit(solution)/shard_map/ppermute | solution.py:64
  30.3 5.8 %collective-permute-done.2 = bf16[10,8,640]{2,0,1:T(8,128)(2,1)S(1)} collective-permute-done((bf16[10,8,640]{2,0,1:T(8,128)(2,1)S(1)}, bf16[10,8,640]{2,0,1:T(8,128)(2,1)S(1)}, u32[]{:S(2)}, u32[]{:S(2)}) %collective-permute-start.2) | collective-permute-done | bytes 102432 | tf_op jit(solution)/shard_map/ppermute | solution.py:64
  36.3 9.3 %collective-permute-start.3 = (bf16[20,8,640]{2,0,1:T(8,128)(2,1)S(1)}, bf16[20,8,640]{2,0,1:T(8,128)(2,1)S(1)}, u32[]{:S(2)}, u32[]{:S(2)}) collective-permute-start(bf16[20,8,640]{2,0,1:T(8,128)(2,1)S(1)} %maximum_select_fusion.2), channel_id=1, source_target_pairs={{0,256},{128,384},{256,0},{384,128},{1,257},{129,385},{257,1},{385... | collective-permute-start | bytes 614408 | tf_op jit(solution)/shard_map/ppermute | solution.py:64
  45.6 8.3 %collective-permute-done.3 = bf16[20,8,640]{2,0,1:T(8,128)(2,1)S(1)} collective-permute-done((bf16[20,8,640]{2,0,1:T(8,128)(2,1)S(1)}, bf16[20,8,640]{2,0,1:T(8,128)(2,1)S(1)}, u32[]{:S(2)}, u32[]{:S(2)}) %collective-permute-start.3) | collective-permute-done | bytes 204832 | tf_op jit(solution)/shard_map/ppermute | solution.py:64
  53.9 0.9 maximum_select_fusion
  54.9 1.0 reshape.332
  55.9 1.3 dynamic_slice.24
  57.8 0.7 convert_bitcast_fusion
  58.8 0.8 pad_maximum_fusion.2
  59.7 0.7 copy.75
  60.8 1.9 %collective-permute-start = (bf16[64,7,128]{2,1,0:T(8,128)(2,1)S(1)}, bf16[64,7,128]{2,1,0:T(8,128)(2,1)S(1)}, u32[]{:S(2)}, u32[]{:S(2)}) collective-permute-start(bf16[64,7,128]{2,1,0:T(8,128)(2,1)S(1)} %pad_maximum_fusion.1), channel_id=1, source_target_pairs={{0,8},{8,0},{1,9},{9,1},{2,10},{10,2},{3,11},{11,3},{4,12},{12,4},... | collective-permute-start | bytes 344072 | tf_op jit(solution)/shard_map/ppermute | solution.py:19
  65.6 1.0 fusion.1
  66.8 2.3 %copy-done.1 = f32[128,5,2048]{2,0,1:T(8,128)} copy-done((f32[128,5,2048]{2,0,1:T(8,128)}, f32[128,5,2048]{2,0,1:T(8,128)S(1)}, u32[]{:S(2)}) %copy-start.1) | copy-done | bytes 5242904
  69.0 1.3 fusion.2
  71.2 3.9 %fusion.13 = f32[128,1,5,128]{3,0,2,1:T(8,128)S(1)} fusion(f32[128,1,5,128]{3,0,2,1:T(8,128)S(1)} %fusion.17, bf16[2048,128,1]{1,0,2:T(8,128)(2,1)S(1)} %bitcast.213, f32[128,5,2048]{2,0,1:T(8,128)} %copy-done.1, f32[5,128]{1,0:T(8,128)S(1)} %get-tuple-element.24, pred[2048]{0:T(1024)(128)(4,1)S(1)} %fusion.59), kind=kOutput, calls=%fused_computation.14 | convolution fusion | flops 342179840 | bytes 6427136 | tf_op jit(solution)/shard_map/cgqk,kcd->qcgd/dot_general | solution.py:44
  75.2 2.4 %collective-permute-start.1 = (bf16[64,1,5,130]{3,0,2,1:T(8,128)(2,1)S(1)}, bf16[64,1,5,130]{3,0,2,1:T(8,128)(2,1)S(1)}, u32[]{:S(2)}, u32[]{:S(2)}) collective-permute-start(bf16[64,1,5,130]{3,0,2,1:T(8,128)(2,1)S(1)} %pad_maximum_fusion), channel_id=1, source_target_pairs={{0,8},{8,0},{1,9},{9,1},{2,10},{10,2},{3,11},{11,3},{4,12},{12,4},... | collective-permute-start | bytes 249608 | tf_op jit(solution)/shard_map/ppermute | solution.py:19
  77.6 1.0 collective-permute-done.1
  79.2 26.9 %all_gather.9 = bf16[64,8,640]{2,0,1:T(8,128)(2,1)S(1)} all-gather(bf16[64,1,640]{2,0,1:T(8,128)(2,1)S(1)} %copy_bitcast_fusion), channel_id=1, replica_groups=mesh['z'=4,'x'=8,'core'=2,'tp'=8] {'tp'}, dimensions={1}, use_global_device_ids=true | all-gather | bytes 737280 | tf_op jit(solution)/shard_map/all_gather | solution.py:177
  106.0 4.9 %fusion.19 = bf16[64,640]{1,0:T(8,128)(2,1)S(1)} fusion(bf16[64,8,640]{2,0,1:T(8,128)(2,1)S(1)} %all_gather.9, bf16[640,8,640]{2,0,1:T(8,128)(2,1)} %all-gather.2.cloned.1.call-done), kind=kOutput, calls=%fused_computation.19 | convolution fusion | flops 419471360 | bytes 7290880 | tf_op jit(solution)/shard_map/dot_general | solution.py:178
  111.5 27.3 %all_gather.11 = bf16[64,64,80]{1,0,2:T(8,128)(2,1)S(1)} all-gather(bf16[64,64,10]{1,0,2:T(8,128)(2,1)S(1)} %copy.86), channel_id=1, replica_groups=mesh['z'=4,'x'=8,'core'=2,'tp'=8] {'tp'}, dimensions={2}, use_global_device_ids=true | all-gather | bytes 737280 | tf_op jit(solution)/shard_map/all_gather | solution.py:188
  138.8 1.5 copy.87
  140.3 2.9 %reshape.331 = bf16[64,5120]{1,0:T(8,128)(2,1)} reshape(bf16[64,64,80]{2,1,0:T(8,128)(2,1)S(1)} %copy.87) | data formatting | bytes 1310720 | tf_op jit(solution)/shard_map/reshape | solution.py:189
  (49 shorter events, 5.0 us)
Async XLA Ops:
  6.5 59.1 %copy-start = (bf16[16,128,128]{2,1,0:T(8,128)(2,1)S(1)}, bf16[16,128,128]{2,1,0:T(8,128)(2,1)}, u32[]{:S(2)}) copy-start(bf16[16,128,128]{2,1,0:T(8,128)(2,1)} %param.11) | copy-start | bytes 1572868
  6.5 99.5 %all-gather.2.cloned.1.call-start = ((), (), s32[]{:S(2)}) async-start(), calls=%async_computation.1 | async-start | bytes 6963200 | tf_op jit(solution)/shard_map/all_gather | solution.py:71
  24.2 11.9 %collective-permute-start.2 = (bf16[10,8,640]{2,0,1:T(8,128)(2,1)S(1)}, bf16[10,8,640]{2,0,1:T(8,128)(2,1)S(1)}, u32[]{:S(2)}, u32[]{:S(2)}) collective-permute-start(bf16[10,8,640]{2,0,1:T(8,128)(2,1)S(1)} %bitcast.208), channel_id=1, source_target_pairs={{0,128},{128,0},{256,384},{384,256},{1,129},{129,1},{257,385},{385... | collective-permute-start | bytes 307208 | tf_op jit(solution)/shard_map/ppermute | solution.py:64
  36.3 17.6 %collective-permute-start.3 = (bf16[20,8,640]{2,0,1:T(8,128)(2,1)S(1)}, bf16[20,8,640]{2,0,1:T(8,128)(2,1)S(1)}, u32[]{:S(2)}, u32[]{:S(2)}) collective-permute-start(bf16[20,8,640]{2,0,1:T(8,128)(2,1)S(1)} %maximum_select_fusion.2), channel_id=1, source_target_pairs={{0,256},{128,384},{256,0},{384,128},{1,257},{129,385},{257,1},{385... | collective-permute-start | bytes 614408 | tf_op jit(solution)/shard_map/ppermute | solution.py:64
  60.8 4.3 %collective-permute-start = (bf16[64,7,128]{2,1,0:T(8,128)(2,1)S(1)}, bf16[64,7,128]{2,1,0:T(8,128)(2,1)S(1)}, u32[]{:S(2)}, u32[]{:S(2)}) collective-permute-start(bf16[64,7,128]{2,1,0:T(8,128)(2,1)S(1)} %pad_maximum_fusion.1), channel_id=1, source_target_pairs={{0,8},{8,0},{1,9},{9,1},{2,10},{10,2},{3,11},{11,3},{4,12},{12,4},... | collective-permute-start | bytes 344072 | tf_op jit(solution)/shard_map/ppermute | solution.py:19
  65.6 5.2 %copy-start.2 = (bf16[64,128]{1,0:T(8,128)(2,1)S(1)}, bf16[64,128]{1,0:T(8,128)(2,1)}, u32[]{:S(2)}) copy-start(bf16[64,128]{1,0:T(8,128)(2,1)} %param.10) | copy-start | bytes 49156
  65.6 5.6 %copy-start.3 = (bf16[16,128,128]{2,1,0:T(8,128)(2,1)S(1)}, bf16[16,128,128]{2,1,0:T(8,128)(2,1)}, u32[]{:S(2)}) copy-start(bf16[16,128,128]{2,1,0:T(8,128)(2,1)} %param.12) | copy-start | bytes 1572868
  66.7 2.4 %copy-start.1 = (f32[128,5,2048]{2,0,1:T(8,128)}, f32[128,5,2048]{2,0,1:T(8,128)S(1)}, u32[]{:S(2)}) copy-start(f32[128,5,2048]{2,0,1:T(8,128)S(1)} %get-tuple-element.30) | copy-start | bytes 15728644
  75.2 3.4 %collective-permute-start.1 = (bf16[64,1,5,130]{3,0,2,1:T(8,128)(2,1)S(1)}, bf16[64,1,5,130]{3,0,2,1:T(8,128)(2,1)S(1)}, u32[]{:S(2)}, u32[]{:S(2)}) collective-permute-start(bf16[64,1,5,130]{3,0,2,1:T(8,128)(2,1)S(1)} %pad_maximum_fusion), channel_id=1, source_target_pairs={{0,8},{8,0},{1,9},{9,1},{2,10},{10,2},{3,11},{11,3},{4,12},{12,4},... | collective-permute-start | bytes 249608 | tf_op jit(solution)/shard_map/ppermute | solution.py:19
Sparse Core Ops, SparseCore 0:
  55.0 46.7 all-gather.1

commit v13 on v11

--- a/solution.py
+++ b/solution.py
@@ -130,9 +130,17 @@
     allowed = jnp.broadcast_to(usable[None, :], (all_rows, pages_local * page_rows))
     pool_keys = k_cache.reshape(pages_local * page_rows, local_heads, HD)
     pool_values = v_cache.reshape(pages_local * page_rows, local_heads, HD)
-    running_max, running_sum, output = absorb(
-        state, queries, pool_keys, pool_values, allowed, scale
-    )
+    half = pool_keys.shape[0] // 2
+    for start in (0, half):
+        state = absorb(
+            state,
+            queries,
+            pool_keys[start : start + half],
+            pool_values[start : start + half],
+            allowed[:, start : start + half],
+            scale,
+        )
+    running_max, running_sum, output = state
     peer_start = (1 - parity) * own_rows
     own_start = parity * own_rows
     outgoing = (

time: 140 us -> 137 us (0.979)
  local copies, waits for them, and re-layouts: 12.2 us -> 9.2 us
    unnamed x11 -> x17, local copies, waits for them, and re-layouts: 2.31 us -> 0.05 us
    dot_general x2 -> x3, matrix products: 4.16 us -> 3.5 us  [absorb(): jnp.einsum('cgqk,kcd->qcgd', weights.astype(jnp.bfloat16), block_values,...]
  transfers between devices with their start and end apart: 3 -> 3, of which waited for: 1 -> 1; matrix products, arithmetic and copies ran while one was open for 10% -> 9% of each run, Pallas kernels for 0% -> 0%
where the time goes in v13:
time: 137 us; the launch traced here: 136 us
  blocking collectives  91.9 us (67%)
  between operations  15.1 us (11%)
  matrix products  9.92 us (7%)
  local copies, waits for them, and re-layouts  9.2 us (7%)
  other arithmetic  4.56 us (3%)
  starting transfers between devices  4.32 us (3%)
    all_to_all x1, blocking collectives, output_rows(): lax.all_to_all(chunks.reshape(depth * parts, share, width), ('z', 'tp'),...  37.4 us
    all_gather x1, blocking collectives, shards(): gathered = lax.all_gather(projected, 'tp', axis=2, tiled=True)  28.2 us
    all_gather x1, blocking collectives, shards(): full_rows = lax.all_gather(attention[:, None], 'tp', axis=1, tiled=True)  26.4 us
    dot_general x1, matrix products, shards(): lax.dot_general(full_rows, weights_mine, (((1, 2), (1, 2)), ((), ())), pr...  4.94 us
    ppermute x2, starting transfers between devices, from_partner(): lax.ppermute(value, axis, [(i, i ^ 1 << distance) for i in range(lax.axis...  4.32 us
    dot_general x3, matrix products, absorb(): jnp.einsum('cgqk,kcd->qcgd', weights.astype(jnp.bfloat16), block_values,...  3.5 us
    reshape x1, local copies, waits for them, and re-layouts, shards(): return gathered.reshape(own_rows, -1)  2.92 us
  transfers between devices with their start and end apart: 3, of which 1 were waited for; matrix products, arithmetic and copies ran while one was open for 9% of the time, Pallas kernels for 0%

profile of v13, /device:TPU:6, one launch (start us, length us, event | category | flops | bytes accessed | tf_op | source)
XLA Modules:
  0.0 136.1 jit_solution(15970826253711002472)
XLA Ops:
  6.5 1.0 broadcast_in_dim.133
  7.6 37.4 %all_to_all.5 = bf16[32,10,640]{2,1,0:T(8,128)(2,1)S(1)} all-to-all(bf16[32,10,640]{2,1,0:T(8,128)(2,1)S(1)} %bitcast.308), channel_id=1, replica_groups=mesh['z'=4,'x'=8,'core'=2,'tp'=8] {'z','tp'}, dimensions={0} | all-to-all | bytes 819200 | tf_op jit(solution)/shard_map/all_to_all | solution.py:60
  45.1 0.8 copy.107
  46.1 0.6 dynamic_slice.24
  48.2 1.9 %collective-permute-start = (bf16[64,7,128]{2,1,0:T(8,128)(2,1)S(1)}, bf16[64,7,128]{2,1,0:T(8,128)(2,1)S(1)}, u32[]{:S(2)}, u32[]{:S(2)}) collective-permute-start(bf16[64,7,128]{2,1,0:T(8,128)(2,1)S(1)} %pad_maximum_fusion.1), channel_id=1, source_target_pairs={{0,8},{8,0},{1,9},{9,1},{2,10},{10,2},{3,11},{11,3},{4,12},{12,4},... | collective-permute-start | bytes 344072 | tf_op jit(solution)/shard_map/ppermute | solution.py:19
  50.9 0.7 fusion.97
  51.8 0.7 fusion.79
  52.6 0.8 fusion.110
  53.7 0.2 fusion.113
  53.9 0.6 fusion.2
  54.5 0.6 fusion.3
  55.3 1.5 %fusion.4 = (f32[5,128]{1,0:T(8,128)S(1)}, f32[5,128]{1,0:T(8,128)S(1)}) fusion(f32[128,5,1024]{2,0,1:T(8,128)S(1)} %get-tuple-element.38, f32[5,128]{1,0:T(8,128)S(1)} %get-tuple-element.10, pred[1024]{0:T(1024)(128)(4,1)S(1)} %get-tuple-element.8, f32[5,128]{1,0:T(8,128)S(1)} %get-tuple-element.9, f32[128,5,1024]{2,0,1:T(8,128)S(1)} %get-tuple-element.36, ...), kind=kLoop, calls=%fused_computation.8 | loop fusion | flops 6552320 | bytes 5255168 | tf_op jit(solution)/shard_map/reduce_sum | solution.py:43
  57.2 0.3 fusion.35
  57.5 2.5 %fusion.31 = f32[128,1,5,128]{3,0,2,1:T(8,128)S(1)} fusion(f32[128,1,5,128]{3,0,2,1:T(8,128)S(1)} %fusion.35, bf16[1024,128,1]{1,0,2:T(8,128)(2,1)} %bitcast.317, f32[128,5,1024]{2,0,1:T(8,128)} %copy-done, f32[5,128]{1,0:T(8,128)S(1)} %get-tuple-element.10, pred[1024]{0:T(1024)(128)(4,1)S(1)} %get-tuple-element.8, f32[128,5]{0,1:T(8,128)S(1)} %get-tuple-element.24), kind=kOutput, calls=%fused_computation.27 | convolution fusion | flops 171212800 | bytes 3545088 | tf_op jit(solution)/shard_map/cgqk,kcd->qcgd/dot_general | solution.py:44
  60.0 0.7 fusion.28
  60.9 2.4 %collective-permute-start.1 = (bf16[64,1,5,130]{3,0,2,1:T(8,128)(2,1)S(1)}, bf16[64,1,5,130]{3,0,2,1:T(8,128)(2,1)S(1)}, u32[]{:S(2)}, u32[]{:S(2)}) collective-permute-start(bf16[64,1,5,130]{3,0,2,1:T(8,128)(2,1)S(1)} %pad_maximum_fusion), channel_id=1, source_target_pairs={{0,8},{8,0},{1,9},{9,1},{2,10},{10,2},{3,11},{11,3},{4,12},{12,4},... | collective-permute-start | bytes 249608 | tf_op jit(solution)/shard_map/ppermute | solution.py:19
  63.3 1.0 collective-permute-done.1
  64.3 0.2 slice_reduce_fusion.1
  64.6 0.2 copy_bitcast_fusion
  64.8 26.4 %all_gather.9 = bf16[64,8,640]{2,0,1:T(8,128)(2,1)S(1)} all-gather(bf16[64,1,640]{2,0,1:T(8,128)(2,1)S(1)} %copy_bitcast_fusion), channel_id=1, replica_groups=mesh['z'=4,'x'=8,'core'=2,'tp'=8] {'tp'}, dimensions={1}, use_global_device_ids=true | all-gather | bytes 737280 | tf_op jit(solution)/shard_map/all_gather | solution.py:179
  91.2 4.9 %fusion.37 = bf16[64,640]{1,0:T(8,128)(2,1)S(1)} fusion(bf16[64,8,640]{2,0,1:T(8,128)(2,1)S(1)} %all_gather.9, bf16[640,8,640]{2,0,1:T(8,128)(2,1)} %all-gather.2.cloned.1.call-done), kind=kOutput, calls=%fused_computation.32 | convolution fusion | flops 419471360 | bytes 7290880 | tf_op jit(solution)/shard_map/dot_general | solution.py:180
  96.7 28.2 %all_gather.11 = bf16[64,64,80]{1,0,2:T(8,128)(2,1)S(1)} all-gather(bf16[64,64,10]{1,0,2:T(8,128)(2,1)S(1)} %copy.110), channel_id=1, replica_groups=mesh['z'=4,'x'=8,'core'=2,'tp'=8] {'tp'}, dimensions={2}, use_global_device_ids=true | all-gather | bytes 737280 | tf_op jit(solution)/shard_map/all_gather | solution.py:190
  124.8 1.5 %copy.111 = bf16[64,64,80]{2,1,0:T(8,128)(2,1)S(1)} copy(bf16[64,64,80]{1,0,2:T(8,128)(2,1)S(1)} %all_gather.11) | data formatting | bytes 1310720 | tf_op jit(solution)/shard_map/all_gather | solution.py:190
  126.3 2.9 %reshape.463 = bf16[64,5120]{1,0:T(8,128)(2,1)} reshape(bf16[64,64,80]{2,1,0:T(8,128)(2,1)S(1)} %copy.111) | data formatting | bytes 1310720 | tf_op jit(solution)/shard_map/reshape | solution.py:191
  (59 shorter events, 2.9 us)
Async XLA Ops:
  6.5 39.4 %copy-start.3 = (bf16[64,640]{1,0:T(8,128)(2,1)S(1)}, bf16[64,640]{1,0:T(8,128)(2,1)}, u32[]{:S(2)}) copy-start(bf16[64,640]{1,0:T(8,128)(2,1)} %param.8) | copy-start | bytes 245764
  6.5 39.5 %copy-start.6 = (s32[32]{0:T(128)S(1)}, s32[32]{0:T(128)}, u32[]{:S(2)}) copy-start(s32[32]{0:T(128)} %param.13) | copy-start | bytes 388
  6.5 40.8 %copy-start.4 = (bf16[64,128]{1,0:T(8,128)(2,1)S(1)}, bf16[64,128]{1,0:T(8,128)(2,1)}, u32[]{:S(2)}) copy-start(bf16[64,128]{1,0:T(8,128)(2,1)} %param.9) | copy-start | bytes 49156
  6.5 84.6 %all-gather.2.cloned.1.call-start = ((), (), s32[]{:S(2)}) async-start(), calls=%async_computation.1 | async-start | bytes 6963200 | tf_op jit(solution)/shard_map/all_gather | solution.py:65
  7.5 40.3 %copy-start.5 = (bf16[64,128]{1,0:T(8,128)(2,1)S(1)}, bf16[64,128]{1,0:T(8,128)(2,1)}, u32[]{:S(2)}) copy-start(bf16[64,128]{1,0:T(8,128)(2,1)} %param.10) | copy-start | bytes 49156
  45.0 7.5 %copy-start.1 = (bf16[16,128,128]{2,1,0:T(8,128)(2,1)S(1)}, bf16[16,128,128]{2,1,0:T(8,128)(2,1)}, u32[]{:S(2)}) copy-start(bf16[16,128,128]{2,1,0:T(8,128)(2,1)} %param.11) | copy-start | bytes 1572868
  45.9 6.7 %copy-start.2 = (bf16[16,128,128]{2,1,0:T(8,128)(2,1)S(1)}, bf16[16,128,128]{2,1,0:T(8,128)(2,1)}, u32[]{:S(2)}) copy-start(bf16[16,128,128]{2,1,0:T(8,128)(2,1)} %param.12) | copy-start | bytes 1572868
  48.2 5.2 %collective-permute-start = (bf16[64,7,128]{2,1,0:T(8,128)(2,1)S(1)}, bf16[64,7,128]{2,1,0:T(8,128)(2,1)S(1)}, u32[]{:S(2)}, u32[]{:S(2)}) collective-permute-start(bf16[64,7,128]{2,1,0:T(8,128)(2,1)S(1)} %pad_maximum_fusion.1), channel_id=1, source_target_pairs={{0,8},{8,0},{1,9},{9,1},{2,10},{10,2},{3,11},{11,3},{4,12},{12,4},... | collective-permute-start | bytes 344072 | tf_op jit(solution)/shard_map/ppermute | solution.py:19
  54.5 2.2 %copy-start = (f32[128,5,1024]{2,0,1:T(8,128)}, f32[128,5,1024]{2,0,1:T(8,128)S(1)}, u32[]{:S(2)}) copy-start(f32[128,5,1024]{2,0,1:T(8,128)S(1)} %get-tuple-element.38) | copy-start | bytes 7864324
  60.9 3.4 %collective-permute-start.1 = (bf16[64,1,5,130]{3,0,2,1:T(8,128)(2,1)S(1)}, bf16[64,1,5,130]{3,0,2,1:T(8,128)(2,1)S(1)}, u32[]{:S(2)}, u32[]{:S(2)}) collective-permute-start(bf16[64,1,5,130]{3,0,2,1:T(8,128)(2,1)S(1)} %pad_maximum_fusion), channel_id=1, source_target_pairs={{0,8},{8,0},{1,9},{9,1},{2,10},{10,2},{3,11},{11,3},{4,12},{12,4},... | collective-permute-start | bytes 249608 | tf_op jit(solution)/shard_map/ppermute | solution.py:19
Sparse Core Ops, SparseCore 0:
  46.0 44.6 all-gather.1

commit v14 on v13

--- a/solution.py
+++ b/solution.py
@@ -130,8 +130,8 @@
     allowed = jnp.broadcast_to(usable[None, :], (all_rows, pages_local * page_rows))
     pool_keys = k_cache.reshape(pages_local * page_rows, local_heads, HD)
     pool_values = v_cache.reshape(pages_local * page_rows, local_heads, HD)
-    half = pool_keys.shape[0] // 2
-    for start in (0, half):
+    half = pool_keys.shape[0] // 4
+    for start in range(0, pool_keys.shape[0], half):
         state = absorb(
             state,
             queries,

time: 137 us -> 144 us (1.051)
  local copies, waits for them, and re-layouts: 9.2 us -> 14.7 us
    convert_element_type x2, local copies, waits for them, and re-layouts: 0.22 us -> 2.69 us  [shards(): jnp.transpose(outgoing[2], (2, 0, 1))[..., None].astype(jnp.bfloat16)]
    unnamed x17 -> x81, local copies, waits for them, and re-layouts: 0.05 us -> 1.82 us
    dot_general x3 -> x5, matrix products: 3.5 us -> 3.6 us  [absorb(): jnp.einsum('cgqk,kcd->qcgd', weights.astype(jnp.bfloat16), block_values,...]
  transfers between devices with their start and end apart: 3 -> 3, of which waited for: 1 -> 1; matrix products, arithmetic and copies ran while one was open for 9% -> 13% of each run, Pallas kernels for 0% -> 0%
where the time goes in v14:
time: 144 us; the launch traced here: 143 us
  blocking collectives  91.3 us (63%)
  between operations  15.6 us (11%)
  local copies, waits for them, and re-layouts  14.7 us (10%)
  matrix products  10.4 us (7%)
  other arithmetic  5.89 us (4%)
  starting transfers between devices  4.31 us (3%)
    all_to_all x1, blocking collectives, output_rows(): lax.all_to_all(chunks.reshape(depth * parts, share, width), ('z', 'tp'),...  37.4 us
    all_gather x1, blocking collectives, shards(): gathered = lax.all_gather(projected, 'tp', axis=2, tiled=True)  27.5 us
    all_gather x1, blocking collectives, shards(): full_rows = lax.all_gather(attention[:, None], 'tp', axis=1, tiled=True)  26.4 us
    dot_general x1, matrix products, shards(): lax.dot_general(full_rows, weights_mine, (((1, 2), (1, 2)), ((), ())), pr...  4.94 us
    ppermute x2, starting transfers between devices, from_partner(): lax.ppermute(value, axis, [(i, i ^ 1 << distance) for i in range(lax.axis...  4.31 us
    dot_general x5, matrix products, absorb(): jnp.einsum('cgqk,kcd->qcgd', weights.astype(jnp.bfloat16), block_values,...  3.6 us
    reshape x1, local copies, waits for them, and re-layouts, shards(): return gathered.reshape(own_rows, -1)  2.92 us
  transfers between devices with their start and end apart: 3, of which 1 were waited for; matrix products, arithmetic and copies ran while one was open for 13% of the time, Pallas kernels for 0%

profile of v14, /device:TPU:6, one launch (start us, length us, event | category | flops | bytes accessed | tf_op | source)
XLA Modules:
  0.0 143.2 jit_solution(5364515921372529161)
XLA Ops:
  6.5 0.9 broadcast_in_dim.169
  7.5 37.4 %all_to_all.5 = bf16[32,10,640]{2,1,0:T(8,128)(2,1)S(1)} all-to-all(bf16[32,10,640]{2,1,0:T(8,128)(2,1)S(1)} %bitcast.379), channel_id=1, replica_groups=mesh['z'=4,'x'=8,'core'=2,'tp'=8] {'z','tp'}, dimensions={0} | all-to-all | bytes 819200 | tf_op jit(solution)/shard_map/all_to_all | solution.py:60
  45.0 0.8 copy.119
  46.0 0.7 dynamic_slice.24
  48.3 1.9 %collective-permute-start = (bf16[64,7,128]{2,1,0:T(8,128)(2,1)S(1)}, bf16[64,7,128]{2,1,0:T(8,128)(2,1)S(1)}, u32[]{:S(2)}, u32[]{:S(2)}) collective-permute-start(bf16[64,7,128]{2,1,0:T(8,128)(2,1)S(1)} %pad_maximum_fusion.1), channel_id=1, source_target_pairs={{0,8},{8,0},{1,9},{9,1},{2,10},{10,2},{3,11},{11,3},{4,12},{12,4},... | collective-permute-start | bytes 344072 | tf_op jit(solution)/shard_map/ppermute | solution.py:19
  51.0 0.7 fusion.114
  52.0 0.8 fusion.92
  52.8 0.7 fusion.125
  56.5 0.6 fusion.110
  57.1 0.8 fusion.28
  58.0 0.7 fusion.32
  58.8 0.6 fusion.109
  60.0 0.7 fusion.105
  60.6 0.8 copy.112
  61.4 1.3 fusion.106
  62.7 1.4 copy.113
  64.2 1.8 %convolution_bitcast_fusion.3 = f32[128,1,5,128]{3,0,2,1:T(8,128)S(1)} fusion(bf16[512,128,1]{1,0,2:T(8,128)(2,1)S(1)} %bitcast.391, f32[1,512,128,5]{1,2,3,0:T(8,128)} %copy-done.2, f32[5,128]{1,0:T(8,128)} %copy-done.22, pred[512]{0:T(512)(128)(4,1)} %copy-done.37), kind=kOutput, calls=%fused_computation.31 | convolution fusion | flops 84869120 | bytes 1772544 | tf_op jit(solution)/shard_map/cgqk,kcd->qcgd/dot_general | solution.py:44
  68.6 2.4 %collective-permute-start.1 = (bf16[64,1,5,130]{3,0,2,1:T(8,128)(2,1)S(1)}, bf16[64,1,5,130]{3,0,2,1:T(8,128)(2,1)S(1)}, u32[]{:S(2)}, u32[]{:S(2)}) collective-permute-start(bf16[64,1,5,130]{3,0,2,1:T(8,128)(2,1)S(1)} %pad_maximum_fusion), channel_id=1, source_target_pairs={{0,8},{8,0},{1,9},{9,1},{2,10},{10,2},{3,11},{11,3},{4,12},{12,4},... | collective-permute-start | bytes 249608 | tf_op jit(solution)/shard_map/ppermute | solution.py:19
  71.0 1.0 collective-permute-done.1
  72.6 26.4 %all_gather.9 = bf16[64,8,640]{2,0,1:T(8,128)(2,1)S(1)} all-gather(bf16[64,1,640]{2,0,1:T(8,128)(2,1)S(1)} %copy_bitcast_fusion), channel_id=1, replica_groups=mesh['z'=4,'x'=8,'core'=2,'tp'=8] {'tp'}, dimensions={1}, use_global_device_ids=true | all-gather | bytes 737280 | tf_op jit(solution)/shard_map/all_gather | solution.py:179
  99.0 4.9 %fusion.27 = bf16[64,640]{1,0:T(8,128)(2,1)S(1)} fusion(bf16[64,8,640]{2,0,1:T(8,128)(2,1)S(1)} %all_gather.9, bf16[640,8,640]{2,0,1:T(8,128)(2,1)} %all-gather.2.cloned.1.call-done), kind=kOutput, calls=%fused_computation.46 | convolution fusion | flops 419471360 | bytes 7290880 | tf_op jit(solution)/shard_map/dot_general | solution.py:180
  104.5 27.5 %all_gather.11 = bf16[64,64,80]{1,0,2:T(8,128)(2,1)S(1)} all-gather(bf16[64,64,10]{1,0,2:T(8,128)(2,1)S(1)} %copy.122), channel_id=1, replica_groups=mesh['z'=4,'x'=8,'core'=2,'tp'=8] {'tp'}, dimensions={2}, use_global_device_ids=true | all-gather | bytes 737280 | tf_op jit(solution)/shard_map/all_gather | solution.py:190
  132.0 1.5 %copy.123 = bf16[64,64,80]{2,1,0:T(8,128)(2,1)S(1)} copy(bf16[64,64,80]{1,0,2:T(8,128)(2,1)S(1)} %all_gather.11) | data formatting | bytes 1310720 | tf_op jit(solution)/shard_map/all_gather | solution.py:190
  133.5 2.9 %reshape.659 = bf16[64,5120]{1,0:T(8,128)(2,1)} reshape(bf16[64,64,80]{2,1,0:T(8,128)(2,1)S(1)} %copy.123) | data formatting | bytes 1310720 | tf_op jit(solution)/shard_map/reshape | solution.py:191
  (130 shorter events, 8.3 us)
Async XLA Ops:
  6.5 92.5 %all-gather.2.cloned.1.call-start = ((), (), s32[]{:S(2)}) async-start(), calls=%async_computation.1 | async-start | bytes 6963200 | tf_op jit(solution)/shard_map/all_gather | solution.py:65
  44.9 2.5 %copy-start.13 = (bf16[64,128]{1,0:T(8,128)(2,1)S(1)}, bf16[64,128]{1,0:T(8,128)(2,1)}, u32[]{:S(2)}) copy-start(bf16[64,128]{1,0:T(8,128)(2,1)} %param.9) | copy-start | bytes 49156
  45.0 2.8 %copy-start.10 = (bf16[64,128]{1,0:T(8,128)(2,1)S(1)}, bf16[64,128]{1,0:T(8,128)(2,1)}, u32[]{:S(2)}) copy-start(bf16[64,128]{1,0:T(8,128)(2,1)} %param.10) | copy-start | bytes 49156
  47.8 4.9 %copy-start.3 = (bf16[16,128,128]{2,1,0:T(8,128)(2,1)S(1)}, bf16[16,128,128]{2,1,0:T(8,128)(2,1)}, u32[]{:S(2)}) copy-start(bf16[16,128,128]{2,1,0:T(8,128)(2,1)} %param.11) | copy-start | bytes 1572868
  48.0 4.7 %copy-start.4 = (bf16[16,128,128]{2,1,0:T(8,128)(2,1)S(1)}, bf16[16,128,128]{2,1,0:T(8,128)(2,1)}, u32[]{:S(2)}) copy-start(bf16[16,128,128]{2,1,0:T(8,128)(2,1)} %param.12) | copy-start | bytes 1572868
  48.3 5.3 %collective-permute-start = (bf16[64,7,128]{2,1,0:T(8,128)(2,1)S(1)}, bf16[64,7,128]{2,1,0:T(8,128)(2,1)S(1)}, u32[]{:S(2)}, u32[]{:S(2)}) collective-permute-start(bf16[64,7,128]{2,1,0:T(8,128)(2,1)S(1)} %pad_maximum_fusion.1), channel_id=1, source_target_pairs={{0,8},{8,0},{1,9},{9,1},{2,10},{10,2},{3,11},{11,3},{4,12},{12,4},... | collective-permute-start | bytes 344072 | tf_op jit(solution)/shard_map/ppermute | solution.py:19
  53.5 2.9 %copy-start.7 = (pred[128,128]{0,1:T(8,128)(4,1)}, pred[128,128]{0,1:T(8,128)(4,1)S(1)}, u32[]{:S(2)}) copy-start(pred[128,128]{0,1:T(8,128)(4,1)S(1)} %fusion.69) | copy-start | bytes 49156
  53.6 3.5 %copy-start.35 = (pred[512]{0:T(512)(128)(4,1)}, pred[512]{0:T(512)(128)(4,1)S(1)}, u32[]{:S(2)}) copy-start(pred[512]{0:T(512)(128)(4,1)S(1)} %get-tuple-element.9) | copy-start | bytes 1540
  53.6 3.5 %copy-start.37 = (pred[512]{0:T(512)(128)(4,1)}, pred[512]{0:T(512)(128)(4,1)S(1)}, u32[]{:S(2)}) copy-start(pred[512]{0:T(512)(128)(4,1)S(1)} %get-tuple-element.10) | copy-start | bytes 1540
  53.6 4.3 %copy-start.31 = (pred[512]{0:T(512)(128)(4,1)}, pred[512]{0:T(512)(128)(4,1)S(1)}, u32[]{:S(2)}) copy-start(pred[512]{0:T(512)(128)(4,1)S(1)} %get-tuple-element.8) | copy-start | bytes 1540
  53.6 4.3 %copy-start.33 = (pred[512]{0:T(512)(128)(4,1)}, pred[512]{0:T(512)(128)(4,1)S(1)}, u32[]{:S(2)}) copy-start(pred[512]{0:T(512)(128)(4,1)S(1)} %get-tuple-element.7) | copy-start | bytes 1540
  55.1 2.0 %copy-start.2 = (f32[1,512,128,5]{1,2,3,0:T(8,128)}, f32[1,512,128,5]{1,2,3,0:T(8,128)S(1)}, u32[]{:S(2)}) copy-start(f32[1,512,128,5]{1,2,3,0:T(8,128)S(1)} %get-tuple-element.53) | copy-start | bytes 3932164
  55.5 1.6 %copy-start = (f32[1,512,128,5]{1,2,3,0:T(8,128)}, f32[1,512,128,5]{1,2,3,0:T(8,128)S(1)}, u32[]{:S(2)}) copy-start(f32[1,512,128,5]{1,2,3,0:T(8,128)S(1)} %get-tuple-element.55) | copy-start | bytes 3932164
  56.4 1.5 %copy-start.14 = (f32[5,128]{1,0:T(8,128)}, f32[5,128]{1,0:T(8,128)S(1)}, u32[]{:S(2)}) copy-start(f32[5,128]{1,0:T(8,128)S(1)} %get-tuple-element.43) | copy-start | bytes 7684
  56.4 1.5 %copy-start.20 = (f32[5,128]{1,0:T(8,128)}, f32[5,128]{1,0:T(8,128)S(1)}, u32[]{:S(2)}) copy-start(f32[5,128]{1,0:T(8,128)S(1)} %get-tuple-element.15) | copy-start | bytes 7684
  56.4 1.6 %copy-start.16 = (f32[5,128]{1,0:T(8,128)}, f32[5,128]{1,0:T(8,128)S(1)}, u32[]{:S(2)}) copy-start(f32[5,128]{1,0:T(8,128)S(1)} %get-tuple-element.13) | copy-start | bytes 7684
  56.4 1.6 %copy-start.18 = (f32[5,128]{1,0:T(8,128)}, f32[5,128]{1,0:T(8,128)S(1)}, u32[]{:S(2)}) copy-start(f32[5,128]{1,0:T(8,128)S(1)} %get-tuple-element.14) | copy-start | bytes 7684
  58.0 6.2 %copy-start.5 = (bf16[4,128,128]{2,1,0:T(8,128)(2,1)S(1)}, bf16[4,128,128]{2,1,0:T(8,128)(2,1)}, u32[]{:S(2)}) copy-start(bf16[4,128,128]{2,1,0:T(8,128)(2,1)} %get-tuple-element.17) | copy-start | bytes 393220
  64.1 1.9 %copy-start.1 = (f32[1,512,128,5]{1,2,3,0:T(8,128)S(1)}, f32[1,512,128,5]{1,2,3,0:T(8,128)}, u32[]{:S(2)}) copy-start(f32[1,512,128,5]{1,2,3,0:T(8,128)} %copy-done) | copy-start | bytes 3932164
  64.1 1.9 %copy-start.21 = (f32[5,128]{1,0:T(8,128)S(1)}, f32[5,128]{1,0:T(8,128)}, u32[]{:S(2)}) copy-start(f32[5,128]{1,0:T(8,128)} %copy-done.20) | copy-start | bytes 7684
  64.1 1.9 %copy-start.36 = (pred[512]{0:T(512)(128)(4,1)S(1)}, pred[512]{0:T(512)(128)(4,1)}, u32[]{:S(2)}) copy-start(pred[512]{0:T(512)(128)(4,1)} %copy-done.35) | copy-start | bytes 1540
  67.9 4.4 %copy-start.23 = (f32[1,5,128]{2,1,0:T(8,128)S(1)}, f32[1,5,128]{2,1,0:T(8,128)}, u32[]{:S(2)}) copy-start(f32[1,5,128]{2,1,0:T(8,128)} %get-tuple-element.35) | copy-start | bytes 7684
  67.9 4.4 %copy-start.25 = (f32[1,5,128]{2,1,0:T(8,128)S(1)}, f32[1,5,128]{2,1,0:T(8,128)}, u32[]{:S(2)}) copy-start(f32[1,5,128]{2,1,0:T(8,128)} %copy-done.24) | copy-start | bytes 7684
  68.6 3.4 %collective-permute-start.1 = (bf16[64,1,5,130]{3,0,2,1:T(8,128)(2,1)S(1)}, bf16[64,1,5,130]{3,0,2,1:T(8,128)(2,1)S(1)}, u32[]{:S(2)}, u32[]{:S(2)}) collective-permute-start(bf16[64,1,5,130]{3,0,2,1:T(8,128)(2,1)S(1)} %pad_maximum_fusion), channel_id=1, source_target_pairs={{0,8},{8,0},{1,9},{9,1},{2,10},{10,2},{3,11},{11,3},{4,12},{12,4},... | collective-permute-start | bytes 249608 | tf_op jit(solution)/shard_map/ppermute | solution.py:19
  (18 other events, 14.3 us)
Sparse Core Ops, SparseCore 0:
  46.0 44.6 all-gather.1

commit v15 on v11

--- a/solution.py
+++ b/solution.py
@@ -105,14 +105,8 @@
     queries = ordered(own_queries, peer_queries).reshape(all_rows, local_heads, GROUP, HD)
     fresh_keys = ordered(own_keys, peer_keys)
     fresh_values = ordered(own_values, peer_values)
-    state = (
-        jnp.full((local_heads, GROUP, all_rows), FLOOR_SCORE, jnp.float32),
-        jnp.zeros((local_heads, GROUP, all_rows), jnp.float32),
-        jnp.zeros((all_rows, local_heads, GROUP, HD), jnp.float32),
-    )
     token_index = jnp.arange(all_rows)
     causal = (token_index[None, :] <= token_index[:, None]) & (parity == 1)
-    state = absorb(state, queries, fresh_keys, fresh_values, causal, scale)
     page_count = (length + page_rows - 1) // page_rows
     even_pages = (page_count + 1) // 2
     first_page = jnp.where(parity == 0, 0, even_pages)
@@ -130,16 +124,32 @@
     allowed = jnp.broadcast_to(usable[None, :], (all_rows, pages_local * page_rows))
     pool_keys = k_cache.reshape(pages_local * page_rows, local_heads, HD)
     pool_values = v_cache.reshape(pages_local * page_rows, local_heads, HD)
-    running_max, running_sum, output = absorb(
-        state, queries, pool_keys, pool_values, allowed, scale
-    )
+    half = pool_keys.shape[0] // 2
+
+    def attend(start):
+        state = (
+            jnp.full((local_heads, GROUP, own_rows), FLOOR_SCORE, jnp.float32),
+            jnp.zeros((local_heads, GROUP, own_rows), jnp.float32),
+            jnp.zeros((own_rows, local_heads, GROUP, HD), jnp.float32),
+        )
+        rows_queries = lax.dynamic_slice_in_dim(queries, start, own_rows, 0)
+        rows_causal = lax.dynamic_slice_in_dim(causal, start, own_rows, 0)
+        state = absorb(state, rows_queries, fresh_keys, fresh_values, rows_causal, scale)
+        for first in (0, half):
+            state = absorb(
+                state,
+                rows_queries,
+                pool_keys[first : first + half],
+                pool_values[first : first + half],
+                allowed[:own_rows, first : first + half],
+                scale,
+            )
+        return state
+
     peer_start = (1 - parity) * own_rows
     own_start = parity * own_rows
-    outgoing = (
-        lax.dynamic_slice_in_dim(output, peer_start, own_rows, 0),
-        lax.dynamic_slice_in_dim(running_max, peer_start, own_rows, 2),
-        lax.dynamic_slice_in_dim(running_sum, peer_start, own_rows, 2),
-    )
+    peer_max, peer_sum, peer_output = attend(peer_start)
+    outgoing = (peer_output, peer_max, peer_sum)
     outgoing = jnp.concatenate(
         [
             outgoing[0].astype(jnp.bfloat16),
@@ -152,9 +162,7 @@
     other_output = incoming[..., :HD]
     other_max = jnp.transpose(incoming[..., HD], (1, 2, 0))
     other_sum = jnp.transpose(incoming[..., HD + 1], (1, 2, 0))
-    mine_output = lax.dynamic_slice_in_dim(output, own_start, own_rows, 0)
-    mine_max = lax.dynamic_slice_in_dim(running_max, own_start, own_rows, 2)
-    mine_sum = lax.dynamic_slice_in_dim(running_sum, own_start, own_rows, 2)
+    mine_max, mine_sum, mine_output = attend(own_start)
     joint_max = jnp.maximum(mine_max, other_max)
     mine_factor = jnp.exp(mine_max - joint_max)
     other_factor = jnp.exp(other_max - joint_max)

time: 140 us -> 142 us (1.014)
  matrix products: 10.4 us -> 13.5 us
  local copies, waits for them, and re-layouts: 12.2 us -> 10.4 us
    dot_general x2 -> x6, matrix products: 1.28 us -> 4.86 us  [absorb(): jnp.einsum('qcgd,kcd->cgqk', queries, block_keys, preferred_element_type=...]
    dot_general x2 -> x6, matrix products: 4.16 us -> 3.69 us  [absorb(): jnp.einsum('cgqk,kcd->qcgd', weights.astype(jnp.bfloat16), block_values,...]
  transfers between devices with their start and end apart: 3 -> 3, of which waited for: 1 -> 0; matrix products, arithmetic and copies ran while one was open for 10% -> 12% of each run, Pallas kernels for 0% -> 0%
where the time goes in v15:
time: 142 us; the launch traced here: 141 us
  blocking collectives  91.4 us (64%)
  between operations  15.5 us (11%)
  matrix products  13.5 us (10%)
  local copies, waits for them, and re-layouts  10.4 us (7%)
  other arithmetic  5.89 us (4%)
  starting transfers between devices  4.38 us (3%)
    all_to_all x1, blocking collectives, output_rows(): lax.all_to_all(chunks.reshape(depth * parts, share, width), ('z', 'tp'),...  37.4 us
    all_gather x1, blocking collectives, shards(): gathered = lax.all_gather(projected, 'tp', axis=2, tiled=True)  27.7 us
    all_gather x1, blocking collectives, shards(): full_rows = lax.all_gather(attention[:, None], 'tp', axis=1, tiled=True)  26.3 us
    dot_general x1, matrix products, shards(): lax.dot_general(full_rows, weights_mine, (((1, 2), (1, 2)), ((), ())), pr...  4.94 us
    dot_general x6, matrix products, absorb(): jnp.einsum('qcgd,kcd->cgqk', queries, block_keys, preferred_element_type=...  4.86 us
    ppermute x2, starting transfers between devices, from_partner(): lax.ppermute(value, axis, [(i, i ^ 1 << distance) for i in range(lax.axis...  4.38 us
    dot_general x6, matrix products, absorb(): jnp.einsum('cgqk,kcd->qcgd', weights.astype(jnp.bfloat16), block_values,...  3.69 us
    reshape x1, local copies, waits for them, and re-layouts, shards(): return gathered.reshape(own_rows, -1)  2.92 us
  transfers between devices with their start and end apart: 3, of which 0 were waited for; matrix products, arithmetic and copies ran while one was open for 12% of the time, Pallas kernels for 0%

profile of v15, /device:TPU:6, one launch (start us, length us, event | category | flops | bytes accessed | tf_op | source)
XLA Modules:
  0.0 141.0 jit_solution(5640150333693739514)
XLA Ops:
  6.5 0.9 broadcast_in_dim.160
  7.5 37.4 %all_to_all.5 = bf16[32,10,640]{2,1,0:T(8,128)(2,1)S(1)} all-to-all(bf16[32,10,640]{2,1,0:T(8,128)(2,1)S(1)} %bitcast.468), channel_id=1, replica_groups=mesh['z'=4,'x'=8,'core'=2,'tp'=8] {'z','tp'}, dimensions={0} | all-to-all | bytes 819200 | tf_op jit(solution)/shard_map/all_to_all | solution.py:60
  45.0 0.8 copy.89
  45.9 0.6 dynamic_slice.15
  47.9 1.9 %collective-permute-start = (bf16[64,7,128]{2,0,1:T(8,128)(2,1)S(1)}, bf16[64,7,128]{2,0,1:T(8,128)(2,1)S(1)}, u32[]{:S(2)}, u32[]{:S(2)}) collective-permute-start(bf16[64,7,128]{2,0,1:T(8,128)(2,1)S(1)} %pad_maximum_fusion.1), channel_id=1, source_target_pairs={{0,8},{8,0},{1,9},{9,1},{2,10},{10,2},{3,11},{11,3},{4,12},{12,4},... | collective-permute-start | bytes 344072 | tf_op jit(solution)/shard_map/ppermute | solution.py:19
  50.5 0.7 fusion.139
  51.5 0.7 fusion.104
  52.2 0.7 fusion.156
  53.1 0.6 slice_bitcast_fusion.1
  54.0 1.5 %bitcast_reduce_fusion.1 = (f32[5,64]{1,0:T(8,128)S(1)}, f32[1,1024,64,5]{1,2,3,0:T(8,128)}) fusion(bf16[1024,128,1]{1,0,2:T(8,128)(2,1)S(1)} %bitcast.470, bf16[128,5,128]{2,0,1:T(8,128)(2,1)S(1)} %maximum_select_fusion, s32[]{:T(128)S(6)} %select_n.140, pred[1024]{0:T(1024)(128)(4,1)S(1)} %get-tuple-element.7), kind=kOutput, calls=%fused_computation.13 | convolution fusion | flops 84868800 | bytes 1657092 | tf_op jit(solution)/shard_map/qcgd,kcd->cgqk/dot_general | solution.py:36
  55.5 1.4 bitcast_reduce_fusion
  57.3 0.9 fusion.159
  58.7 0.4 bitcast_reduce_fusion.3
  59.1 0.6 fusion.154
  59.9 1.8 %fusion.33 = (f32[5,64]{1,0:T(8,128)}, f32[5,64]{1,0:T(8,128)S(1)}, f32[5,64]{1,0:T(8,128)S(1)}, f32[5,64]{1,0:T(8,128)}) fusion(f32[1,1024,64,5]{1,2,3,0:T(8,128)S(1)} %get-tuple-element.55, f32[5,64]{1,0:T(8,128)S(1)} %get-tuple-element.16, pred[1024]{0:T(1024)(128)(4,1)S(1)} %copy-done.48, f32[5,64]{1,0:T(8,128)S(1)} %get-tuple-element.14, ...), kind=kLoop, calls=%fused_computation.54 | loop fusion | flops 3930880 | bytes 5255168 | tf_op jit(solution)/shard_map/reduce_sum | solution.py:43
  61.8 0.6 fusion.129
  62.6 1.8 %convolution_bitcast_fusion.2 = f32[64,1,5,128]{3,0,2,1:T(8,128)S(1)} fusion(bf16[1024,128,1]{1,0,2:T(8,128)(2,1)S(1)} %bitcast.480, f32[1,1024,64,5]{1,2,3,0:T(8,128)} %get-tuple-element.49, f32[5,64]{1,0:T(8,128)} %copy-done.39, pred[1024]{0:T(1024)(128)(4,1)S(1)} %copy-done.49), kind=kOutput, calls=%fused_computation.30 | convolution fusion | flops 84869120 | bytes 1739008 | tf_op jit(solution)/shard_map/cgqk,kcd->qcgd/dot_general | solution.py:44
  65.6 2.5 %collective-permute-start.1 = (bf16[64,1,5,130]{3,0,2,1:T(8,128)(2,1)S(1)}, bf16[64,1,5,130]{3,0,2,1:T(8,128)(2,1)S(1)}, u32[]{:S(2)}, u32[]{:S(2)}) collective-permute-start(bf16[64,1,5,130]{3,0,2,1:T(8,128)(2,1)S(1)} %pad_maximum_fusion), channel_id=1, source_target_pairs={{0,8},{8,0},{1,9},{9,1},{2,10},{10,2},{3,11},{11,3},{4,12},{12,4},... | collective-permute-start | bytes 249608 | tf_op jit(solution)/shard_map/ppermute | solution.py:19
  69.0 0.4 copy-done.7
  70.4 26.3 %all_gather.9 = bf16[64,8,640]{2,0,1:T(8,128)(2,1)S(1)} all-gather(bf16[64,1,640]{2,0,1:T(8,128)(2,1)S(1)} %bitcast.477), channel_id=1, replica_groups=mesh['z'=4,'x'=8,'core'=2,'tp'=8] {'tp'}, dimensions={1}, use_global_device_ids=true | all-gather | bytes 737280 | tf_op jit(solution)/shard_map/all_gather | solution.py:179
  96.7 4.9 %fusion.30 = bf16[64,640]{1,0:T(8,128)(2,1)S(1)} fusion(bf16[64,8,640]{2,0,1:T(8,128)(2,1)S(1)} %all_gather.9, bf16[640,8,640]{2,0,1:T(8,128)(2,1)} %all-gather.2.cloned.1.call-done), kind=kOutput, calls=%fused_computation.51 | convolution fusion | flops 419471360 | bytes 7290880 | tf_op jit(solution)/shard_map/dot_general | solution.py:180
  102.1 27.7 %all_gather.11 = bf16[64,64,80]{1,0,2:T(8,128)(2,1)S(1)} all-gather(bf16[64,64,10]{1,0,2:T(8,128)(2,1)S(1)} %copy.92), channel_id=1, replica_groups=mesh['z'=4,'x'=8,'core'=2,'tp'=8] {'tp'}, dimensions={2}, use_global_device_ids=true | all-gather | bytes 737280 | tf_op jit(solution)/shard_map/all_gather | solution.py:190
  129.8 1.5 %copy.93 = bf16[64,64,80]{2,1,0:T(8,128)(2,1)S(1)} copy(bf16[64,64,80]{1,0,2:T(8,128)(2,1)S(1)} %all_gather.11) | data formatting | bytes 1310720 | tf_op jit(solution)/shard_map/all_gather | solution.py:190
  131.3 2.9 %reshape.640 = bf16[64,5120]{1,0:T(8,128)(2,1)} reshape(bf16[64,64,80]{2,1,0:T(8,128)(2,1)S(1)} %copy.93) | data formatting | bytes 1310720 | tf_op jit(solution)/shard_map/reshape | solution.py:191
  (153 shorter events, 5.9 us)
Async XLA Ops:
  6.5 90.1 %all-gather.2.cloned.1.call-start = ((), (), s32[]{:S(2)}) async-start(), calls=%async_computation.1 | async-start | bytes 6963200 | tf_op jit(solution)/shard_map/all_gather | solution.py:65
  44.9 2.2 %copy-start.14 = (bf16[64,128]{1,0:T(8,128)(2,1)S(1)}, bf16[64,128]{1,0:T(8,128)(2,1)}, u32[]{:S(2)}) copy-start(bf16[64,128]{1,0:T(8,128)(2,1)} %param.9) | copy-start | bytes 49156
  44.9 2.6 %copy-start.5 = (bf16[64,640]{1,0:T(8,128)(2,1)S(1)}, bf16[64,640]{1,0:T(8,128)(2,1)}, u32[]{:S(2)}) copy-start(bf16[64,640]{1,0:T(8,128)(2,1)} %param.8) | copy-start | bytes 245764
  45.8 6.3 %copy-start.3 = (bf16[16,128,128]{2,1,0:T(8,128)(2,1)S(1)}, bf16[16,128,128]{2,1,0:T(8,128)(2,1)}, u32[]{:S(2)}) copy-start(bf16[16,128,128]{2,1,0:T(8,128)(2,1)} %param.11) | copy-start | bytes 1572868
  47.6 4.6 %copy-start.4 = (bf16[16,128,128]{2,1,0:T(8,128)(2,1)S(1)}, bf16[16,128,128]{2,1,0:T(8,128)(2,1)}, u32[]{:S(2)}) copy-start(bf16[16,128,128]{2,1,0:T(8,128)(2,1)} %param.12) | copy-start | bytes 1572868
  47.9 5.1 %collective-permute-start = (bf16[64,7,128]{2,0,1:T(8,128)(2,1)S(1)}, bf16[64,7,128]{2,0,1:T(8,128)(2,1)S(1)}, u32[]{:S(2)}, u32[]{:S(2)}) collective-permute-start(bf16[64,7,128]{2,0,1:T(8,128)(2,1)S(1)} %pad_maximum_fusion.1), channel_id=1, source_target_pairs={{0,8},{8,0},{1,9},{9,1},{2,10},{10,2},{3,11},{11,3},{4,12},{12,4},... | collective-permute-start | bytes 344072 | tf_op jit(solution)/shard_map/ppermute | solution.py:19
  52.9 4.2 %copy-start.8 = (pred[64,128]{1,0:T(8,128)(4,1)}, pred[64,128]{1,0:T(8,128)(4,1)S(1)}, u32[]{:S(2)}) copy-start(pred[64,128]{1,0:T(8,128)(4,1)S(1)} %get-tuple-element.33) | copy-start | bytes 24580
  52.9 4.4 %copy-start.26 = (pred[64,128]{1,0:T(8,128)(4,1)}, pred[64,128]{1,0:T(8,128)(4,1)S(1)}, u32[]{:S(2)}) copy-start(pred[64,128]{1,0:T(8,128)(4,1)S(1)} %get-tuple-element.34) | copy-start | bytes 24580
  53.0 3.9 %copy-start.47 = (pred[1024]{0:T(1024)(128)(4,1)}, pred[1024]{0:T(1024)(128)(4,1)S(1)}, u32[]{:S(2)}) copy-start(pred[1024]{0:T(1024)(128)(4,1)S(1)} %get-tuple-element.7) | copy-start | bytes 3076
  53.0 5.2 %copy-start.43 = (pred[1024]{0:T(1024)(128)(4,1)}, pred[1024]{0:T(1024)(128)(4,1)S(1)}, u32[]{:S(2)}) copy-start(pred[1024]{0:T(1024)(128)(4,1)S(1)} %get-tuple-element.8) | copy-start | bytes 3076
  54.0 3.1 %copy-start.24 = (f32[5,64]{1,0:T(8,128)}, f32[5,64]{1,0:T(8,128)S(1)}, u32[]{:S(2)}) copy-start(f32[5,64]{1,0:T(8,128)S(1)} %get-tuple-element.50) | copy-start | bytes 3844
  55.5 2.7 %copy-start.10 = (f32[5,64]{1,0:T(8,128)}, f32[5,64]{1,0:T(8,128)S(1)}, u32[]{:S(2)}) copy-start(f32[5,64]{1,0:T(8,128)S(1)} %get-tuple-element.48) | copy-start | bytes 3844
  57.1 2.6 %copy-start.37 = (f32[5,64]{1,0:T(8,128)}, f32[5,64]{1,0:T(8,128)S(1)}, u32[]{:S(2)}) copy-start(f32[5,64]{1,0:T(8,128)S(1)} %get-tuple-element.13) | copy-start | bytes 3844
  57.1 4.7 %copy-start.39 = (f32[5,64]{1,0:T(8,128)}, f32[5,64]{1,0:T(8,128)S(1)}, u32[]{:S(2)}) copy-start(f32[5,64]{1,0:T(8,128)S(1)} %get-tuple-element.14) | copy-start | bytes 3844
  59.7 2.1 %copy-start.35 = (f32[5,64]{1,0:T(8,128)}, f32[5,64]{1,0:T(8,128)S(1)}, u32[]{:S(2)}) copy-start(f32[5,64]{1,0:T(8,128)S(1)} %get-tuple-element.16) | copy-start | bytes 3844
  59.9 2.7 %copy-start.6 = (bf16[8,128,128]{2,1,0:T(8,128)(2,1)S(1)}, bf16[8,128,128]{2,1,0:T(8,128)(2,1)}, u32[]{:S(2)}) copy-start(bf16[8,128,128]{2,1,0:T(8,128)(2,1)} %get-tuple-element.17) | copy-start | bytes 786436
  59.9 2.7 %copy-start.49 = (pred[1024]{0:T(1024)(128)(4,1)S(1)}, pred[1024]{0:T(1024)(128)(4,1)}, u32[]{:S(2)}) copy-start(pred[1024]{0:T(1024)(128)(4,1)} %copy-done.47) | copy-start | bytes 3076
  61.8 2.8 %copy-start.38 = (f32[5,64]{1,0:T(8,128)S(1)}, f32[5,64]{1,0:T(8,128)}, u32[]{:S(2)}) copy-start(f32[5,64]{1,0:T(8,128)} %copy-done.37) | copy-start | bytes 3844
  61.8 2.8 %copy-start.45 = (pred[1024]{0:T(1024)(128)(4,1)S(1)}, pred[1024]{0:T(1024)(128)(4,1)}, u32[]{:S(2)}) copy-start(pred[1024]{0:T(1024)(128)(4,1)} %copy-done.43) | copy-start | bytes 3076
  64.5 3.5 %copy-start.36 = (f32[5,64]{1,0:T(8,128)S(1)}, f32[5,64]{1,0:T(8,128)}, u32[]{:S(2)}) copy-start(f32[5,64]{1,0:T(8,128)} %copy-done.35) | copy-start | bytes 3844
  64.6 3.5 %copy-start.50 = (pred[1024]{0:T(1024)(128)(4,1)S(1)}, pred[1024]{0:T(1024)(128)(4,1)}, u32[]{:S(2)}) copy-start(pred[1024]{0:T(1024)(128)(4,1)} %copy-done.47) | copy-start | bytes 3076
  65.2 3.3 %copy-start.34 = (f32[5,64]{1,0:T(8,128)S(1)}, f32[5,64]{1,0:T(8,128)}, u32[]{:S(2)}) copy-start(f32[5,64]{1,0:T(8,128)} %copy-done.33) | copy-start | bytes 3844
  65.2 3.3 %copy-start.46 = (pred[1024]{0:T(1024)(128)(4,1)S(1)}, pred[1024]{0:T(1024)(128)(4,1)}, u32[]{:S(2)}) copy-start(pred[1024]{0:T(1024)(128)(4,1)} %copy-done.43) | copy-start | bytes 3076
  65.6 4.0 %collective-permute-start.1 = (bf16[64,1,5,130]{3,0,2,1:T(8,128)(2,1)S(1)}, bf16[64,1,5,130]{3,0,2,1:T(8,128)(2,1)S(1)}, u32[]{:S(2)}, u32[]{:S(2)}) collective-permute-start(bf16[64,1,5,130]{3,0,2,1:T(8,128)(2,1)S(1)} %pad_maximum_fusion), channel_id=1, source_target_pairs={{0,8},{8,0},{1,9},{9,1},{2,10},{10,2},{3,11},{11,3},{4,12},{12,4},... | collective-permute-start | bytes 249608 | tf_op jit(solution)/shard_map/ppermute | solution.py:19
  (31 other events, 38.2 us)
Sparse Core Ops, SparseCore 0:
  46.0 44.6 all-gather.1

commit v16 on v11

--- a/solution.py
+++ b/solution.py
@@ -112,7 +112,6 @@
     )
     token_index = jnp.arange(all_rows)
     causal = (token_index[None, :] <= token_index[:, None]) & (parity == 1)
-    state = absorb(state, queries, fresh_keys, fresh_values, causal, scale)
     page_count = (length + page_rows - 1) // page_rows
     even_pages = (page_count + 1) // 2
     first_page = jnp.where(parity == 0, 0, even_pages)
@@ -130,9 +129,17 @@
     allowed = jnp.broadcast_to(usable[None, :], (all_rows, pages_local * page_rows))
     pool_keys = k_cache.reshape(pages_local * page_rows, local_heads, HD)
     pool_values = v_cache.reshape(pages_local * page_rows, local_heads, HD)
-    running_max, running_sum, output = absorb(
-        state, queries, pool_keys, pool_values, allowed, scale
-    )
+    half = pool_keys.shape[0] // 2
+    state = absorb(
+        state,
+        queries,
+        jnp.concatenate([fresh_keys, pool_keys[:half]], axis=0),
+        jnp.concatenate([fresh_values, pool_values[:half]], axis=0),
+        jnp.concatenate([causal, allowed[:, :half]], axis=1),
+        scale,
+    )
+    state = absorb(state, queries, pool_keys[half:], pool_values[half:], allowed[:, half:], scale)
+    running_max, running_sum, output = state
     peer_start = (1 - parity) * own_rows
     own_start = parity * own_rows
     outgoing = (

time: 140 us -> 138 us (0.986)
  matrix products: 10.4 us -> 8.91 us
    slice x0 -> x4, local copies, waits for them, and re-layouts: none -> 1.53 us  [the longest x1 0.75 us: shards(): pool_values[half:]]
    dot_general x2, matrix products: 4.16 us -> 2.73 us  [absorb(): jnp.einsum('cgqk,kcd->qcgd', weights.astype(jnp.bfloat16), block_values,...]
  transfers between devices with their start and end apart: 3 -> 3, of which waited for: 1 -> 1; matrix products, arithmetic and copies ran while one was open for 10% -> 9% of each run, Pallas kernels for 0% -> 0%
where the time goes in v16:
time: 138 us
  blocking collectives  91.6 us (66%)
  between operations  15.2 us (11%)
  local copies, waits for them, and re-layouts  11.8 us (9%)
  matrix products  8.91 us (6%)
  other arithmetic  4.87 us (4%)
  starting transfers between devices  4.33 us (3%)
    all_to_all x1, blocking collectives, output_rows(): lax.all_to_all(chunks.reshape(depth * parts, share, width), ('z', 'tp'),...  37.4 us
    all_gather x1, blocking collectives, shards(): gathered = lax.all_gather(projected, 'tp', axis=2, tiled=True)  27.8 us
    all_gather x1, blocking collectives, shards(): full_rows = lax.all_gather(attention[:, None], 'tp', axis=1, tiled=True)  26.4 us
    dot_general x1, matrix products, shards(): lax.dot_general(full_rows, weights_mine, (((1, 2), (1, 2)), ((), ())), pr...  4.94 us
    ppermute x2, starting transfers between devices, from_partner(): lax.ppermute(value, axis, [(i, i ^ 1 << distance) for i in range(lax.axis...  4.33 us
    reshape x1, local copies, waits for them, and re-layouts, shards(): return gathered.reshape(own_rows, -1)  2.92 us
  transfers between devices with their start and end apart: 3, of which 1 were waited for; matrix products, arithmetic and copies ran while one was open for 9% of the time, Pallas kernels for 0%

profile of v16, /device:TPU:6, one launch (start us, length us, event | category | flops | bytes accessed | tf_op | source)
XLA Modules:
  0.0 137.7 jit_solution(6068313169130050647)
XLA Ops:
  6.5 1.0 broadcast_in_dim.118
  7.6 37.4 %all_to_all.5 = bf16[32,10,640]{2,1,0:T(8,128)(2,1)S(1)} all-to-all(bf16[32,10,640]{2,1,0:T(8,128)(2,1)S(1)} %bitcast.227), channel_id=1, replica_groups=mesh['z'=4,'x'=8,'core'=2,'tp'=8] {'z','tp'}, dimensions={0} | all-to-all | bytes 819200 | tf_op jit(solution)/shard_map/all_to_all | solution.py:60
  45.1 0.8 copy.96
  45.9 0.6 dynamic_slice.24
  47.9 1.9 %collective-permute-start = (bf16[64,7,128]{2,0,1:T(8,128)(2,1)S(1)}, bf16[64,7,128]{2,0,1:T(8,128)(2,1)S(1)}, u32[]{:S(2)}, u32[]{:S(2)}) collective-permute-start(bf16[64,7,128]{2,0,1:T(8,128)(2,1)S(1)} %pad_maximum_fusion.1), channel_id=1, source_target_pairs={{0,8},{8,0},{1,9},{9,1},{2,10},{10,2},{3,11},{11,3},{4,12},{12,4},... | collective-permute-start | bytes 344072 | tf_op jit(solution)/shard_map/ppermute | solution.py:19
  50.6 0.7 fusion.70
  51.5 0.7 fusion.54
  52.3 0.7 fusion.80
  53.3 0.7 fusion.79
  54.1 0.6 fusion.5
  55.0 0.6 fusion.82
  56.3 0.7 fusion.6
  57.0 0.6 fusion.66
  58.4 0.6 fusion.65
  59.1 0.8 copy.90
  59.9 2.0 %fusion.31 = f32[128,1,5,128]{3,0,2,1:T(8,128)S(1)} fusion(f32[1,5,128,1152]{2,3,1,0:T(8,128)S(1)} %get-tuple-element.34, f32[5,128]{1,0:T(8,128)} %copy-done.14, pred[128,1152]{0,1:T(8,128)(4,1)S(1)} %pad_add_fusion, bf16[1024,1,128]{2,0,1:T(8,128)(2,1)} %bitcast.233, bf16[128,1,128]{2,0,1:T(8,128)(2,1)S(1)} %get-tuple-element.38, ...), kind=kOutput, calls=%fused_computation.25 | convolution fusion | flops 191709184 | bytes 3726848 | tf_op jit(solution)/shard_map/cgqk,kcd->qcgd/dot_general | solution.py:44
  61.9 0.7 fusion.25
  62.8 2.4 %collective-permute-start.1 = (bf16[64,1,5,130]{3,0,2,1:T(8,128)(2,1)S(1)}, bf16[64,1,5,130]{3,0,2,1:T(8,128)(2,1)S(1)}, u32[]{:S(2)}, u32[]{:S(2)}) collective-permute-start(bf16[64,1,5,130]{3,0,2,1:T(8,128)(2,1)S(1)} %pad_maximum_fusion), channel_id=1, source_target_pairs={{0,8},{8,0},{1,9},{9,1},{2,10},{10,2},{3,11},{11,3},{4,12},{12,4},... | collective-permute-start | bytes 249608 | tf_op jit(solution)/shard_map/ppermute | solution.py:19
  65.2 1.0 collective-permute-done.1
  66.8 26.4 %all_gather.9 = bf16[64,8,640]{2,0,1:T(8,128)(2,1)S(1)} all-gather(bf16[64,1,640]{2,0,1:T(8,128)(2,1)S(1)} %copy_bitcast_fusion.1), channel_id=1, replica_groups=mesh['z'=4,'x'=8,'core'=2,'tp'=8] {'tp'}, dimensions={1}, use_global_device_ids=true | all-gather | bytes 737280 | tf_op jit(solution)/shard_map/all_gather | solution.py:178
  93.2 4.9 %fusion.34 = bf16[64,640]{1,0:T(8,128)(2,1)S(1)} fusion(bf16[64,8,640]{2,0,1:T(8,128)(2,1)S(1)} %all_gather.9, bf16[640,8,640]{2,0,1:T(8,128)(2,1)} %all-gather.2.cloned.1.call-done), kind=kOutput, calls=%fused_computation.27 | convolution fusion | flops 419471360 | bytes 7290880 | tf_op jit(solution)/shard_map/dot_general | solution.py:179
  98.6 27.8 %all_gather.11 = bf16[64,64,80]{1,0,2:T(8,128)(2,1)S(1)} all-gather(bf16[64,64,10]{1,0,2:T(8,128)(2,1)S(1)} %copy.99), channel_id=1, replica_groups=mesh['z'=4,'x'=8,'core'=2,'tp'=8] {'tp'}, dimensions={2}, use_global_device_ids=true | all-gather | bytes 737280 | tf_op jit(solution)/shard_map/all_gather | solution.py:189
  126.5 1.5 %copy.100 = bf16[64,64,80]{2,1,0:T(8,128)(2,1)S(1)} copy(bf16[64,64,80]{1,0,2:T(8,128)(2,1)S(1)} %all_gather.11) | data formatting | bytes 1310720 | tf_op jit(solution)/shard_map/all_gather | solution.py:189
  127.9 2.9 %reshape.445 = bf16[64,5120]{1,0:T(8,128)(2,1)} reshape(bf16[64,64,80]{2,1,0:T(8,128)(2,1)S(1)} %copy.100) | data formatting | bytes 1310720 | tf_op jit(solution)/shard_map/reshape | solution.py:190
  (78 shorter events, 4.3 us)
Async XLA Ops:
  6.5 39.4 %copy-start.17 = (s32[32]{0:T(128)S(1)}, s32[32]{0:T(128)}, u32[]{:S(2)}) copy-start(s32[32]{0:T(128)} %param.13) | copy-start | bytes 388
  6.5 40.7 %copy-start.6 = (bf16[64,128]{1,0:T(8,128)(2,1)S(1)}, bf16[64,128]{1,0:T(8,128)(2,1)}, u32[]{:S(2)}) copy-start(bf16[64,128]{1,0:T(8,128)(2,1)} %param.9) | copy-start | bytes 49156
  6.5 41.1 %copy-start.4 = (bf16[64,640]{1,0:T(8,128)(2,1)S(1)}, bf16[64,640]{1,0:T(8,128)(2,1)}, u32[]{:S(2)}) copy-start(bf16[64,640]{1,0:T(8,128)(2,1)} %param.8) | copy-start | bytes 245764
  6.5 86.6 %all-gather.2.cloned.1.call-start = ((), (), s32[]{:S(2)}) async-start(), calls=%async_computation.1 | async-start | bytes 6963200 | tf_op jit(solution)/shard_map/all_gather | solution.py:65
  7.6 40.3 %copy-start.7 = (bf16[64,128]{1,0:T(8,128)(2,1)S(1)}, bf16[64,128]{1,0:T(8,128)(2,1)}, u32[]{:S(2)}) copy-start(bf16[64,128]{1,0:T(8,128)(2,1)} %param.10) | copy-start | bytes 49156
  45.0 7.3 %copy-start.2 = (bf16[16,128,128]{2,1,0:T(8,128)(2,1)S(1)}, bf16[16,128,128]{2,1,0:T(8,128)(2,1)}, u32[]{:S(2)}) copy-start(bf16[16,128,128]{2,1,0:T(8,128)(2,1)} %param.11) | copy-start | bytes 1572868
  45.1 8.2 %copy-start.3 = (bf16[16,128,128]{2,1,0:T(8,128)(2,1)S(1)}, bf16[16,128,128]{2,1,0:T(8,128)(2,1)}, u32[]{:S(2)}) copy-start(bf16[16,128,128]{2,1,0:T(8,128)(2,1)} %param.12) | copy-start | bytes 1572868
  47.9 6.1 %collective-permute-start = (bf16[64,7,128]{2,0,1:T(8,128)(2,1)S(1)}, bf16[64,7,128]{2,0,1:T(8,128)(2,1)S(1)}, u32[]{:S(2)}, u32[]{:S(2)}) collective-permute-start(bf16[64,7,128]{2,0,1:T(8,128)(2,1)S(1)} %pad_maximum_fusion.1), channel_id=1, source_target_pairs={{0,8},{8,0},{1,9},{9,1},{2,10},{10,2},{3,11},{11,3},{4,12},{12,4},... | collective-permute-start | bytes 344072 | tf_op jit(solution)/shard_map/ppermute | solution.py:19
  52.3 3.9 %copy-start.15 = (pred[1024]{0:T(1024)(128)(4,1)}, pred[1024]{0:T(1024)(128)(4,1)S(1)}, u32[]{:S(2)}) copy-start(pred[1024]{0:T(1024)(128)(4,1)S(1)} %get-tuple-element.8) | copy-start | bytes 3076
  54.1 0.9 copy-start.5
  54.7 1.5 %copy-start = (f32[128,5,1024]{2,0,1:T(8,128)}, f32[128,5,1024]{2,0,1:T(8,128)S(1)}, u32[]{:S(2)}) copy-start(f32[128,5,1024]{2,0,1:T(8,128)S(1)} %get-tuple-element.36) | copy-start | bytes 7864324
  55.6 0.6 copy-start.12
  55.6 2.0 %copy-start.14 = (f32[5,128]{1,0:T(8,128)}, f32[5,128]{1,0:T(8,128)S(1)}, u32[]{:S(2)}) copy-start(f32[5,128]{1,0:T(8,128)S(1)} %get-tuple-element.29) | copy-start | bytes 7684
  57.6 0.6 copy-start.8
  57.6 0.8 copy-start.10
  59.8 2.0 %copy-start.1 = (f32[128,5,1024]{2,0,1:T(8,128)S(1)}, f32[128,5,1024]{2,0,1:T(8,128)}, u32[]{:S(2)}) copy-start(f32[128,5,1024]{2,0,1:T(8,128)} %copy-done) | copy-start | bytes 7864324
  59.8 2.0 %copy-start.13 = (f32[5,128]{1,0:T(8,128)S(1)}, f32[5,128]{1,0:T(8,128)}, u32[]{:S(2)}) copy-start(f32[5,128]{1,0:T(8,128)} %copy-done.12) | copy-start | bytes 7684
  59.8 2.0 %copy-start.16 = (pred[1024]{0:T(1024)(128)(4,1)S(1)}, pred[1024]{0:T(1024)(128)(4,1)}, u32[]{:S(2)}) copy-start(pred[1024]{0:T(1024)(128)(4,1)} %copy-done.15) | copy-start | bytes 3076
  61.9 4.6 %copy-start.9 = (f32[1,5,128]{2,1,0:T(8,128)S(1)}, f32[1,5,128]{2,1,0:T(8,128)}, u32[]{:S(2)}) copy-start(f32[1,5,128]{2,1,0:T(8,128)} %copy-done.8) | copy-start | bytes 7684
  61.9 4.6 %copy-start.11 = (f32[1,5,128]{2,1,0:T(8,128)S(1)}, f32[1,5,128]{2,1,0:T(8,128)}, u32[]{:S(2)}) copy-start(f32[1,5,128]{2,1,0:T(8,128)} %copy-done.10) | copy-start | bytes 7684
  62.8 3.4 %collective-permute-start.1 = (bf16[64,1,5,130]{3,0,2,1:T(8,128)(2,1)S(1)}, bf16[64,1,5,130]{3,0,2,1:T(8,128)(2,1)S(1)}, u32[]{:S(2)}, u32[]{:S(2)}) collective-permute-start(bf16[64,1,5,130]{3,0,2,1:T(8,128)(2,1)S(1)} %pad_maximum_fusion), channel_id=1, source_target_pairs={{0,8},{8,0},{1,9},{9,1},{2,10},{10,2},{3,11},{11,3},{4,12},{12,4},... | collective-permute-start | bytes 249608 | tf_op jit(solution)/shard_map/ppermute | solution.py:19
Sparse Core Ops, SparseCore 0:
  46.0 44.6 all-gather.1

commit v17 on v13

--- a/solution.py
+++ b/solution.py
@@ -53,15 +53,11 @@
 
 def output_rows(w_out):
     parts = lax.axis_size("tp")
-    depth = lax.axis_size("z")
     rows, width = w_out.shape
     share = rows // parts
-    chunks = jnp.broadcast_to(w_out.reshape(1, parts, share, width), (depth, parts, share, width))
-    pieces = lax.all_to_all(
-        chunks.reshape(depth * parts, share, width), ("z", "tp"), 0, 0, tiled=True
-    )
-    near = jnp.transpose(pieces.reshape(depth, parts, share, width), (0, 2, 1, 3))
-    near = near.reshape(depth * share, parts, width)
+    pieces = lax.all_to_all(w_out.reshape(parts, share, width), "tp", 0, 0, tiled=True)
+    mine = jnp.transpose(pieces, (1, 0, 2))
+    near = lax.all_gather(mine, "z", axis=0, tiled=True)
     return lax.all_gather(near, ("x", "core"), axis=0, tiled=True), share
 
 

time: 137 us -> 135 us (0.985)
    all_gather x0 -> x1, blocking collectives: none -> 21 us  [output_rows(): near = lax.all_gather(mine, 'z', axis=0, tiled=True)]
    all_to_all x1, blocking collectives: 37.4 us -> 16.7 us  [output_rows(): lax.all_to_all(w_out.reshape(parts, share, width), 'tp', 0, 0, tiled=True)]
where the time goes in v17:
time: 135 us
  blocking collectives  90.9 us (67%)
  between operations  15.1 us (11%)
  matrix products  9.93 us (7%)
  local copies, waits for them, and re-layouts  9.09 us (7%)
  other arithmetic  4.56 us (3%)
  starting transfers between devices  4.38 us (3%)
    all_gather x1, blocking collectives, shards(): gathered = lax.all_gather(projected, 'tp', axis=2, tiled=True)  27.6 us
    all_gather x1, blocking collectives, shards(): full_rows = lax.all_gather(attention[:, None], 'tp', axis=1, tiled=True)  25.7 us
    all_gather x1, blocking collectives, output_rows(): near = lax.all_gather(mine, 'z', axis=0, tiled=True)  21 us
    all_to_all x1, blocking collectives, output_rows(): lax.all_to_all(w_out.reshape(parts, share, width), 'tp', 0, 0, tiled=True)  16.7 us
    dot_general x1, matrix products, shards(): lax.dot_general(full_rows, weights_mine, (((1, 2), (1, 2)), ((), ())), pr...  4.94 us
    ppermute x2, starting transfers between devices, from_partner(): lax.ppermute(value, axis, [(i, i ^ 1 << distance) for i in range(lax.axis...  4.35 us
    dot_general x3, matrix products, absorb(): jnp.einsum('cgqk,kcd->qcgd', weights.astype(jnp.bfloat16), block_values,...  3.52 us
    reshape x1, local copies, waits for them, and re-layouts, shards(): return gathered.reshape(own_rows, -1)  2.92 us
  transfers between devices with their start and end apart: 3, of which 1 were waited for; matrix products, arithmetic and copies ran while one was open for 9% of the time, Pallas kernels for 0%

profile of v17, /device:TPU:6, one launch (start us, length us, event | category | flops | bytes accessed | tf_op | source)
XLA Modules:
  0.0 135.1 jit_solution(9151260461402743674)
XLA Ops:
  6.6 1.0 reshape.452
  7.6 16.7 %all_to_all.5 = bf16[8,10,640]{2,1,0:T(8,128)(2,1)S(1)} all-to-all(bf16[8,10,640]{2,1,0:T(8,128)(2,1)S(1)} %reshape.452), channel_id=1, replica_groups=mesh['z'=4,'x'=8,'core'=2,'tp'=8] {'tp'}, dimensions={0} | all-to-all | bytes 204800 | tf_op jit(solution)/shard_map/all_to_all | solution.py:58
  24.3 21.0 %all_gather.13 = bf16[40,8,640]{2,1,0:T(8,128)(2,1)S(1)} all-gather(bf16[10,8,640]{2,1,0:T(8,128)(2,1)S(1)} %copy.92), channel_id=1, replica_groups=mesh['z'=4,'x'=8,'core'=2,'tp'=8] {'z'}, dimensions={0}, use_global_device_ids=true | all-gather | bytes 512000 | tf_op jit(solution)/shard_map/all_gather | solution.py:60
  45.3 0.8 copy.93
  46.2 0.6 dynamic_slice.24
  48.4 1.9 %collective-permute-start = (bf16[64,7,128]{2,1,0:T(8,128)(2,1)S(1)}, bf16[64,7,128]{2,1,0:T(8,128)(2,1)S(1)}, u32[]{:S(2)}, u32[]{:S(2)}) collective-permute-start(bf16[64,7,128]{2,1,0:T(8,128)(2,1)S(1)} %pad_maximum_fusion.1), channel_id=1, source_target_pairs={{0,8},{8,0},{1,9},{9,1},{2,10},{10,2},{3,11},{11,3},{4,12},{12,4},... | collective-permute-start | bytes 344072 | tf_op jit(solution)/shard_map/ppermute | solution.py:19
  51.1 0.7 fusion.97
  52.0 0.7 fusion.79
  52.8 0.8 fusion.110
  53.9 0.2 fusion.113
  54.1 0.6 fusion.2
  54.7 0.6 fusion.3
  55.4 1.5 %fusion.4 = (f32[5,128]{1,0:T(8,128)S(1)}, f32[5,128]{1,0:T(8,128)S(1)}) fusion(f32[128,5,1024]{2,0,1:T(8,128)S(1)} %get-tuple-element.38, f32[5,128]{1,0:T(8,128)S(1)} %get-tuple-element.10, pred[1024]{0:T(1024)(128)(4,1)S(1)} %get-tuple-element.8, f32[5,128]{1,0:T(8,128)S(1)} %get-tuple-element.9, f32[128,5,1024]{2,0,1:T(8,128)S(1)} %get-tuple-element.36, ...), kind=kLoop, calls=%fused_computation.8 | loop fusion | flops 6552320 | bytes 5255168 | tf_op jit(solution)/shard_map/reduce_sum | solution.py:43
  57.4 0.3 fusion.35
  57.7 2.5 %fusion.31 = f32[128,1,5,128]{3,0,2,1:T(8,128)S(1)} fusion(f32[128,1,5,128]{3,0,2,1:T(8,128)S(1)} %fusion.35, bf16[1024,128,1]{1,0,2:T(8,128)(2,1)} %bitcast.311, f32[128,5,1024]{2,0,1:T(8,128)} %copy-done, f32[5,128]{1,0:T(8,128)S(1)} %get-tuple-element.10, pred[1024]{0:T(1024)(128)(4,1)S(1)} %get-tuple-element.8, f32[128,5]{0,1:T(8,128)S(1)} %get-tuple-element.24), kind=kOutput, calls=%fused_computation.27 | convolution fusion | flops 171212800 | bytes 3545088 | tf_op jit(solution)/shard_map/cgqk,kcd->qcgd/dot_general | solution.py:44
  60.2 0.7 fusion.28
  61.1 2.4 %collective-permute-start.1 = (bf16[64,1,5,130]{3,0,2,1:T(8,128)(2,1)S(1)}, bf16[64,1,5,130]{3,0,2,1:T(8,128)(2,1)S(1)}, u32[]{:S(2)}, u32[]{:S(2)}) collective-permute-start(bf16[64,1,5,130]{3,0,2,1:T(8,128)(2,1)S(1)} %pad_maximum_fusion), channel_id=1, source_target_pairs={{0,8},{8,0},{1,9},{9,1},{2,10},{10,2},{3,11},{11,3},{4,12},{12,4},... | collective-permute-start | bytes 249608 | tf_op jit(solution)/shard_map/ppermute | solution.py:19
  63.5 1.0 collective-permute-done.1
  64.5 0.2 slice_reduce_fusion.1
  65.1 25.7 %all_gather.12 = bf16[64,8,640]{2,0,1:T(8,128)(2,1)S(1)} all-gather(bf16[64,1,640]{2,0,1:T(8,128)(2,1)S(1)} %copy_bitcast_fusion), channel_id=1, replica_groups=mesh['z'=4,'x'=8,'core'=2,'tp'=8] {'tp'}, dimensions={1}, use_global_device_ids=true | all-gather | bytes 737280 | tf_op jit(solution)/shard_map/all_gather | solution.py:175
  90.7 4.9 %fusion.37 = bf16[64,640]{1,0:T(8,128)(2,1)S(1)} fusion(bf16[64,8,640]{2,0,1:T(8,128)(2,1)S(1)} %all_gather.12, bf16[640,8,640]{2,0,1:T(8,128)(2,1)} %all-gather.2.cloned.1.call-done), kind=kOutput, calls=%fused_computation.32 | convolution fusion | flops 419471360 | bytes 7290880 | tf_op jit(solution)/shard_map/dot_general | solution.py:176
  96.2 27.6 %all_gather.15 = bf16[64,64,80]{1,0,2:T(8,128)(2,1)S(1)} all-gather(bf16[64,64,10]{1,0,2:T(8,128)(2,1)S(1)} %copy.96), channel_id=1, replica_groups=mesh['z'=4,'x'=8,'core'=2,'tp'=8] {'tp'}, dimensions={2}, use_global_device_ids=true | all-gather | bytes 737280 | tf_op jit(solution)/shard_map/all_gather | solution.py:186
  123.8 1.5 %copy.97 = bf16[64,64,80]{2,1,0:T(8,128)(2,1)S(1)} copy(bf16[64,64,80]{1,0,2:T(8,128)(2,1)S(1)} %all_gather.15) | data formatting | bytes 1310720 | tf_op jit(solution)/shard_map/all_gather | solution.py:186
  125.3 2.9 %reshape.453 = bf16[64,5120]{1,0:T(8,128)(2,1)} reshape(bf16[64,64,80]{2,1,0:T(8,128)(2,1)S(1)} %copy.97) | data formatting | bytes 1310720 | tf_op jit(solution)/shard_map/reshape | solution.py:187
  (59 shorter events, 3.1 us)
Async XLA Ops:
  6.5 39.6 %copy-start.3 = (bf16[64,640]{1,0:T(8,128)(2,1)S(1)}, bf16[64,640]{1,0:T(8,128)(2,1)}, u32[]{:S(2)}) copy-start(bf16[64,640]{1,0:T(8,128)(2,1)} %param.8) | copy-start | bytes 245764
  6.5 39.7 %copy-start.6 = (s32[32]{0:T(128)S(1)}, s32[32]{0:T(128)}, u32[]{:S(2)}) copy-start(s32[32]{0:T(128)} %param.13) | copy-start | bytes 388
  6.5 41.0 %copy-start.4 = (bf16[64,128]{1,0:T(8,128)(2,1)S(1)}, bf16[64,128]{1,0:T(8,128)(2,1)}, u32[]{:S(2)}) copy-start(bf16[64,128]{1,0:T(8,128)(2,1)} %param.9) | copy-start | bytes 49156
  6.5 41.4 %copy-start.5 = (bf16[64,128]{1,0:T(8,128)(2,1)S(1)}, bf16[64,128]{1,0:T(8,128)(2,1)}, u32[]{:S(2)}) copy-start(bf16[64,128]{1,0:T(8,128)(2,1)} %param.10) | copy-start | bytes 49156
  6.5 84.2 %all-gather.2.cloned.1.call-start = ((), (), s32[]{:S(2)}) async-start(), calls=%async_computation.1 | async-start | bytes 6963200 | tf_op jit(solution)/shard_map/all_gather | solution.py:61
  24.2 28.5 %copy-start.1 = (bf16[16,128,128]{2,1,0:T(8,128)(2,1)S(1)}, bf16[16,128,128]{2,1,0:T(8,128)(2,1)}, u32[]{:S(2)}) copy-start(bf16[16,128,128]{2,1,0:T(8,128)(2,1)} %param.11) | copy-start | bytes 1572868
  46.0 6.7 %copy-start.2 = (bf16[16,128,128]{2,1,0:T(8,128)(2,1)S(1)}, bf16[16,128,128]{2,1,0:T(8,128)(2,1)}, u32[]{:S(2)}) copy-start(bf16[16,128,128]{2,1,0:T(8,128)(2,1)} %param.12) | copy-start | bytes 1572868
  48.4 5.2 %collective-permute-start = (bf16[64,7,128]{2,1,0:T(8,128)(2,1)S(1)}, bf16[64,7,128]{2,1,0:T(8,128)(2,1)S(1)}, u32[]{:S(2)}, u32[]{:S(2)}) collective-permute-start(bf16[64,7,128]{2,1,0:T(8,128)(2,1)S(1)} %pad_maximum_fusion.1), channel_id=1, source_target_pairs={{0,8},{8,0},{1,9},{9,1},{2,10},{10,2},{3,11},{11,3},{4,12},{12,4},... | collective-permute-start | bytes 344072 | tf_op jit(solution)/shard_map/ppermute | solution.py:19
  54.7 2.2 %copy-start = (f32[128,5,1024]{2,0,1:T(8,128)}, f32[128,5,1024]{2,0,1:T(8,128)S(1)}, u32[]{:S(2)}) copy-start(f32[128,5,1024]{2,0,1:T(8,128)S(1)} %get-tuple-element.38) | copy-start | bytes 7864324
  61.1 3.4 %collective-permute-start.1 = (bf16[64,1,5,130]{3,0,2,1:T(8,128)(2,1)S(1)}, bf16[64,1,5,130]{3,0,2,1:T(8,128)(2,1)S(1)}, u32[]{:S(2)}, u32[]{:S(2)}) collective-permute-start(bf16[64,1,5,130]{3,0,2,1:T(8,128)(2,1)S(1)} %pad_maximum_fusion), channel_id=1, source_target_pairs={{0,8},{8,0},{1,9},{9,1},{2,10},{10,2},{3,11},{11,3},{4,12},{12,4},... | collective-permute-start | bytes 249608 | tf_op jit(solution)/shard_map/ppermute | solution.py:19
Sparse Core Ops, SparseCore 0:
  46.2 43.5 all-gather.1
